TPU v7x, 32 devices: a whole 2x2x4 slice. The times are simulated.
32 devices in a mesh: dp: 4 (over z), space: 4 (over x, core), rep: 2 (over y).
Axes of the slice: x: 2, y: 2, z: 4, core: 2. Of those that a mesh axis runs over, the one named last changes fastest.
Arguments:
- frames: bfloat16 [6, 8, 32, 32, 512], P(None, ('dp', 'rep'), 'space'), may hold values from -6 to 6
- membrane: bfloat16 [8, 32, 32, 512], P(('dp', 'rep'), 'space'), may hold values from -6 to 6
- cotangent: bfloat16 [6, 8, 32, 32, 512], P(None, ('dp', 'rep'), 'space'), may hold values from -6 to 6
- master: float32 [4608, 512], P('dp'), may hold values from -0.09375 to 0.09375
- moment: float32 [4608, 512], P('dp'), may hold values from -4 to 4
- second: float32 [4608, 512], P('dp'), may hold values from 0.05 to 5
Outputs:
- grad_input: bfloat16 [6, 8, 32, 32, 512], P(None, ('dp', 'rep'), 'space')
- membrane_grad: float32 [8, 32, 32, 512], P(('dp', 'rep'), 'space')
- weight_grad: float32 [4608, 512], P('dp')
- new_moment: float32 [4608, 512], P('dp')
- new_second: float32 [4608, 512], P('dp')
- update: float32 [4608, 512], P('dp')
All inputs are finite; a program needn't handle non-finite values.
Results may differ from a plain program's by a relative error of at most 0.003.
Values may be sent and summed in bfloat16 or wider, within the bound.
No kernel may reach another device: no remote copies, remote signals or barrier semaphores. Data moves between devices by JAX's collectives and lax.ppermute only.
A program may use at most 192 MiB of HBM per device.

v0:
```python
import math

import jax
import jax.numpy as jnp
from jax import lax
from jax.sharding import PartitionSpec as P


def extended(x, sides, width):
    for axis, dim in sides:
        peers, length = (lax.axis_size(axis), x.shape[dim])
        up = [(i, (i + 1) % peers) for i in range(peers - 1)]
        down = [(j, i) for i, j in up]
        last = lax.slice_in_dim(x, length - width, length, axis=dim)
        first = lax.slice_in_dim(x, 0, width, axis=dim)
        before = lax.ppermute(last, axis, up)
        after = lax.ppermute(first, axis, down)
        x = jnp.concatenate([before, x, after], axis=dim)
    return x


def surrogate(potential):
    return 1.0 / (1.0 + (math.pi * (potential - 1.0)) ** 2)


def offsets_list():
    return [(row_shift, col_shift) for row_shift in (-1, 0, 1) for col_shift in (-1, 0, 1)]


def on_device(frames, membrane, cotangent, master, moment, second):
    steps_count, samples, rows, cols, chans = frames.shape
    weights = lax.all_gather(master.astype(jnp.bfloat16), "dp", axis=0, tiled=True)
    stacked = jnp.concatenate([membrane[None], frames], axis=0)
    rimmed = extended(stacked, (("space", 2),), 1)
    voltage = rimmed[0].astype(jnp.float32)
    potentials = []
    fired = []
    for position in range(steps_count):
        potential = 0.5 * voltage + rimmed[position + 1].astype(jnp.float32)
        spikes = jnp.where(potential >= 1.0, jnp.float32(1.0), jnp.float32(0.0))
        voltage = potential - spikes
        potentials.append(potential[:, 1:-1])
        fired.append(spikes)
    potential_all = jnp.stack(potentials)
    spike_all = jnp.stack(fired).astype(jnp.bfloat16)
    col_pad = ((0, 0), (0, 0), (0, 0), (1, 1), (0, 0))
    spike_pad = jnp.pad(spike_all, col_pad)
    grad_rim = extended(cotangent, (("space", 2),), 1)
    grad_pad = jnp.pad(grad_rim, col_pad)
    spike_cols = jnp.concatenate(
        [spike_pad[:, :, 1 + a : 1 + a + rows, 1 + b : 1 + b + cols] for a, b in offsets_list()],
        axis=-1,
    ).reshape(-1, 9 * chans)
    grad_cols = jnp.concatenate(
        [grad_pad[:, :, 1 - a : 1 - a + rows, 1 - b : 1 - b + cols] for a, b in offsets_list()],
        axis=-1,
    ).reshape(-1, 9, chans)
    grad_flat = cotangent.reshape(-1, chans)
    weight_local = lax.dot_general(
        spike_cols, grad_flat, (((0,), (0,)), ((), ())), preferred_element_type=jnp.float32
    )
    dspikes = jnp.einsum(
        "nkd,kcd->nc",
        grad_cols,
        weights.reshape(9, chans, chans),
        preferred_element_type=jnp.float32,
    )
    dspikes = dspikes.reshape(steps_count, samples, rows, cols, chans)
    carried = jnp.zeros((samples, rows, cols, chans), jnp.float32)
    outs = [None] * steps_count
    for position in reversed(range(steps_count)):
        carried = dspikes[position] * surrogate(potential_all[position]) + 0.5 * carried
        outs[position] = (cotangent[position].astype(jnp.float32) + carried).astype(jnp.bfloat16)
    grad_input = jnp.stack(outs)
    membrane_grad = 0.5 * carried
    data_count = lax.axis_size("dp")
    total_cells = samples * data_count * lax.axis_size("rep") * rows * lax.axis_size("space") * cols
    shard_part = lax.psum_scatter(weight_local, "dp", scatter_dimension=0, tiled=True)
    summed = lax.psum(shard_part, ("space", "rep"))
    weight_grad = summed * (1.0 / math.sqrt(steps_count * total_cells))
    new_moment = 0.9 * moment + 0.1 * weight_grad
    new_second = 0.95 * second + 0.05 * weight_grad * weight_grad
    update = new_moment / (jnp.sqrt(new_second) + 1e-08)
    return (grad_input, membrane_grad, weight_grad, new_moment, new_second, update)


def solution(mesh):
    return jax.shard_map(
        on_device,
        mesh=mesh,
        in_specs=(
            P(None, ("dp", "rep"), "space", None, None),
            P(("dp", "rep"), "space", None, None),
            P(None, ("dp", "rep"), "space", None, None),
            P("dp", None),
            P("dp", None),
            P("dp", None),
        ),
        out_specs=(
            P(None, ("dp", "rep"), "space", None, None),
            P(("dp", "rep"), "space", None, None),
            P("dp", None),
            P("dp", None),
            P("dp", None),
            P("dp", None),
        ),
        check_vma=False,
    )
```

profile of v0, /device:TPU:0, one launch (start us, length us, event | category | flops | bytes accessed | tf_op | source)
XLA Modules:
  0.0 351.5 jit_solution(18133478292274602957)
XLA Ops:
  7.2 0.0 all-gather.2.cloned.1.call-start
  7.2 1.1 pad_maximum_fusion.4
  8.3 1.3 collective-permute-start.3
  9.6 3.2 collective-permute-start.2
  12.8 2.8 convert_element_type.357
  15.6 0.0 all-gather.2.cloned.1.call-update
  15.6 0.0 reduce-scatter.2.cloned.1.call-start
  15.7 1.8 pad_maximum_fusion
  17.5 0.1 fusion.76
  17.6 0.3 fusion.78
  17.9 0.4 fusion.80
  18.3 0.5 fusion.82
  18.9 0.2 fusion.83
  19.0 0.3 fusion.74
  19.4 0.5 fusion.16
  19.9 0.1 slice_dynamic-update-slice_fusion.2
  20.0 0.7 fusion.17
  20.7 0.7 fusion.18
  21.5 0.1 slice_dynamic-update-slice_fusion.1
  21.6 0.7 fusion.19
  22.3 0.8 fusion.20
  23.0 0.1 slice_dynamic-update-slice_fusion
  23.2 0.7 fusion.21
  23.9 0.7 copy-done
  24.6 10.2 %fusion.4 = f32[4608,512]{1,0:T(8,128)} fusion(bf16[6,1,8,32,4608]{4,3,2,0,1:T(8,128)(2,1)S(1)} %fusion.21, bf16[6,1,8,32,512]{4,3,2,1,0:T(8,128)(2,1)S(1)} %copy-done), kind=kOutput, calls=%fused_computation.4 | convolution fusion | flops 7247757312 | bytes 25165824 | tf_op jit(solution)/shard_map/dot_general | solution.py:59
  34.8 0.0 all-reduce.4.cloned.1.call-start
  34.8 1.1 fusion.104
  35.9 1.3 collective-permute-start.1
  37.2 5.5 %collective-permute-start = (bf16[6,1,1,32,512]{4,3,2,1,0:T(8,128)(2,1)S(1)}, bf16[6,1,1,32,512]{4,3,2,1,0:T(8,128)(2,1)S(1)}, u32[]{:S(2)}, u32[]{:S(2)}) collective-permute-start(bf16[6,1,1,32,512]{4,3,2,1,0:T(8,128)(2,1)S(1)} %get-tuple-element.29), channel_id=1, source_target_pairs={{0,2},{2,4},{4,6},{1,3},{3,5},{5,7},{8,10},{10,12},{12,14},{9,11},... | collective-permute-start | bytes 589832 | tf_op jit(solution)/shard_map/ppermute | solution.py:16
  42.7 0.8 collective-permute-done
  43.5 2.3 fusion.15
  45.9 1.7 slice_dynamic-update-slice_fusion.8
  47.5 1.4 fusion.23
  49.0 1.4 slice_dynamic-update-slice_fusion.7
  50.4 2.1 slice_dynamic-update-slice_fusion.6
  52.5 1.4 constant_dynamic-update-slice_fusion
  53.8 1.4 slice_dynamic-update-slice_fusion.5
  55.2 2.0 slice_dynamic-update-slice_fusion.4
  57.2 1.4 fusion.22
  58.6 1.4 slice_dynamic-update-slice_fusion.3
  60.0 26.6 %reshape.515 = bf16[1536,9,512]{2,1,0:T(8,128)(2,1)} reshape(bf16[6,1,8,32,4608]{4,3,2,1,0:T(8,128)(2,1)} %slice_dynamic-update-slice_fusion.3) | data formatting | bytes 28311552 | tf_op jit(solution)/shard_map/reshape | solution.py:57
  86.6 1.0 fusion.73
  87.6 0.9 convert_bitcast_fusion.1
  88.6 1.8 fusion.28
  90.4 17.5 %all-gather.2.cloned.1.call-done = bf16[4608,512]{1,0:T(8,128)(2,1)} async-done(((bf16[1152,512]{1,0:T(8,128)(2,1)}), bf16[4608,512]{1,0:T(8,128)(2,1)}) %all-gather.2.cloned.1.call-update) | async-done | bytes 4718608 | tf_op jit(solution)/shard_map/all_gather | solution.py:32
  107.9 25.8 %fusion.8 = f32[1536,512]{1,0:T(8,128)S(1)} fusion(bf16[9,512,512]{2,1,0:T(8,128)(2,1)} %bitcast.158, bf16[1536,9,512]{2,1,0:T(8,128)(2,1)} %reshape.515), kind=kOutput, calls=%fused_computation.8 | convolution fusion | flops 7247757312 | bytes 22020096 | tf_op jit(solution)/shard_map/nkd,kcd->nc/dot_general | solution.py:62
  133.8 0.3 fusion.103
  134.1 0.7 copy-done.4
  134.8 0.2 copy-done.6
  135.0 0.2 copy-done.7
  135.2 0.2 copy-done.8
  135.4 0.2 copy-done.9
  135.6 0.2 copy-done.10
  135.8 1.7 broadcast_multiply_fusion.1
  137.6 0.8 fusion.85
  138.3 131.7 %reduce-scatter.2.cloned.1.call-done = f32[1152,512]{1,0:T(8,128)} async-done(((f32[4608,512]{1,0:T(8,128)}), f32[1152,512]{1,0:T(8,128)}) %reduce-scatter.2.cloned.1.call-update) | async-done | bytes 2359312 | tf_op jit(solution)/shard_map/reduce_scatter | solution.py:78
  270.0 0.0 all-reduce.4.cloned.1.call-update
  270.1 2.2 fusion.87
  272.3 0.8 fusion.89
  273.1 0.8 fusion.91
  273.9 0.9 fusion.93
  274.8 0.8 fusion.95
  275.6 61.5 %all-reduce.4.cloned.1.call-done = f32[1152,512]{1,0:T(8,128)} async-done(((f32[1152,512]{1,0:T(8,128)}), f32[1152,512]{1,0:T(8,128)}) %all-reduce.4.cloned.1.call-update) | async-done | bytes 2359312 | tf_op jit(solution)/shard_map/psum | solution.py:79
  337.1 7.9 %add_divide_fusion = (f32[1152,512]{1,0:T(8,128)}, f32[1152,512]{1,0:T(8,128)}, f32[1152,512]{1,0:T(8,128)}, f32[1152,512]{1,0:T(8,128)}) fusion(f32[1152,512]{1,0:T(8,128)} %all-reduce.4.cloned.1.call-done, f32[1152,512]{1,0:T(8,128)} %param.11, f32[1152,512]{1,0:T(8,128)} %param.10), kind=kLoop, calls=%fused_computation.14 | loop fusion | flops 5898240 | bytes 16515072 | tf_op jit(solution)/shard_map/div | solution.py:83
  (23 shorter events, 0.1 us)
Async XLA Ops:
  7.2 100.7 %all-gather.2.cloned.1.call-start = ((), (), s32[]{:S(2)}) async-start(), calls=%async_computation.1 | async-start | bytes 5898240 | tf_op jit(solution)/shard_map/all_gather | solution.py:32
  8.3 7.4 %collective-permute-start.3 = (bf16[7,1,1,32,512]{4,3,2,1,0:T(8,128)(2,1)S(1)}, bf16[7,1,1,32,512]{4,3,2,1,0:T(8,128)(2,1)S(1)}, u32[]{:S(2)}, u32[]{:S(2)}) collective-permute-start(bf16[7,1,1,32,512]{4,3,2,1,0:T(8,128)(2,1)S(1)} %get-tuple-element.28), channel_id=1, source_target_pairs={{2,0},{4,2},{6,4},{3,1},{5,3},{7,5},{10,8},{12,10},{14,12},{11,9},... | collective-permute-start | bytes 688136 | tf_op jit(solution)/shard_map/ppermute | solution.py:17
  9.6 6.1 %copy-start.12 = (bf16[1,8,32,512]{3,2,1,0:T(8,128)(2,1)S(1)}, bf16[1,8,32,512]{3,2,1,0:T(8,128)(2,1)}, u32[]{:S(2)}) copy-start(bf16[1,8,32,512]{3,2,1,0:T(8,128)(2,1)} %param.7) | copy-start | bytes 786436
  9.6 6.1 %collective-permute-start.2 = (bf16[7,1,1,32,512]{4,3,2,1,0:T(8,128)(2,1)S(1)}, bf16[7,1,1,32,512]{4,3,2,1,0:T(8,128)(2,1)S(1)}, u32[]{:S(2)}, u32[]{:S(2)}) collective-permute-start(bf16[7,1,1,32,512]{4,3,2,1,0:T(8,128)(2,1)S(1)} %get-tuple-element.27), channel_id=1, source_target_pairs={{0,2},{2,4},{4,6},{1,3},{3,5},{5,7},{8,10},{10,12},{12,14},{9,11},... | collective-permute-start | bytes 688136 | tf_op jit(solution)/shard_map/ppermute | solution.py:16
  15.6 254.4 %reduce-scatter.2.cloned.1.call-start = ((), (), s32[]{:S(2)}) async-start(), calls=%async_computation.2 | async-start | bytes 11796480 | tf_op jit(solution)/shard_map/reduce_scatter | solution.py:78
  23.2 1.4 copy-start
  34.8 302.3 %all-reduce.4.cloned.1.call-start = ((), (), s32[]{:S(2)}) async-start(), calls=%async_computation.3 | async-start | bytes 4718592 | tf_op jit(solution)/shard_map/psum | solution.py:79
  35.9 6.8 %collective-permute-start.1 = (bf16[6,1,1,32,512]{4,3,2,1,0:T(8,128)(2,1)S(1)}, bf16[6,1,1,32,512]{4,3,2,1,0:T(8,128)(2,1)S(1)}, u32[]{:S(2)}, u32[]{:S(2)}) collective-permute-start(bf16[6,1,1,32,512]{4,3,2,1,0:T(8,128)(2,1)S(1)} %get-tuple-element.30), channel_id=1, source_target_pairs={{2,0},{4,2},{6,4},{3,1},{5,3},{7,5},{10,8},{12,10},{14,12},{11,9},... | collective-permute-start | bytes 589832 | tf_op jit(solution)/shard_map/ppermute | solution.py:17
  37.2 6.3 %collective-permute-start = (bf16[6,1,1,32,512]{4,3,2,1,0:T(8,128)(2,1)S(1)}, bf16[6,1,1,32,512]{4,3,2,1,0:T(8,128)(2,1)S(1)}, u32[]{:S(2)}, u32[]{:S(2)}) collective-permute-start(bf16[6,1,1,32,512]{4,3,2,1,0:T(8,128)(2,1)S(1)} %get-tuple-element.29), channel_id=1, source_target_pairs={{0,2},{2,4},{4,6},{1,3},{3,5},{5,7},{8,10},{10,12},{12,14},{9,11},... | collective-permute-start | bytes 589832 | tf_op jit(solution)/shard_map/ppermute | solution.py:16
  45.8 1.7 copy-start.1
  133.7 1.1 copy-start.4
  133.7 1.3 copy-start.6
  133.7 1.5 copy-start.7
  133.8 1.7 copy-start.8
  133.8 1.8 copy-start.9
  133.8 2.0 copy-start.10
  135.8 1.7 copy-start.2
  270.1 2.3 copy-start.3
  270.1 3.0 copy-start.11
  270.1 3.8 %copy-start.5 = (f32[1,10,32,512]{3,2,1,0:T(8,128)S(1)}, f32[1,10,32,512]{3,2,1,0:T(8,128)}, u32[]{:S(2)}) copy-start(f32[1,10,32,512]{3,2,1,0:T(8,128)} %get-tuple-element.17) | copy-start | bytes 1966084
Sparse Core Ops, SparseCore 0:
  15.8 92.1 all-gather.1
  110.3 159.7 reduce-scatter.1
  273.3 63.7 all-reduce.3
where the time goes:
time: 353 us; the launch traced here: 352 us
  waiting for transfers between devices  212 us (60%)
  local copies, waits for them, and re-layouts  46.2 us (13%)
  matrix products  36 us (10%)
  other arithmetic  32.3 us (9%)
  between operations  14.1 us (4%)
  starting transfers between devices  11.3 us (3%)
    reduce_scatter x1, waiting for transfers between devices, on_device(): lax.psum_scatter(weight_local, 'dp', scatter_dimension=0, tiled=True)  132 us
    psum x1, waiting for transfers between devices, on_device(): summed = lax.psum(shard_part, ('space', 'rep'))  61.5 us
    reshape x1, local copies, waits for them, and re-layouts, on_device(): grad_cols = jnp.concatenate([grad_pad[:, :, 1 - a:1 - a + rows, 1 - b:1 -...  26.6 us
    dot_general x1, matrix products, on_device(): jnp.einsum('nkd,kcd->nc', grad_cols, weights.reshape(9, chans, chans), pr...  25.8 us
    all_gather x1, waiting for transfers between devices, on_device(): lax.all_gather(master.astype(jnp.bfloat16), 'dp', axis=0, tiled=True)  17.5 us
    unnamed x40, local copies, waits for them, and re-layouts  16.1 us
    dot_general x1, matrix products, on_device(): lax.dot_general(spike_cols, grad_flat, (((0,), (0,)), ((), ())), preferre...  10.2 us
    unnamed x12, other arithmetic  9.82 us
  transfers between devices with their start and end apart: 7, of which 4 were waited for; matrix products, arithmetic and copies ran while one was open for 29% of the time, Pallas kernels for 0%

commit v1 on v0

--- a/solution.py
+++ b/solution.py
@@ -29,7 +29,16 @@
 
 def on_device(frames, membrane, cotangent, master, moment, second):
     steps_count, samples, rows, cols, chans = frames.shape
-    weights = lax.all_gather(master.astype(jnp.bfloat16), "dp", axis=0, tiled=True)
+    rest = ("space", "rep")
+    rest_count = lax.axis_size("space") * lax.axis_size("rep")
+    data_count = lax.axis_size("dp")
+    shard_rows = master.shape[0]
+    piece_rows = shard_rows // rest_count
+    local = master.astype(jnp.bfloat16)
+    piece = lax.dynamic_slice_in_dim(local, lax.axis_index(rest) * piece_rows, piece_rows, 0)
+    over_dp = lax.all_gather(piece, "dp", axis=0, tiled=False)
+    over_all = lax.all_gather(over_dp, rest, axis=0, tiled=False)
+    weights = jnp.swapaxes(over_all, 0, 1).reshape(data_count * shard_rows, master.shape[1])
     stacked = jnp.concatenate([membrane[None], frames], axis=0)
     rimmed = extended(stacked, (("space", 2),), 1)
     voltage = rimmed[0].astype(jnp.float32)
@@ -73,10 +82,9 @@
         outs[position] = (cotangent[position].astype(jnp.float32) + carried).astype(jnp.bfloat16)
     grad_input = jnp.stack(outs)
     membrane_grad = 0.5 * carried
-    data_count = lax.axis_size("dp")
     total_cells = samples * data_count * lax.axis_size("rep") * rows * lax.axis_size("space") * cols
-    shard_part = lax.psum_scatter(weight_local, "dp", scatter_dimension=0, tiled=True)
-    summed = lax.psum(shard_part, ("space", "rep"))
+    shard_part = lax.psum_scatter(weight_local, ("dp",) + rest, scatter_dimension=0, tiled=True)
+    summed = lax.all_gather(shard_part, rest, axis=0, tiled=True)
     weight_grad = summed * (1.0 / math.sqrt(steps_count * total_cells))
     new_moment = 0.9 * moment + 0.1 * weight_grad
     new_second = 0.95 * second + 0.05 * weight_grad * weight_grad

time: 353 us -> 240 us (0.68)
  waiting for transfers between devices: 212 us -> 78.9 us
  blocking collectives: 0 us -> 19.5 us
  local copies, waits for them, and re-layouts: 46.2 us -> 51.4 us
  other arithmetic: 32.3 us -> 28.1 us
    psum x1 -> x0, waiting for transfers between devices: 61.5 us -> none  [on_device(): summed = lax.psum(shard_part, ('space', 'rep'))]
    reduce_scatter x1, waiting for transfers between devices: 132 us -> 77.7 us  [on_device(): lax.psum_scatter(weight_local, ('dp',) + rest, scatter_dimension=0, tiled...]
    all_gather x0 -> x1, blocking collectives: none -> 19.5 us  [on_device(): over_dp = lax.all_gather(piece, 'dp', axis=0, tiled=False)]
    all_gather x1 -> x2, waiting for transfers between devices: 17.5 us -> 0.01 us  [the longest x1 0.01 us: on_device(): over_all = lax.all_gather(over_dp, rest, axis=0, tiled=False)]
    transpose x0 -> x1, local copies, waits for them, and re-layouts: none -> 4.98 us  [on_device(): jnp.swapaxes(over_all, 0, 1)]
    unnamed x40 -> x36, local copies, waits for them, and re-layouts: 16.1 us -> 15.9 us
  transfers between devices with their start and end apart: 7 -> 7, of which waited for: 4 -> 2; matrix products, arithmetic and copies ran while one was open for 29% -> 43% of each run, Pallas kernels for 0% -> 0%
where the time goes in v1:
time: 240 us; the launch traced here: 238 us
  waiting for transfers between devices  78.9 us (33%)
  local copies, waits for them, and re-layouts  51.4 us (21%)
  matrix products  35.8 us (15%)
  other arithmetic  28.1 us (12%)
  blocking collectives  19.5 us (8%)
  between operations  15.8 us (7%)
  starting transfers between devices  8.97 us (4%)
    reduce_scatter x1, waiting for transfers between devices, on_device(): lax.psum_scatter(weight_local, ('dp',) + rest, scatter_dimension=0, tiled...  77.7 us
    reshape x1, local copies, waits for them, and re-layouts, on_device(): grad_cols = jnp.concatenate([grad_pad[:, :, 1 - a:1 - a + rows, 1 - b:1 -...  26.9 us
    dot_general x1, matrix products, on_device(): jnp.einsum('nkd,kcd->nc', grad_cols, weights.reshape(9, chans, chans), pr...  25.6 us
    all_gather x1, blocking collectives, on_device(): over_dp = lax.all_gather(piece, 'dp', axis=0, tiled=False)  19.5 us
    unnamed x36, local copies, waits for them, and re-layouts  15.9 us
    dot_general x1, matrix products, on_device(): lax.dot_general(spike_cols, grad_flat, (((0,), (0,)), ((), ())), preferre...  10.2 us
    unnamed x12, other arithmetic  8.48 us
    div x1, other arithmetic, on_device(): update = new_moment / (jnp.sqrt(new_second) + 1e-08)  8.02 us
  transfers between devices with their start and end apart: 7, of which 2 were waited for; matrix products, arithmetic and copies ran while one was open for 43% of the time, Pallas kernels for 0%

profile of v1, /device:TPU:0, one launch (start us, length us, event | category | flops | bytes accessed | tf_op | source)
XLA Modules:
  0.0 238.4 jit_solution(17857498897906321048)
XLA Ops:
  8.0 0.0 copy-start
  8.0 0.0 all-gather.7.cloned.1.call-start
  8.1 1.2 pad_maximum_fusion.4
  9.3 1.3 collective-permute-start.3
  10.6 3.0 %collective-permute-start.2 = (bf16[7,1,1,32,512]{4,3,2,1,0:T(8,128)(2,1)S(1)}, bf16[7,1,1,32,512]{4,3,2,1,0:T(8,128)(2,1)S(1)}, u32[]{:S(2)}, u32[]{:S(2)}) collective-permute-start(bf16[7,1,1,32,512]{4,3,2,1,0:T(8,128)(2,1)S(1)} %get-tuple-element.27), channel_id=1, source_target_pairs={{0,2},{2,4},{4,6},{1,3},{3,5},{5,7},{8,10},{10,12},{12,14},{9,11},... | collective-permute-start | bytes 688136 | tf_op jit(solution)/shard_map/ppermute | solution.py:16
  13.7 19.5 %all-gather = bf16[576,512]{1,0:T(8,128)(2,1)} all-gather(bf16[144,512]{1,0:T(8,128)(2,1)S(1)} %dynamic-slice_convert_fusion), channel_id=2, replica_groups=mesh['dp'=4,'space'=4,'rep'=2] {'dp'}, dimensions={0}, use_global_device_ids=true | all-gather | bytes 737280 | tf_op jit(solution)/shard_map/all_gather | solution.py:39
  33.2 0.0 all-gather.7.cloned.1.call-update
  33.2 0.0 reduce-scatter.2.cloned.1.call-start
  33.3 1.8 pad_maximum_fusion
  35.1 0.1 fusion.76
  35.2 0.3 fusion.78
  35.5 0.4 fusion.80
  35.9 0.5 fusion.82
  36.5 0.2 fusion.83
  36.7 0.3 fusion.74
  37.0 0.5 fusion.16
  37.5 0.1 slice_dynamic-update-slice_fusion.2
  37.6 0.7 fusion.17
  38.3 0.7 fusion.18
  39.1 0.1 slice_dynamic-update-slice_fusion.1
  39.2 0.7 fusion.19
  39.9 0.7 fusion.20
  40.6 0.1 slice_dynamic-update-slice_fusion
  40.8 0.7 fusion.21
  41.5 0.8 copy-done.2
  42.3 10.2 %fusion.4 = f32[4608,512]{1,0:T(8,128)} fusion(bf16[6,1,8,32,4608]{4,3,2,0,1:T(8,128)(2,1)S(1)} %fusion.21, bf16[6,1,8,32,512]{4,3,2,1,0:T(8,128)(2,1)S(1)} %copy-done.2), kind=kOutput, calls=%fused_computation.4 | convolution fusion | flops 7247757312 | bytes 25165824 | tf_op jit(solution)/shard_map/dot_general | solution.py:68
  52.5 0.0 reduce-scatter.2.cloned.1.call-update
  52.5 0.0 all-gather.5.cloned.1.call-start
  52.5 1.1 fusion.104
  53.6 1.3 collective-permute-start.1
  54.9 3.2 %collective-permute-start = (bf16[6,1,1,32,512]{4,3,2,1,0:T(8,128)(2,1)S(1)}, bf16[6,1,1,32,512]{4,3,2,1,0:T(8,128)(2,1)S(1)}, u32[]{:S(2)}, u32[]{:S(2)}) collective-permute-start(bf16[6,1,1,32,512]{4,3,2,1,0:T(8,128)(2,1)S(1)} %get-tuple-element.29), channel_id=1, source_target_pairs={{0,2},{2,4},{4,6},{1,3},{3,5},{5,7},{8,10},{10,12},{12,14},{9,11},... | collective-permute-start | bytes 589832 | tf_op jit(solution)/shard_map/ppermute | solution.py:16
  58.1 1.1 collective-permute-done
  59.2 2.3 fusion.15
  61.6 1.7 slice_dynamic-update-slice_fusion.8
  63.3 1.5 fusion.23
  64.7 1.4 slice_dynamic-update-slice_fusion.7
  66.1 2.0 slice_dynamic-update-slice_fusion.6
  68.1 1.4 constant_dynamic-update-slice_fusion
  69.5 1.4 slice_dynamic-update-slice_fusion.5
  70.9 2.0 slice_dynamic-update-slice_fusion.4
  72.9 1.4 fusion.22
  74.2 1.5 slice_dynamic-update-slice_fusion.3
  75.7 26.9 %reshape.512 = bf16[1536,9,512]{2,1,0:T(8,128)(2,1)} reshape(bf16[6,1,8,32,4608]{4,3,2,1,0:T(8,128)(2,1)} %slice_dynamic-update-slice_fusion.3) | data formatting | bytes 28311552 | tf_op jit(solution)/shard_map/reshape | solution.py:66
  102.6 0.9 fusion.73
  103.5 0.9 convert_bitcast_fusion.1
  104.4 1.6 fusion.28
  106.1 5.0 %copy.54 = bf16[4,8,144,512]{3,2,1,0:T(8,128)(2,1)} copy(bf16[4,8,144,512]{3,2,0,1:T(8,128)(2,1)} %bitcast.156) | data formatting | bytes 9437184 | tf_op jit(solution)/shard_map/transpose | solution.py:41
  111.0 77.7 %reduce-scatter.2.cloned.1.call-done = f32[144,512]{1,0:T(8,128)} async-done(((f32[4608,512]{1,0:T(8,128)}), f32[144,512]{1,0:T(8,128)}) %reduce-scatter.2.cloned.1.call-update) | async-done | bytes 294928 | tf_op jit(solution)/shard_map/reduce_scatter | solution.py:86
  188.8 0.0 all-gather.5.cloned.1.call-update
  188.8 25.6 %fusion.8 = f32[1536,512]{1,0:T(8,128)S(1)} fusion(bf16[9,512,512]{2,1,0:T(8,128)(2,1)} %bitcast.157, bf16[1536,9,512]{2,1,0:T(8,128)(2,1)} %reshape.512), kind=kOutput, calls=%fused_computation.8 | convolution fusion | flops 7247757312 | bytes 22020096 | tf_op jit(solution)/shard_map/nkd,kcd->nc/dot_general | solution.py:71
  214.5 0.3 fusion.103
  214.8 0.7 copy-done.5
  215.5 0.2 copy-done.6
  215.7 0.2 copy-done.7
  215.9 0.2 copy-done.8
  216.1 0.2 copy-done.9
  216.3 1.7 broadcast_multiply_fusion.1
  218.0 0.8 fusion.85
  218.8 0.9 fusion.87
  219.7 0.8 fusion.89
  220.5 0.8 fusion.91
  221.3 0.9 fusion.93
  222.2 0.8 fusion.95
  223.0 8.0 %add_divide_fusion = (f32[1152,512]{1,0:T(8,128)}, f32[1152,512]{1,0:T(8,128)}, f32[1152,512]{1,0:T(8,128)}, f32[1152,512]{1,0:T(8,128)}) fusion(f32[1152,512]{1,0:T(8,128)} %all-gather.5.cloned.1.call-done, f32[1152,512]{1,0:T(8,128)} %param.11, f32[1152,512]{1,0:T(8,128)} %param.10), kind=kLoop, calls=%fused_computation.14 | loop fusion | flops 5898240 | bytes 16515072 | tf_op jit(solution)/shard_map/div | solution.py:91
  (21 shorter events, 0.1 us)
Async XLA Ops:
  8.0 5.7 %copy-start = (f32[1152,512]{1,0:T(8,128)S(1)}, f32[1152,512]{1,0:T(8,128)}, u32[]{:S(2)}) copy-start(f32[1152,512]{1,0:T(8,128)} %param.9) | copy-start | bytes 7077892
  8.0 25.3 %copy-start.10 = (bf16[1,8,32,512]{3,2,1,0:T(8,128)(2,1)S(1)}, bf16[1,8,32,512]{3,2,1,0:T(8,128)(2,1)}, u32[]{:S(2)}) copy-start(bf16[1,8,32,512]{3,2,1,0:T(8,128)(2,1)} %param.7) | copy-start | bytes 786436
  8.0 98.0 %all-gather.7.cloned.1.call-start = ((), (), s32[]{:S(2)}) async-start(), calls=%async_computation.3 | async-start | bytes 5308416 | tf_op jit(solution)/shard_map/all_gather | solution.py:40
  9.3 24.0 %collective-permute-start.3 = (bf16[7,1,1,32,512]{4,3,2,1,0:T(8,128)(2,1)S(1)}, bf16[7,1,1,32,512]{4,3,2,1,0:T(8,128)(2,1)S(1)}, u32[]{:S(2)}, u32[]{:S(2)}) collective-permute-start(bf16[7,1,1,32,512]{4,3,2,1,0:T(8,128)(2,1)S(1)} %get-tuple-element.28), channel_id=1, source_target_pairs={{2,0},{4,2},{6,4},{3,1},{5,3},{7,5},{10,8},{12,10},{14,12},{11,9},... | collective-permute-start | bytes 688136 | tf_op jit(solution)/shard_map/ppermute | solution.py:17
  10.6 22.7 %collective-permute-start.2 = (bf16[7,1,1,32,512]{4,3,2,1,0:T(8,128)(2,1)S(1)}, bf16[7,1,1,32,512]{4,3,2,1,0:T(8,128)(2,1)S(1)}, u32[]{:S(2)}, u32[]{:S(2)}) collective-permute-start(bf16[7,1,1,32,512]{4,3,2,1,0:T(8,128)(2,1)S(1)} %get-tuple-element.27), channel_id=1, source_target_pairs={{0,2},{2,4},{4,6},{1,3},{3,5},{5,7},{8,10},{10,12},{12,14},{9,11},... | collective-permute-start | bytes 688136 | tf_op jit(solution)/shard_map/ppermute | solution.py:16
  33.2 155.5 %reduce-scatter.2.cloned.1.call-start = ((), (), s32[]{:S(2)}) async-start(), calls=%async_computation.1 | async-start | bytes 9732096 | tf_op jit(solution)/shard_map/reduce_scatter | solution.py:86
  40.8 1.5 copy-start.2
  52.5 170.5 %all-gather.5.cloned.1.call-start = ((), (), s32[]{:S(2)}) async-start(), calls=%async_computation.2 | async-start | bytes 2654208 | tf_op jit(solution)/shard_map/all_gather | solution.py:87
  53.6 4.5 %collective-permute-start.1 = (bf16[6,1,1,32,512]{4,3,2,1,0:T(8,128)(2,1)S(1)}, bf16[6,1,1,32,512]{4,3,2,1,0:T(8,128)(2,1)S(1)}, u32[]{:S(2)}, u32[]{:S(2)}) collective-permute-start(bf16[6,1,1,32,512]{4,3,2,1,0:T(8,128)(2,1)S(1)} %get-tuple-element.30), channel_id=1, source_target_pairs={{2,0},{4,2},{6,4},{3,1},{5,3},{7,5},{10,8},{12,10},{14,12},{11,9},... | collective-permute-start | bytes 589832 | tf_op jit(solution)/shard_map/ppermute | solution.py:17
  54.9 4.3 %collective-permute-start = (bf16[6,1,1,32,512]{4,3,2,1,0:T(8,128)(2,1)S(1)}, bf16[6,1,1,32,512]{4,3,2,1,0:T(8,128)(2,1)S(1)}, u32[]{:S(2)}, u32[]{:S(2)}) collective-permute-start(bf16[6,1,1,32,512]{4,3,2,1,0:T(8,128)(2,1)S(1)} %get-tuple-element.29), channel_id=1, source_target_pairs={{0,2},{2,4},{4,6},{1,3},{3,5},{5,7},{8,10},{10,12},{12,14},{9,11},... | collective-permute-start | bytes 589832 | tf_op jit(solution)/shard_map/ppermute | solution.py:16
  61.6 1.7 copy-start.3
  214.4 1.1 copy-start.5
  214.4 1.3 copy-start.6
  214.4 1.5 copy-start.7
  214.4 1.7 copy-start.8
  214.5 1.9 copy-start.9
  216.3 1.7 copy-start.4
  223.0 8.0 %copy-start.1 = (f32[1152,512]{1,0:T(8,128)S(1)}, f32[1152,512]{1,0:T(8,128)}, u32[]{:S(2)}) copy-start(f32[1152,512]{1,0:T(8,128)} %param.9) | copy-start | bytes 7077892
Sparse Core Ops, SparseCore 0:
  33.4 40.9 all-gather.6
  188.9 27.8 all-gather.4
Sparse Core Ops, SparseCore 1:
  52.6 136.1 reduce-scatter.1

commit v2 on v1

--- a/solution.py
+++ b/solution.py
@@ -17,6 +17,25 @@
         after = lax.ppermute(first, axis, down)
         x = jnp.concatenate([before, x, after], axis=dim)
     return x
+
+
+def halving_scatter(blocks, layout):
+    names = list(layout)
+    stage_list = sorted(layout, key=lambda e: (["space", "rep", "dp"].index(e[0]), e[1]))
+    for axis, bit in stage_list:
+        dim = names.index((axis, bit))
+        peers = lax.axis_size(axis)
+        mine = (lax.axis_index(axis) // (1 << bit)) % 2
+        keep = lax.dynamic_index_in_dim(blocks, mine, dim, keepdims=False)
+        send = lax.dynamic_index_in_dim(blocks, 1 - mine, dim, keepdims=False)
+        pairs = [(j, j ^ (1 << bit)) for j in range(peers)]
+        blocks = keep + lax.ppermute(send, axis, pairs)
+        names.pop(dim)
+    return blocks
+
+
+def bit_count(n):
+    return n.bit_length() - 1
 
 
 def surrogate(potential):
@@ -83,7 +102,11 @@
     grad_input = jnp.stack(outs)
     membrane_grad = 0.5 * carried
     total_cells = samples * data_count * lax.axis_size("rep") * rows * lax.axis_size("space") * cols
-    shard_part = lax.psum_scatter(weight_local, ("dp",) + rest, scatter_dimension=0, tiled=True)
+    layout = []
+    for axis in ("dp",) + rest:
+        layout += [(axis, bit) for bit in reversed(range(bit_count(lax.axis_size(axis))))]
+    piece_shape = (weight_local.shape[0] // 2 ** len(layout), weight_local.shape[1])
+    shard_part = halving_scatter(weight_local.reshape((2,) * len(layout) + piece_shape), layout)
     summed = lax.all_gather(shard_part, rest, axis=0, tiled=True)
     weight_grad = summed * (1.0 / math.sqrt(steps_count * total_cells))
     new_moment = 0.9 * moment + 0.1 * weight_grad

time: 240 us -> 294 us (1.23)
  local copies, waits for them, and re-layouts: 51.4 us -> 83.9 us
  starting transfers between devices: 8.97 us -> 22.4 us
  other arithmetic: 28.1 us -> 36.2 us
    ppermute x0 -> x5, waiting for transfers between devices: none -> 78.5 us  [halving_scatter(): blocks = keep + lax.ppermute(send, axis, pairs)]
    reduce_scatter x1 -> x0, waiting for transfers between devices: 77.7 us -> none  [on_device(): lax.psum_scatter(weight_local, ('dp',) + rest, scatter_dimension=0, tiled...]
    reshape x0 -> x1, local copies, waits for them, and re-layouts: none -> 18.6 us  [on_device(): spike_cols = jnp.concatenate([spike_pad[:, :, 1 + a:1 + a + rows, 1 + b:1...]
    ppermute x0 -> x5, starting transfers between devices: none -> 13.5 us  [halving_scatter(): blocks = keep + lax.ppermute(send, axis, pairs)]
    add x0 -> x5, other arithmetic: none -> 9.3 us  [halving_scatter(): blocks = keep + lax.ppermute(send, axis, pairs)]
    unnamed x36 -> x48, local copies, waits for them, and re-layouts: 15.9 us -> 22.7 us
    squeeze x0 -> x4, local copies, waits for them, and re-layouts: none -> 4.81 us  [halving_scatter(): send = lax.dynamic_index_in_dim(blocks, 1 - mine, dim, keepdims=False)]
    dynamic_slice x0 -> x2, local copies, waits for them, and re-layouts: none -> 3.58 us  [the longest x1 1.97 us: halving_scatter(): keep = lax.dynamic_index_in_dim(blocks, mine, dim, keepdims=False)]
  transfers between devices with their start and end apart: 7 -> 11, of which waited for: 2 -> 5; matrix products, arithmetic and copies ran while one was open for 43% -> 33% of each run, Pallas kernels for 0% -> 0%
where the time goes in v2:
time: 294 us; the launch traced here: 292 us
  local copies, waits for them, and re-layouts  83.9 us (29%)
  waiting for transfers between devices  80.5 us (27%)
  matrix products  36.8 us (13%)
  other arithmetic  36.2 us (12%)
  starting transfers between devices  22.4 us (8%)
  blocking collectives  17.2 us (6%)
  between operations  14.5 us (5%)
    ppermute x5, waiting for transfers between devices, halving_scatter(): blocks = keep + lax.ppermute(send, axis, pairs)  78.5 us
    reshape x1, local copies, waits for them, and re-layouts, on_device(): grad_cols = jnp.concatenate([grad_pad[:, :, 1 - a:1 - a + rows, 1 - b:1 -...  26.6 us
    dot_general x1, matrix products, on_device(): jnp.einsum('nkd,kcd->nc', grad_cols, weights.reshape(9, chans, chans), pr...  25.8 us
    unnamed x48, local copies, waits for them, and re-layouts  22.7 us
    reshape x1, local copies, waits for them, and re-layouts, on_device(): spike_cols = jnp.concatenate([spike_pad[:, :, 1 + a:1 + a + rows, 1 + b:1...  18.6 us
    all_gather x1, blocking collectives, on_device(): over_dp = lax.all_gather(piece, 'dp', axis=0, tiled=False)  17.2 us
    ppermute x5, starting transfers between devices, halving_scatter(): blocks = keep + lax.ppermute(send, axis, pairs)  13.5 us
    dot_general x1, matrix products, on_device(): lax.dot_general(spike_cols, grad_flat, (((0,), (0,)), ((), ())), preferre...  11 us
  transfers between devices with their start and end apart: 11, of which 5 were waited for; matrix products, arithmetic and copies ran while one was open for 33% of the time, Pallas kernels for 0%

profile of v2, /device:TPU:0, one launch (start us, length us, event | category | flops | bytes accessed | tf_op | source)
XLA Modules:
  0.0 291.5 jit_solution(14060493763691116597)
XLA Ops:
  7.2 1.2 pad_maximum_fusion.4
  8.5 1.3 collective-permute-start.3
  9.8 3.0 %collective-permute-start.2 = (bf16[7,1,1,32,512]{4,3,2,1,0:T(8,128)(2,1)S(1)}, bf16[7,1,1,32,512]{4,3,2,1,0:T(8,128)(2,1)S(1)}, u32[]{:S(2)}, u32[]{:S(2)}) collective-permute-start(bf16[7,1,1,32,512]{4,3,2,1,0:T(8,128)(2,1)S(1)} %get-tuple-element.31), channel_id=1, source_target_pairs={{0,2},{2,4},{4,6},{1,3},{3,5},{5,7},{8,10},{10,12},{12,14},{9,11},... | collective-permute-start | bytes 688136 | tf_op jit(solution)/shard_map/ppermute | solution.py:16
  12.9 1.1 collective-permute-done.2
  13.9 1.8 pad_maximum_fusion
  16.1 0.4 fusion.69
  16.5 0.5 fusion.70
  17.3 1.2 fusion.66
  18.4 0.5 fusion.11
  19.1 0.7 fusion.12
  19.9 0.7 fusion.13
  20.8 0.7 fusion.14
  21.5 0.7 fusion.15
  22.4 0.7 fusion.16
  23.2 5.0 %copy-done.6 = bf16[6,1,8,32,4608]{4,3,2,1,0:T(8,128)(2,1)} copy-done((bf16[6,1,8,32,4608]{4,3,2,1,0:T(8,128)(2,1)}, bf16[6,1,8,32,4608]{4,3,2,1,0:T(8,128)(2,1)S(1)}, u32[]{:S(2)}) %copy-start.6) | copy-done | bytes 14155800
  28.2 18.6 %copy.20 = bf16[1536,4608]{0,1:T(8,128)(2,1)} copy(bf16[1536,4608]{1,0:T(8,128)(2,1)} %bitcast.118) | data formatting | bytes 28311552 | tf_op jit(solution)/shard_map/reshape | solution.py:81
  46.8 11.0 %fusion.93 = f32[2,2,2,2,2,144,512]{6,5,4,3,2,1,0:T(8,128)S(1)} fusion(bf16[2,2,2,2,2,144,1536]{6,5,4,3,2,1,0:T(8,128)(2,1)} %bitcast.119, bf16[1536,512,1,1,1,1,1]{1,0,6,5,4,3,2:T(8,128)(2,1)} %bitcast.117), kind=kOutput, calls=%fused_computation.159 | convolution fusion | flops 7247757312 | bytes 25165824 | tf_op jit(solution)/shard_map/dot_general | solution.py:87
  57.8 3.1 %dynamic-slice_bitcast_fusion = f32[2,2,2,2,144,512]{5,4,3,2,1,0:T(8,128)} fusion(f32[2,2,2,2,2,144,512]{6,5,4,3,2,1,0:T(8,128)S(1)} %fusion.93, s32[]{:T(128)S(6)} %select_n.237), kind=kLoop, calls=%fused_computation.6 | loop fusion | bytes 9437188 | tf_op jit(solution)/shard_map/jit(dynamic_index_in_dim)/squeeze | solution.py:30
  60.9 1.9 copy-done.8
  62.8 4.4 %collective-permute-start.4 = (f32[2,2,2,2,144,512]{5,4,3,2,1,0:T(8,128)}, f32[2,2,2,2,144,512]{5,4,3,2,1,0:T(8,128)}, u32[]{:S(2)}, u32[]{:S(2)}) collective-permute-start(f32[2,2,2,2,144,512]{5,4,3,2,1,0:T(8,128)} %dynamic-slice_bitcast_fusion), channel_id=1, source_target_pairs={{0,2},{2,0},{4,6},{6,4},{1,3},{3,1},{5,7},{7,5},{8,10},{10,8},{12,... | collective-permute-start | bytes 14155784 | tf_op jit(solution)/shard_map/ppermute | solution.py:32
  67.2 17.2 %all-gather = bf16[576,512]{1,0:T(8,128)(2,1)} all-gather(bf16[144,512]{1,0:T(8,128)(2,1)S(1)} %dynamic-slice_convert_fusion), channel_id=2, replica_groups=mesh['dp'=4,'space'=4,'rep'=2] {'dp'}, dimensions={0}, use_global_device_ids=true | all-gather | bytes 737280 | tf_op jit(solution)/shard_map/all_gather | solution.py:58
  84.7 4.9 %bitcast_add_fusion = f32[2,2,2,2,144,512]{5,4,3,2,1,0:T(8,128)S(1)} fusion(f32[2,2,2,2,144,512]{5,4,3,2,1,0:T(8,128)} %collective-permute-done.4, f32[2,2,2,2,2,144,512]{6,5,4,3,2,1,0:T(8,128)} %copy-done.8, s32[]{:T(128)S(6)} %select_n.236), kind=kLoop, calls=%fused_computation.5 | loop fusion | flops 1179648 | bytes 14155780 | tf_op jit(solution)/shard_map/add | solution.py:32
  89.7 2.0 constant_dynamic-slice_fusion.1
  91.6 1.6 copy.30
  93.2 2.8 collective-permute-start.5
  96.1 1.3 collective-permute-start.1
  97.4 3.0 %collective-permute-start = (bf16[6,1,1,32,512]{4,3,2,1,0:T(8,128)(2,1)S(1)}, bf16[6,1,1,32,512]{4,3,2,1,0:T(8,128)(2,1)S(1)}, u32[]{:S(2)}, u32[]{:S(2)}) collective-permute-start(bf16[6,1,1,32,512]{4,3,2,1,0:T(8,128)(2,1)S(1)} %get-tuple-element.33), channel_id=1, source_target_pairs={{0,2},{2,4},{4,6},{1,3},{3,5},{5,7},{8,10},{10,12},{12,14},{9,11},... | collective-permute-start | bytes 589832 | tf_op jit(solution)/shard_map/ppermute | solution.py:16
  100.6 1.0 collective-permute-done
  101.5 1.3 fusion.10
  102.8 1.7 slice_dynamic-update-slice_fusion.8
  104.5 1.4 fusion.18
  105.9 59.9 %collective-permute-done.5 = f32[2,2,2,144,512]{4,3,1,0,2:T(8,128)} collective-permute-done((f32[2,2,2,144,512]{4,3,1,0,2:T(8,128)}, f32[2,2,2,144,512]{4,3,1,0,2:T(8,128)}, u32[]{:S(2)}, u32[]{:S(2)}) %collective-permute-start.5) | collective-permute-done | bytes 2359328 | tf_op jit(solution)/shard_map/ppermute | solution.py:32
  165.8 2.2 bitcast_add_fusion.1
  168.1 1.6 collective-permute-start.6
  169.7 1.5 slice_dynamic-update-slice_fusion.7
  171.1 2.0 slice_dynamic-update-slice_fusion.6
  173.1 1.4 constant_dynamic-update-slice_fusion
  174.6 1.4 slice_dynamic-update-slice_fusion.5
  176.0 2.0 slice_dynamic-update-slice_fusion.4
  178.0 12.9 %collective-permute-done.6 = f32[2,2,144,512]{3,2,1,0:T(8,128)S(1)} collective-permute-done((f32[2,2,144,512]{3,2,1,0:T(8,128)S(1)}, f32[2,2,144,512]{3,2,1,0:T(8,128)S(1)}, u32[]{:S(2)}, u32[]{:S(2)}) %collective-permute-start.6) | collective-permute-done | bytes 1179680 | tf_op jit(solution)/shard_map/ppermute | solution.py:32
  191.1 0.9 dynamic-slice_bitcast_fusion.2
  192.0 2.0 collective-permute-start.7
  193.9 1.4 fusion.17
  195.3 1.4 slice_dynamic-update-slice_fusion.3
  196.7 26.6 %reshape.512 = bf16[1536,9,512]{2,1,0:T(8,128)(2,1)} reshape(bf16[6,1,8,32,4608]{4,3,2,1,0:T(8,128)(2,1)} %slice_dynamic-update-slice_fusion.3) | data formatting | bytes 28311552 | tf_op jit(solution)/shard_map/reshape | solution.py:85
  223.4 0.9 fusion.65
  224.3 1.2 bitcast_add_fusion.3
  225.5 0.8 dynamic-slice_bitcast_fusion.3
  226.5 2.7 collective-permute-start.8
  229.1 1.6 fusion.22
  230.8 5.0 %copy.18 = bf16[4,8,144,512]{3,2,1,0:T(8,128)(2,1)} copy(bf16[4,8,144,512]{3,2,0,1:T(8,128)(2,1)} %bitcast.124) | data formatting | bytes 9437184 | tf_op jit(solution)/shard_map/transpose | solution.py:60
  235.8 5.7 %collective-permute-done.8 = f32[144,512]{1,0:T(8,128)S(1)} collective-permute-done((f32[144,512]{1,0:T(8,128)}, f32[144,512]{1,0:T(8,128)S(1)}, u32[]{:S(2)}, u32[]{:S(2)}) %collective-permute-start.8) | collective-permute-done | bytes 294944 | tf_op jit(solution)/shard_map/ppermute | solution.py:32
  241.5 0.8 bitcast_add_fusion.4
  242.3 25.8 %fusion.3 = f32[1536,512]{1,0:T(8,128)S(1)} fusion(bf16[9,512,512]{2,1,0:T(8,128)(2,1)} %bitcast.125, bf16[1536,9,512]{2,1,0:T(8,128)(2,1)} %reshape.512), kind=kOutput, calls=%fused_computation.7 | convolution fusion | flops 7247757312 | bytes 22020096 | tf_op jit(solution)/shard_map/nkd,kcd->nc/dot_general | solution.py:90
  268.1 0.3 fusion.91
  268.5 0.7 copy-done.9
  270.0 1.7 broadcast_multiply_fusion.1
  271.7 0.8 fusion.73
  272.5 0.9 fusion.75
  273.4 0.8 fusion.77
  274.2 0.8 fusion.79
  275.0 0.9 fusion.81
  275.9 0.8 fusion.83
  276.6 8.0 %add_divide_fusion = (f32[1152,512]{1,0:T(8,128)}, f32[1152,512]{1,0:T(8,128)}, f32[1152,512]{1,0:T(8,128)}, f32[1152,512]{1,0:T(8,128)}) fusion(f32[1152,512]{1,0:T(8,128)} %all-gather.5.cloned.1.call-done, f32[1152,512]{1,0:T(8,128)} %param.11, f32[1152,512]{1,0:T(8,128)} %param.10), kind=kLoop, calls=%fused_computation.15 | loop fusion | flops 5898240 | bytes 16515072 | tf_op jit(solution)/shard_map/div | solution.py:114
  (51 shorter events, 2.9 us)
Async XLA Ops:
  7.2 60.0 %copy-start = (f32[1152,512]{1,0:T(8,128)S(1)}, f32[1152,512]{1,0:T(8,128)}, u32[]{:S(2)}) copy-start(f32[1152,512]{1,0:T(8,128)} %param.9) | copy-start | bytes 7077892
  7.2 6.7 %copy-start.16 = (bf16[1,8,32,512]{3,2,1,0:T(8,128)(2,1)S(1)}, bf16[1,8,32,512]{3,2,1,0:T(8,128)(2,1)}, u32[]{:S(2)}) copy-start(bf16[1,8,32,512]{3,2,1,0:T(8,128)(2,1)} %param.7) | copy-start | bytes 786436
  7.2 223.6 %all-gather.7.cloned.1.call-start = ((), (), s32[]{:S(2)}) async-start(), calls=%async_computation.1 | async-start | bytes 5308416 | tf_op jit(solution)/shard_map/all_gather | solution.py:59
  8.5 4.4 %collective-permute-start.3 = (bf16[7,1,1,32,512]{4,3,2,1,0:T(8,128)(2,1)S(1)}, bf16[7,1,1,32,512]{4,3,2,1,0:T(8,128)(2,1)S(1)}, u32[]{:S(2)}, u32[]{:S(2)}) collective-permute-start(bf16[7,1,1,32,512]{4,3,2,1,0:T(8,128)(2,1)S(1)} %get-tuple-element.32), channel_id=1, source_target_pairs={{2,0},{4,2},{6,4},{3,1},{5,3},{7,5},{10,8},{12,10},{14,12},{11,9},... | collective-permute-start | bytes 688136 | tf_op jit(solution)/shard_map/ppermute | solution.py:17
  9.8 4.1 %collective-permute-start.2 = (bf16[7,1,1,32,512]{4,3,2,1,0:T(8,128)(2,1)S(1)}, bf16[7,1,1,32,512]{4,3,2,1,0:T(8,128)(2,1)S(1)}, u32[]{:S(2)}, u32[]{:S(2)}) collective-permute-start(bf16[7,1,1,32,512]{4,3,2,1,0:T(8,128)(2,1)S(1)} %get-tuple-element.31), channel_id=1, source_target_pairs={{0,2},{2,4},{4,6},{1,3},{3,5},{5,7},{8,10},{10,12},{12,14},{9,11},... | collective-permute-start | bytes 688136 | tf_op jit(solution)/shard_map/ppermute | solution.py:16
  15.7 1.6 copy-start.2
  23.2 5.0 %copy-start.6 = (bf16[6,1,8,32,4608]{4,3,2,1,0:T(8,128)(2,1)}, bf16[6,1,8,32,4608]{4,3,2,1,0:T(8,128)(2,1)S(1)}, u32[]{:S(2)}) copy-start(bf16[6,1,8,32,4608]{4,3,2,1,0:T(8,128)(2,1)S(1)} %fusion.16) | copy-start | bytes 42467332
  57.8 5.0 %copy-start.8 = (f32[2,2,2,2,2,144,512]{6,5,4,3,2,1,0:T(8,128)}, f32[2,2,2,2,2,144,512]{6,5,4,3,2,1,0:T(8,128)S(1)}, u32[]{:S(2)}) copy-start(f32[2,2,2,2,2,144,512]{6,5,4,3,2,1,0:T(8,128)S(1)} %fusion.93) | copy-start | bytes 28311556
  62.8 21.9 %collective-permute-start.4 = (f32[2,2,2,2,144,512]{5,4,3,2,1,0:T(8,128)}, f32[2,2,2,2,144,512]{5,4,3,2,1,0:T(8,128)}, u32[]{:S(2)}, u32[]{:S(2)}) collective-permute-start(f32[2,2,2,2,144,512]{5,4,3,2,1,0:T(8,128)} %dynamic-slice_bitcast_fusion), channel_id=1, source_target_pairs={{0,2},{2,0},{4,6},{6,4},{1,3},{3,1},{5,7},{7,5},{8,10},{10,8},{12,... | collective-permute-start | bytes 14155784 | tf_op jit(solution)/shard_map/ppermute | solution.py:32
  84.4 192.2 %all-gather.5.cloned.1.call-start = ((), (), s32[]{:S(2)}) async-start(), calls=%async_computation | async-start | bytes 2654208 | tf_op jit(solution)/shard_map/all_gather | solution.py:110
  91.6 4.5 %copy-start.4 = (bf16[6,1,8,32,512]{4,3,2,1,0:T(8,128)(2,1)S(1)}, bf16[6,1,8,32,512]{4,3,2,1,0:T(8,128)(2,1)}, u32[]{:S(2)}) copy-start(bf16[6,1,8,32,512]{4,3,2,1,0:T(8,128)(2,1)} %param.8) | copy-start | bytes 4718596
  93.2 72.5 %collective-permute-start.5 = (f32[2,2,2,144,512]{4,3,1,0,2:T(8,128)}, f32[2,2,2,144,512]{4,3,1,0,2:T(8,128)}, u32[]{:S(2)}, u32[]{:S(2)}) collective-permute-start(f32[2,2,2,144,512]{4,3,1,0,2:T(8,128)} %bitcast.116), channel_id=1, source_target_pairs={{0,4},{2,6},{4,0},{6,2},{1,5},{3,7},{5,1},{7,3},{8,12},{10,14},{12... | collective-permute-start | bytes 7077896 | tf_op jit(solution)/shard_map/ppermute | solution.py:32
  96.1 4.4 %collective-permute-start.1 = (bf16[6,1,1,32,512]{4,3,2,1,0:T(8,128)(2,1)S(1)}, bf16[6,1,1,32,512]{4,3,2,1,0:T(8,128)(2,1)S(1)}, u32[]{:S(2)}, u32[]{:S(2)}) collective-permute-start(bf16[6,1,1,32,512]{4,3,2,1,0:T(8,128)(2,1)S(1)} %get-tuple-element.34), channel_id=1, source_target_pairs={{2,0},{4,2},{6,4},{3,1},{5,3},{7,5},{10,8},{12,10},{14,12},{11,9},... | collective-permute-start | bytes 589832 | tf_op jit(solution)/shard_map/ppermute | solution.py:17
  97.4 4.1 %collective-permute-start = (bf16[6,1,1,32,512]{4,3,2,1,0:T(8,128)(2,1)S(1)}, bf16[6,1,1,32,512]{4,3,2,1,0:T(8,128)(2,1)S(1)}, u32[]{:S(2)}, u32[]{:S(2)}) collective-permute-start(bf16[6,1,1,32,512]{4,3,2,1,0:T(8,128)(2,1)S(1)} %get-tuple-element.33), channel_id=1, source_target_pairs={{0,2},{2,4},{4,6},{1,3},{3,5},{5,7},{8,10},{10,12},{12,14},{9,11},... | collective-permute-start | bytes 589832 | tf_op jit(solution)/shard_map/ppermute | solution.py:16
  104.5 61.3 %copy-start.7 = (f32[2,2,1,2,144,512]{5,4,3,2,1,0:T(8,128)S(1)}, f32[2,2,1,2,144,512]{5,4,3,2,1,0:T(8,128)}, u32[]{:S(2)}) copy-start(f32[2,2,1,2,144,512]{5,4,3,2,1,0:T(8,128)} %get-tuple-element.21) | copy-start | bytes 7077892
  168.1 22.7 %collective-permute-start.6 = (f32[2,2,144,512]{3,2,1,0:T(8,128)S(1)}, f32[2,2,144,512]{3,2,1,0:T(8,128)S(1)}, u32[]{:S(2)}, u32[]{:S(2)}) collective-permute-start(f32[2,2,144,512]{3,2,1,0:T(8,128)S(1)} %dynamic-slice_bitcast_fusion.1), channel_id=1, source_target_pairs={{0,1},{1,0},{2,3},{3,2},{4,5},{5,4},{6,7},{7,6},{8,9},{9,8},{10,11... | collective-permute-start | bytes 3538952 | tf_op jit(solution)/shard_map/ppermute | solution.py:32
  192.0 32.4 %collective-permute-start.7 = (f32[2,144,512]{2,1,0:T(8,128)}, f32[2,144,512]{2,1,0:T(8,128)}, u32[]{:S(2)}, u32[]{:S(2)}) collective-permute-start(f32[2,144,512]{2,1,0:T(8,128)} %dynamic-slice_bitcast_fusion.2), channel_id=1, source_target_pairs={{0,8},{8,0},{16,24},{24,16},{1,9},{9,1},{17,25},{25,17},{2,10},{10... | collective-permute-start | bytes 1769480 | tf_op jit(solution)/shard_map/ppermute | solution.py:32
  196.7 26.7 %copy-start.3 = (bf16[7,1,10,32,512]{4,3,2,1,0:T(8,128)(2,1)S(1)}, bf16[7,1,10,32,512]{4,3,2,1,0:T(8,128)(2,1)}, u32[]{:S(2)}) copy-start(bf16[7,1,10,32,512]{4,3,2,1,0:T(8,128)(2,1)} %copy-done.2) | copy-start | bytes 6881284
  225.5 1.0 copy-start.10
  226.5 15.0 %collective-permute-start.8 = (f32[144,512]{1,0:T(8,128)}, f32[144,512]{1,0:T(8,128)S(1)}, u32[]{:S(2)}, u32[]{:S(2)}) collective-permute-start(f32[144,512]{1,0:T(8,128)} %dynamic-slice_bitcast_fusion.3), channel_id=1, source_target_pairs={{0,16},{8,24},{16,0},{24,8},{1,17},{9,25},{17,1},{25,9},{2,18},{10... | collective-permute-start | bytes 884744 | tf_op jit(solution)/shard_map/ppermute | solution.py:32
  230.8 10.7 %copy-start.11 = (f32[2,144,512]{2,1,0:T(8,128)S(1)}, f32[2,144,512]{2,1,0:T(8,128)}, u32[]{:S(2)}) copy-start(f32[2,144,512]{2,1,0:T(8,128)} %copy-done.10) | copy-start | bytes 1769476
  268.1 1.1 copy-start.9
  268.1 1.3 copy-start.12
  268.1 1.5 copy-start.13
  268.1 1.7 copy-start.14
  268.1 1.9 copy-start.15
  270.0 1.7 copy-start.5
  276.6 8.0 %copy-start.1 = (f32[1152,512]{1,0:T(8,128)S(1)}, f32[1152,512]{1,0:T(8,128)}, u32[]{:S(2)}) copy-start(f32[1152,512]{1,0:T(8,128)} %param.9) | copy-start | bytes 7077892
Sparse Core Ops, SparseCore 0:
  84.6 59.8 all-gather.6
  242.4 29.5 all-gather.4

commit v3 on v1

--- a/solution.py
+++ b/solution.py
@@ -32,13 +32,7 @@
     rest = ("space", "rep")
     rest_count = lax.axis_size("space") * lax.axis_size("rep")
     data_count = lax.axis_size("dp")
-    shard_rows = master.shape[0]
-    piece_rows = shard_rows // rest_count
-    local = master.astype(jnp.bfloat16)
-    piece = lax.dynamic_slice_in_dim(local, lax.axis_index(rest) * piece_rows, piece_rows, 0)
-    over_dp = lax.all_gather(piece, "dp", axis=0, tiled=False)
-    over_all = lax.all_gather(over_dp, rest, axis=0, tiled=False)
-    weights = jnp.swapaxes(over_all, 0, 1).reshape(data_count * shard_rows, master.shape[1])
+    piece_rows = master.shape[0] // rest_count
     stacked = jnp.concatenate([membrane[None], frames], axis=0)
     rimmed = extended(stacked, (("space", 2),), 1)
     voltage = rimmed[0].astype(jnp.float32)
@@ -68,6 +62,9 @@
     weight_local = lax.dot_general(
         spike_cols, grad_flat, (((0,), (0,)), ((), ())), preferred_element_type=jnp.float32
     )
+    weight_local, local = lax.optimization_barrier((weight_local, master))
+    piece = lax.dynamic_slice_in_dim(local, lax.axis_index(rest) * piece_rows, piece_rows, 0)
+    weights = lax.all_gather(piece.astype(jnp.bfloat16), ("dp",) + rest, axis=0, tiled=True)
     dspikes = jnp.einsum(
         "nkd,kcd->nc",
         grad_cols,

time: 240 us -> 291 us (1.21)
  waiting for transfers between devices: 78.9 us -> 151 us
  blocking collectives: 19.5 us -> 0 us
  local copies, waits for them, and re-layouts: 51.4 us -> 47 us
    all_gather x1, waiting for transfers between devices: 0.01 us -> 66.6 us  [on_device(): lax.all_gather(piece.astype(jnp.bfloat16), ('dp',) + rest, axis=0, tiled=...]
    all_gather x1 -> x0, blocking collectives: 19.5 us -> none  [on_device(): over_dp = lax.all_gather(piece, 'dp', axis=0, tiled=False)]
    ppermute x2, waiting for transfers between devices: 0.01 us -> 6.01 us  [extended(): after = lax.ppermute(first, axis, down)]
    transpose x1 -> x0, local copies, waits for them, and re-layouts: 4.98 us -> none  [on_device(): jnp.swapaxes(over_all, 0, 1)]
    unnamed x36 -> x38, local copies, waits for them, and re-layouts: 15.9 us -> 15.9 us
  transfers between devices with their start and end apart: 7 -> 7, of which waited for: 2 -> 4; matrix products, arithmetic and copies ran while one was open for 43% -> 29% of each run, Pallas kernels for 0% -> 0%
where the time goes in v3:
time: 291 us; the launch traced here: 290 us
  waiting for transfers between devices  151 us (52%)
  local copies, waits for them, and re-layouts  47 us (16%)
  matrix products  36 us (12%)
  other arithmetic  30.1 us (10%)
  between operations  14.1 us (5%)
  starting transfers between devices  11.8 us (4%)
    reduce_scatter x1, waiting for transfers between devices, on_device(): lax.psum_scatter(weight_local, ('dp',) + rest, scatter_dimension=0, tiled...  78.1 us
    all_gather x1, waiting for transfers between devices, on_device(): lax.all_gather(piece.astype(jnp.bfloat16), ('dp',) + rest, axis=0, tiled=...  66.6 us
    reshape x1, local copies, waits for them, and re-layouts, on_device(): grad_cols = jnp.concatenate([grad_pad[:, :, 1 - a:1 - a + rows, 1 - b:1 -...  26.8 us
    dot_general x1, matrix products, on_device(): jnp.einsum('nkd,kcd->nc', grad_cols, weights.reshape(9, chans, chans), pr...  25.8 us
    unnamed x38, local copies, waits for them, and re-layouts  15.9 us
    dot_general x1, matrix products, on_device(): lax.dot_general(spike_cols, grad_flat, (((0,), (0,)), ((), ())), preferre...  10.2 us
    ppermute x2, starting transfers between devices, extended(): before = lax.ppermute(last, axis, up)  8.87 us
    unnamed x12, other arithmetic  8.42 us
  transfers between devices with their start and end apart: 7, of which 4 were waited for; matrix products, arithmetic and copies ran while one was open for 29% of the time, Pallas kernels for 0%

profile of v3, /device:TPU:0, one launch (start us, length us, event | category | flops | bytes accessed | tf_op | source)
XLA Modules:
  0.0 289.7 jit_solution(4104841324934013969)
XLA Ops:
  7.2 0.0 reduce-scatter.2.cloned.1.call-start
  7.2 1.2 pad_maximum_fusion.4
  8.5 2.5 collective-permute-start.2
  11.0 1.3 collective-permute-start.3
  12.3 4.2 %collective-permute-done.3 = bf16[7,1,1,32,512]{4,3,2,1,0:T(8,128)(2,1)S(1)} collective-permute-done((bf16[7,1,1,32,512]{4,3,2,1,0:T(8,128)(2,1)S(1)}, bf16[7,1,1,32,512]{4,3,2,1,0:T(8,128)(2,1)S(1)}, u32[]{:S(2)}, u32[]{:S(2)}) %collective-permute-start.3) | collective-permute-done | bytes 229408 | tf_op jit(solution)/shard_map/ppermute | solution.py:17
  16.5 0.4 pad_maximum_fusion
  16.8 0.1 fusion.76
  17.0 0.3 fusion.78
  17.3 0.4 fusion.80
  17.7 0.5 fusion.82
  18.2 0.2 fusion.83
  18.4 0.3 fusion.74
  18.7 0.5 fusion.16
  19.2 0.1 slice_dynamic-update-slice_fusion.2
  19.3 0.7 fusion.17
  20.1 0.7 fusion.18
  20.8 0.1 slice_dynamic-update-slice_fusion.1
  20.9 0.7 fusion.19
  21.7 0.7 fusion.20
  22.4 0.1 slice_dynamic-update-slice_fusion
  22.5 0.7 fusion.21
  23.3 0.7 copy-done.2
  23.9 10.2 %fusion.4 = f32[4608,512]{1,0:T(8,128)} fusion(bf16[6,1,8,32,4608]{4,3,2,0,1:T(8,128)(2,1)S(1)} %fusion.21, bf16[6,1,8,32,512]{4,3,2,1,0:T(8,128)(2,1)S(1)} %copy-done.2), kind=kOutput, calls=%fused_computation.4 | convolution fusion | flops 7247757312 | bytes 25165824 | tf_op jit(solution)/shard_map/dot_general | solution.py:62
  34.1 0.0 reduce-scatter.2.cloned.1.call-update
  34.1 0.0 all-gather.3.cloned.1.call-start
  34.2 0.7 dynamic-slice_convert_fusion
  34.9 0.0 all-gather.3.cloned.1.call-update
  34.9 0.0 all-gather.5.cloned.1.call-start
  35.0 1.1 fusion.104
  36.0 6.4 %collective-permute-start = (bf16[6,1,1,32,512]{4,3,2,1,0:T(8,128)(2,1)S(1)}, bf16[6,1,1,32,512]{4,3,2,1,0:T(8,128)(2,1)S(1)}, u32[]{:S(2)}, u32[]{:S(2)}) collective-permute-start(bf16[6,1,1,32,512]{4,3,2,1,0:T(8,128)(2,1)S(1)} %get-tuple-element.33), channel_id=1, source_target_pairs={{0,2},{2,4},{4,6},{1,3},{3,5},{5,7},{8,10},{10,12},{12,14},{9,11},... | collective-permute-start | bytes 589832 | tf_op jit(solution)/shard_map/ppermute | solution.py:16
  42.4 1.5 collective-permute-start.1
  43.9 1.8 collective-permute-done.1
  45.7 2.4 fusion.15
  48.1 1.7 slice_dynamic-update-slice_fusion.8
  49.8 1.4 fusion.23
  51.2 1.4 slice_dynamic-update-slice_fusion.7
  52.6 2.0 slice_dynamic-update-slice_fusion.6
  54.6 1.4 constant_dynamic-update-slice_fusion
  55.9 1.4 slice_dynamic-update-slice_fusion.5
  57.3 2.0 slice_dynamic-update-slice_fusion.4
  59.4 1.4 fusion.22
  60.7 1.5 slice_dynamic-update-slice_fusion.3
  62.2 26.8 %reshape.515 = bf16[1536,9,512]{2,1,0:T(8,128)(2,1)} reshape(bf16[6,1,8,32,4608]{4,3,2,1,0:T(8,128)(2,1)} %slice_dynamic-update-slice_fusion.3) | data formatting | bytes 28311552 | tf_op jit(solution)/shard_map/reshape | solution.py:60
  89.1 1.9 convert_bitcast_fusion
  91.0 2.0 fusion.73
  93.0 3.1 %fusion.28 = (f32[1,10,32,512]{3,2,1,0:T(8,128)S(1)}, f32[1,10,32,512]{3,2,1,0:T(8,128)}, f32[1,10,32,512]{3,2,1,0:T(8,128)}, f32[1,10,32,512]{3,2,1,0:T(8,128)}) fusion(bf16[7,1,10,32,512]{4,3,2,1,0:T(8,128)(2,1)} %copy-done.1), kind=kLoop, calls=%fused_computation.68 | loop fusion | flops 4587520 | bytes 4587520 | tf_op jit(solution)/shard_map/add | solution.py:42
  96.1 78.1 %reduce-scatter.2.cloned.1.call-done = f32[144,512]{1,0:T(8,128)} async-done(((f32[4608,512]{1,0:T(8,128)}), f32[144,512]{1,0:T(8,128)}) %reduce-scatter.2.cloned.1.call-update) | async-done | bytes 294928 | tf_op jit(solution)/shard_map/reduce_scatter | solution.py:83
  174.2 0.0 all-gather.5.cloned.1.call-update
  174.2 66.6 %all-gather.3.cloned.1.call-done = bf16[4608,512]{1,0:T(8,128)(2,1)} async-done(((bf16[144,512]{1,0:T(8,128)(2,1)}), bf16[4608,512]{1,0:T(8,128)(2,1)}) %all-gather.3.cloned.1.call-update) | async-done | bytes 4718608 | tf_op jit(solution)/shard_map/all_gather | solution.py:67
  240.9 25.8 %fusion.8 = f32[1536,512]{1,0:T(8,128)S(1)} fusion(bf16[9,512,512]{2,1,0:T(8,128)(2,1)} %bitcast.158, bf16[1536,9,512]{2,1,0:T(8,128)(2,1)} %reshape.515), kind=kOutput, calls=%fused_computation.8 | convolution fusion | flops 7247757312 | bytes 22020096 | tf_op jit(solution)/shard_map/nkd,kcd->nc/dot_general | solution.py:68
  266.8 0.3 fusion.103
  267.1 0.7 copy-done.6
  267.8 0.2 copy-done.7
  268.0 0.2 copy-done.8
  268.2 0.2 copy-done.9
  268.4 0.2 copy-done.10
  268.6 1.7 broadcast_multiply_fusion.1
  270.3 0.8 fusion.85
  271.1 0.9 fusion.87
  272.0 0.8 fusion.89
  272.8 0.8 fusion.91
  273.6 0.9 fusion.93
  274.5 0.8 fusion.95
  275.3 7.9 %add_divide_fusion = (f32[1152,512]{1,0:T(8,128)}, f32[1152,512]{1,0:T(8,128)}, f32[1152,512]{1,0:T(8,128)}, f32[1152,512]{1,0:T(8,128)}) fusion(f32[1152,512]{1,0:T(8,128)} %all-gather.5.cloned.1.call-done, f32[1152,512]{1,0:T(8,128)} %param.11, f32[1152,512]{1,0:T(8,128)} %param.10), kind=kLoop, calls=%fused_computation.14 | loop fusion | flops 5898240 | bytes 16515072 | tf_op jit(solution)/shard_map/div | solution.py:88
  (21 shorter events, 0.1 us)
Async XLA Ops:
  7.2 27.0 %copy-start = (f32[1152,512]{1,0:T(8,128)S(1)}, f32[1152,512]{1,0:T(8,128)}, u32[]{:S(2)}) copy-start(f32[1152,512]{1,0:T(8,128)} %param.9) | copy-start | bytes 7077892
  7.2 9.3 %copy-start.11 = (bf16[1,8,32,512]{3,2,1,0:T(8,128)(2,1)S(1)}, bf16[1,8,32,512]{3,2,1,0:T(8,128)(2,1)}, u32[]{:S(2)}) copy-start(bf16[1,8,32,512]{3,2,1,0:T(8,128)(2,1)} %param.7) | copy-start | bytes 786436
  7.2 167.0 %reduce-scatter.2.cloned.1.call-start = ((), (), s32[]{:S(2)}) async-start(), calls=%async_computation.2 | async-start | bytes 9732096 | tf_op jit(solution)/shard_map/reduce_scatter | solution.py:83
  7.2 9.2 %copy-start.5 = (bf16[6,1,8,32,512]{4,3,2,1,0:T(8,128)(2,1)S(1)}, bf16[6,1,8,32,512]{4,3,2,1,0:T(8,128)(2,1)}, u32[]{:S(2)}) copy-start(bf16[6,1,8,32,512]{4,3,2,1,0:T(8,128)(2,1)} %param.6) | copy-start | bytes 4718596
  8.5 3.8 %collective-permute-start.2 = (bf16[7,1,1,32,512]{4,3,2,1,0:T(8,128)(2,1)S(1)}, bf16[7,1,1,32,512]{4,3,2,1,0:T(8,128)(2,1)S(1)}, u32[]{:S(2)}, u32[]{:S(2)}) collective-permute-start(bf16[7,1,1,32,512]{4,3,2,1,0:T(8,128)(2,1)S(1)} %get-tuple-element.31), channel_id=1, source_target_pairs={{0,2},{2,4},{4,6},{1,3},{3,5},{5,7},{8,10},{10,12},{12,14},{9,11},... | collective-permute-start | bytes 688136 | tf_op jit(solution)/shard_map/ppermute | solution.py:16
  11.0 5.5 %collective-permute-start.3 = (bf16[7,1,1,32,512]{4,3,2,1,0:T(8,128)(2,1)S(1)}, bf16[7,1,1,32,512]{4,3,2,1,0:T(8,128)(2,1)S(1)}, u32[]{:S(2)}, u32[]{:S(2)}) collective-permute-start(bf16[7,1,1,32,512]{4,3,2,1,0:T(8,128)(2,1)S(1)} %get-tuple-element.32), channel_id=1, source_target_pairs={{2,0},{4,2},{6,4},{3,1},{5,3},{7,5},{10,8},{12,10},{14,12},{11,9},... | collective-permute-start | bytes 688136 | tf_op jit(solution)/shard_map/ppermute | solution.py:17
  16.8 1.6 copy-start.1
  22.5 1.4 copy-start.2
  34.1 206.7 %all-gather.3.cloned.1.call-start = ((), (), s32[]{:S(2)}) async-start(), calls=%async_computation.1 | async-start | bytes 4866048 | tf_op jit(solution)/shard_map/all_gather | solution.py:67
  34.9 240.3 %all-gather.5.cloned.1.call-start = ((), (), s32[]{:S(2)}) async-start(), calls=%async_computation.3 | async-start | bytes 2654208 | tf_op jit(solution)/shard_map/all_gather | solution.py:84
  36.0 7.9 %collective-permute-start = (bf16[6,1,1,32,512]{4,3,2,1,0:T(8,128)(2,1)S(1)}, bf16[6,1,1,32,512]{4,3,2,1,0:T(8,128)(2,1)S(1)}, u32[]{:S(2)}, u32[]{:S(2)}) collective-permute-start(bf16[6,1,1,32,512]{4,3,2,1,0:T(8,128)(2,1)S(1)} %get-tuple-element.33), channel_id=1, source_target_pairs={{0,2},{2,4},{4,6},{1,3},{3,5},{5,7},{8,10},{10,12},{12,14},{9,11},... | collective-permute-start | bytes 589832 | tf_op jit(solution)/shard_map/ppermute | solution.py:16
  42.4 3.3 %collective-permute-start.1 = (bf16[6,1,1,32,512]{4,3,2,1,0:T(8,128)(2,1)S(1)}, bf16[6,1,1,32,512]{4,3,2,1,0:T(8,128)(2,1)S(1)}, u32[]{:S(2)}, u32[]{:S(2)}) collective-permute-start(bf16[6,1,1,32,512]{4,3,2,1,0:T(8,128)(2,1)S(1)} %get-tuple-element.34), channel_id=1, source_target_pairs={{2,0},{4,2},{6,4},{3,1},{5,3},{7,5},{10,8},{12,10},{14,12},{11,9},... | collective-permute-start | bytes 589832 | tf_op jit(solution)/shard_map/ppermute | solution.py:17
  48.1 1.7 copy-start.3
  266.7 1.1 copy-start.6
  266.7 1.3 copy-start.7
  266.7 1.5 copy-start.8
  266.7 1.7 copy-start.9
  266.7 1.9 copy-start.10
  268.6 1.7 copy-start.4
Sparse Core Ops, SparseCore 0:
  34.3 139.9 reduce-scatter.1
  178.1 62.7 all-gather.2
  242.9 27.8 all-gather.4

commit v4 on v1

--- a/solution.py
+++ b/solution.py
@@ -19,6 +19,19 @@
     return x
 
 
+def doubling_gather(blocks, axis):
+    peers = lax.axis_size(axis)
+    me = lax.axis_index(axis)
+    bit = 0
+    while (1 << bit) < peers:
+        pairs = [(j, j ^ (1 << bit)) for j in range(peers)]
+        other = lax.ppermute(blocks, axis, pairs)
+        low = (me // (1 << bit)) % 2 == 0
+        blocks = jnp.where(low, jnp.concatenate([blocks, other]), jnp.concatenate([other, blocks]))
+        bit += 1
+    return blocks
+
+
 def surrogate(potential):
     return 1.0 / (1.0 + (math.pi * (potential - 1.0)) ** 2)
 
@@ -36,7 +49,7 @@
     piece_rows = shard_rows // rest_count
     local = master.astype(jnp.bfloat16)
     piece = lax.dynamic_slice_in_dim(local, lax.axis_index(rest) * piece_rows, piece_rows, 0)
-    over_dp = lax.all_gather(piece, "dp", axis=0, tiled=False)
+    over_dp = doubling_gather(piece[None], "dp")
     over_all = lax.all_gather(over_dp, rest, axis=0, tiled=False)
     weights = jnp.swapaxes(over_all, 0, 1).reshape(data_count * shard_rows, master.shape[1])
     stacked = jnp.concatenate([membrane[None], frames], axis=0)

time: 240 us -> 226 us (0.942)
  blocking collectives: 19.5 us -> 0 us
  starting transfers between devices: 8.97 us -> 15.8 us
  local copies, waits for them, and re-layouts: 51.4 us -> 46.7 us
  other arithmetic: 28.1 us -> 31.1 us
    all_gather x1 -> x0, blocking collectives: 19.5 us -> none  [on_device(): over_dp = lax.all_gather(piece, 'dp', axis=0, tiled=False)]
    reduce_scatter x1, waiting for transfers between devices: 77.7 us -> 61.6 us  [on_device(): lax.psum_scatter(weight_local, ('dp',) + rest, scatter_dimension=0, tiled...]
    ppermute x0 -> x2, waiting for transfers between devices: none -> 16.1 us  [doubling_gather(): other = lax.ppermute(blocks, axis, pairs)]
    ppermute x0 -> x2, starting transfers between devices: none -> 6.21 us  [doubling_gather(): other = lax.ppermute(blocks, axis, pairs)]
    transpose x1 -> x0, local copies, waits for them, and re-layouts: 4.98 us -> none  [on_device(): jnp.swapaxes(over_all, 0, 1)]
    add x2, other arithmetic: 2.56 us -> 5.14 us  [on_device(): potential = 0.5 * voltage + rimmed[position + 1].astype(jnp.float32)]
    unnamed x36 -> x38, local copies, waits for them, and re-layouts: 15.9 us -> 16.3 us
  transfers between devices with their start and end apart: 7 -> 9, of which waited for: 2 -> 5; matrix products, arithmetic and copies ran while one was open for 43% -> 38% of each run, Pallas kernels for 0% -> 0%
where the time goes in v4:
time: 226 us; the launch traced here: 225 us
  waiting for transfers between devices  79.6 us (35%)
  local copies, waits for them, and re-layouts  46.7 us (21%)
  matrix products  36 us (16%)
  other arithmetic  31.1 us (14%)
  starting transfers between devices  15.8 us (7%)
  between operations  15.8 us (7%)
    reduce_scatter x1, waiting for transfers between devices, on_device(): lax.psum_scatter(weight_local, ('dp',) + rest, scatter_dimension=0, tiled...  61.6 us
    reshape x1, local copies, waits for them, and re-layouts, on_device(): grad_cols = jnp.concatenate([grad_pad[:, :, 1 - a:1 - a + rows, 1 - b:1 -...  26.8 us
    dot_general x1, matrix products, on_device(): jnp.einsum('nkd,kcd->nc', grad_cols, weights.reshape(9, chans, chans), pr...  25.8 us
    unnamed x38, local copies, waits for them, and re-layouts  16.3 us
    ppermute x2, waiting for transfers between devices, doubling_gather(): other = lax.ppermute(blocks, axis, pairs)  16.1 us
    dot_general x1, matrix products, on_device(): lax.dot_general(spike_cols, grad_flat, (((0,), (0,)), ((), ())), preferre...  10.2 us
    unnamed x12, other arithmetic  8.43 us
    div x1, other arithmetic, on_device(): update = new_moment / (jnp.sqrt(new_second) + 1e-08)  7.88 us
  transfers between devices with their start and end apart: 9, of which 5 were waited for; matrix products, arithmetic and copies ran while one was open for 38% of the time, Pallas kernels for 0%

profile of v4, /device:TPU:0, one launch (start us, length us, event | category | flops | bytes accessed | tf_op | source)
XLA Modules:
  0.0 225.0 jit_solution(16927803293861535660)
XLA Ops:
  8.1 1.2 pad_maximum_fusion.4
  9.3 1.4 collective-permute-start.5
  10.7 3.0 %collective-permute-start.4 = (bf16[7,1,1,32,512]{4,3,2,1,0:T(8,128)(2,1)S(1)}, bf16[7,1,1,32,512]{4,3,2,1,0:T(8,128)(2,1)S(1)}, u32[]{:S(2)}, u32[]{:S(2)}) collective-permute-start(bf16[7,1,1,32,512]{4,3,2,1,0:T(8,128)(2,1)S(1)} %get-tuple-element.27), channel_id=1, source_target_pairs={{0,2},{2,4},{4,6},{1,3},{3,5},{5,7},{8,10},{10,12},{12,14},{9,11},... | collective-permute-start | bytes 688136 | tf_op jit(solution)/shard_map/ppermute | solution.py:16
  13.8 1.1 collective-permute-done.4
  14.9 0.4 pad_maximum_fusion
  15.2 0.1 fusion.76
  15.4 0.3 fusion.78
  15.7 0.4 fusion.80
  16.1 0.5 fusion.82
  16.6 0.2 fusion.83
  16.8 0.3 fusion.74
  17.2 0.5 fusion.16
  17.6 0.1 slice_dynamic-update-slice_fusion.2
  17.8 0.7 fusion.17
  18.5 0.7 fusion.18
  19.2 0.1 slice_dynamic-update-slice_fusion.1
  19.3 0.7 fusion.19
  20.1 0.7 fusion.20
  20.8 0.1 slice_dynamic-update-slice_fusion
  20.9 0.7 fusion.21
  21.7 0.7 copy-done.2
  22.3 10.2 %fusion.4 = f32[4608,512]{1,0:T(8,128)} fusion(bf16[6,1,8,32,4608]{4,3,2,0,1:T(8,128)(2,1)S(1)} %fusion.21, bf16[6,1,8,32,512]{4,3,2,1,0:T(8,128)(2,1)S(1)} %copy-done.2), kind=kOutput, calls=%fused_computation.4 | convolution fusion | flops 7247757312 | bytes 25165824 | tf_op jit(solution)/shard_map/dot_general | solution.py:81
  32.5 0.0 all-gather.3.cloned.1.call-start
  32.6 3.1 %collective-permute-start.2 = (bf16[1,144,512]{2,1,0:T(8,128)(2,1)S(1)}, bf16[1,144,512]{2,1,0:T(8,128)(2,1)S(1)}, u32[]{:S(2)}, u32[]{:S(2)}) collective-permute-start(bf16[1,144,512]{2,1,0:T(8,128)(2,1)S(1)} %fusion.96), channel_id=1, source_target_pairs={{0,8},{8,0},{16,24},{24,16},{1,9},{9,1},{17,25},{25,17},{2,10},{10... | collective-permute-start | bytes 442376 | tf_op jit(solution)/shard_map/ppermute | solution.py:28
  35.8 3.1 %collective-permute-done.2 = bf16[1,144,512]{2,1,0:T(8,128)(2,1)S(1)} collective-permute-done((bf16[1,144,512]{2,1,0:T(8,128)(2,1)S(1)}, bf16[1,144,512]{2,1,0:T(8,128)(2,1)S(1)}, u32[]{:S(2)}, u32[]{:S(2)}) %collective-permute-start.2) | collective-permute-done | bytes 147488 | tf_op jit(solution)/shard_map/ppermute | solution.py:28
  38.9 3.1 %collective-permute-start.3 = (bf16[2,144,512]{2,1,0:T(8,128)(2,1)S(1)}, bf16[2,144,512]{2,1,0:T(8,128)(2,1)S(1)}, u32[]{:S(2)}, u32[]{:S(2)}) collective-permute-start(bf16[2,144,512]{2,1,0:T(8,128)(2,1)S(1)} %maximum_select_fusion.1), channel_id=1, source_target_pairs={{0,16},{8,24},{16,0},{24,8},{1,17},{9,25},{17,1},{25,9},{2,18},{10... | collective-permute-start | bytes 884744 | tf_op jit(solution)/shard_map/ppermute | solution.py:28
  42.0 13.0 %collective-permute-done.3 = bf16[2,144,512]{2,1,0:T(8,128)(2,1)S(1)} collective-permute-done((bf16[2,144,512]{2,1,0:T(8,128)(2,1)S(1)}, bf16[2,144,512]{2,1,0:T(8,128)(2,1)S(1)}, u32[]{:S(2)}, u32[]{:S(2)}) %collective-permute-start.3) | collective-permute-done | bytes 294944 | tf_op jit(solution)/shard_map/ppermute | solution.py:28
  55.0 0.9 maximum_select_fusion
  55.9 0.0 all-gather.5.cloned.1.call-start
  56.0 1.1 fusion.105
  57.1 1.3 collective-permute-start.1
  58.4 3.7 %collective-permute-start = (bf16[6,1,1,32,512]{4,3,2,1,0:T(8,128)(2,1)S(1)}, bf16[6,1,1,32,512]{4,3,2,1,0:T(8,128)(2,1)S(1)}, u32[]{:S(2)}, u32[]{:S(2)}) collective-permute-start(bf16[6,1,1,32,512]{4,3,2,1,0:T(8,128)(2,1)S(1)} %get-tuple-element.29), channel_id=1, source_target_pairs={{0,2},{2,4},{4,6},{1,3},{3,5},{5,7},{8,10},{10,12},{12,14},{9,11},... | collective-permute-start | bytes 589832 | tf_op jit(solution)/shard_map/ppermute | solution.py:16
  62.1 0.8 collective-permute-done
  63.0 2.4 %fusion.15 = bf16[6,1,10,34,512]{4,3,2,1,0:T(8,128)(2,1)S(1)} fusion(bf16[6,1,1,32,512]{4,3,2,1,0:T(8,128)(2,1)S(1)} %collective-permute-done.1, bf16[6,1,8,32,512]{4,3,2,1,0:T(8,128)(2,1)} %param.8, bf16[6,1,1,32,512]{4,3,2,1,0:T(8,128)(2,1)S(1)} %collective-permute-done), kind=kLoop, calls=%fused_computation.13 | loop fusion | flops 12533760 | bytes 4055040 | tf_op jit(solution)/shard_map/concatenate | solution.py:18
  65.4 1.7 slice_dynamic-update-slice_fusion.8
  67.0 0.3 copy-done.3
  67.4 1.4 fusion.23
  68.7 1.5 slice_dynamic-update-slice_fusion.7
  70.2 2.0 slice_dynamic-update-slice_fusion.6
  72.2 1.5 constant_dynamic-update-slice_fusion
  73.6 1.4 slice_dynamic-update-slice_fusion.5
  75.0 2.0 slice_dynamic-update-slice_fusion.4
  77.0 1.4 fusion.22
  78.4 1.4 slice_dynamic-update-slice_fusion.3
  79.8 26.8 %reshape.621 = bf16[1536,9,512]{2,1,0:T(8,128)(2,1)} reshape(bf16[6,1,8,32,4608]{4,3,2,1,0:T(8,128)(2,1)} %slice_dynamic-update-slice_fusion.3) | data formatting | bytes 28311552 | tf_op jit(solution)/shard_map/reshape | solution.py:79
  106.7 2.0 fusion.73
  108.7 1.9 convert_bitcast_fusion.1
  110.6 3.1 %fusion.28 = (f32[1,10,32,512]{3,2,1,0:T(8,128)S(1)}, f32[1,10,32,512]{3,2,1,0:T(8,128)}, f32[1,10,32,512]{3,2,1,0:T(8,128)}, f32[1,10,32,512]{3,2,1,0:T(8,128)}) fusion(bf16[7,1,10,32,512]{4,3,2,1,0:T(8,128)(2,1)} %copy-done.1), kind=kLoop, calls=%fused_computation.68 | loop fusion | flops 4587520 | bytes 4587520 | tf_op jit(solution)/shard_map/add | solution.py:61
  113.7 61.6 %reduce-scatter.2.cloned.1.call-done = f32[144,512]{1,0:T(8,128)} async-done(((f32[4608,512]{1,0:T(8,128)}), f32[144,512]{1,0:T(8,128)}) %reduce-scatter.2.cloned.1.call-update) | async-done | bytes 294928 | tf_op jit(solution)/shard_map/reduce_scatter | solution.py:99
  175.3 25.8 %fusion.8 = f32[1536,512]{1,0:T(8,128)S(1)} fusion(bf16[9,512,512]{2,1,0:T(8,128)(2,1)} %bitcast.166, bf16[1536,9,512]{2,1,0:T(8,128)(2,1)} %reshape.621), kind=kOutput, calls=%fused_computation.8 | convolution fusion | flops 7247757312 | bytes 22020096 | tf_op jit(solution)/shard_map/nkd,kcd->nc/dot_general | solution.py:84
  201.2 0.3 fusion.104
  201.5 0.7 copy-done.6
  202.2 0.2 copy-done.7
  202.4 0.2 copy-done.8
  202.6 0.2 copy-done.9
  202.8 0.2 copy-done.10
  203.1 1.7 broadcast_multiply_fusion.1
  204.8 0.8 fusion.85
  205.6 0.9 fusion.87
  206.5 0.8 fusion.89
  207.3 0.8 fusion.91
  208.0 0.9 fusion.93
  209.0 0.8 fusion.95
  209.7 7.9 %add_divide_fusion = (f32[1152,512]{1,0:T(8,128)}, f32[1152,512]{1,0:T(8,128)}, f32[1152,512]{1,0:T(8,128)}, f32[1152,512]{1,0:T(8,128)}) fusion(f32[1152,512]{1,0:T(8,128)} %all-gather.5.cloned.1.call-done, f32[1152,512]{1,0:T(8,128)} %param.11, f32[1152,512]{1,0:T(8,128)} %param.10), kind=kLoop, calls=%fused_computation.14 | loop fusion | flops 5898240 | bytes 16515072 | tf_op jit(solution)/shard_map/div | solution.py:104
  (28 shorter events, 0.3 us)
Async XLA Ops:
  8.0 24.6 %copy-start = (f32[1152,512]{1,0:T(8,128)S(1)}, f32[1152,512]{1,0:T(8,128)}, u32[]{:S(2)}) copy-start(f32[1152,512]{1,0:T(8,128)} %param.9) | copy-start | bytes 7077892
  8.0 6.9 %copy-start.11 = (bf16[1,8,32,512]{3,2,1,0:T(8,128)(2,1)S(1)}, bf16[1,8,32,512]{3,2,1,0:T(8,128)(2,1)}, u32[]{:S(2)}) copy-start(bf16[1,8,32,512]{3,2,1,0:T(8,128)(2,1)} %param.7) | copy-start | bytes 786436
  8.0 167.2 %reduce-scatter.2.cloned.1.call-start = ((), (), s32[]{:S(2)}) async-start(), calls=%async_computation.2 | async-start | bytes 9732096 | tf_op jit(solution)/shard_map/reduce_scatter | solution.py:99
  8.1 6.8 %copy-start.5 = (bf16[6,1,8,32,512]{4,3,2,1,0:T(8,128)(2,1)S(1)}, bf16[6,1,8,32,512]{4,3,2,1,0:T(8,128)(2,1)}, u32[]{:S(2)}) copy-start(bf16[6,1,8,32,512]{4,3,2,1,0:T(8,128)(2,1)} %param.6) | copy-start | bytes 4718596
  9.3 4.5 %collective-permute-start.5 = (bf16[7,1,1,32,512]{4,3,2,1,0:T(8,128)(2,1)S(1)}, bf16[7,1,1,32,512]{4,3,2,1,0:T(8,128)(2,1)S(1)}, u32[]{:S(2)}, u32[]{:S(2)}) collective-permute-start(bf16[7,1,1,32,512]{4,3,2,1,0:T(8,128)(2,1)S(1)} %get-tuple-element.28), channel_id=1, source_target_pairs={{2,0},{4,2},{6,4},{3,1},{5,3},{7,5},{10,8},{12,10},{14,12},{11,9},... | collective-permute-start | bytes 688136 | tf_op jit(solution)/shard_map/ppermute | solution.py:17
  10.7 4.1 %collective-permute-start.4 = (bf16[7,1,1,32,512]{4,3,2,1,0:T(8,128)(2,1)S(1)}, bf16[7,1,1,32,512]{4,3,2,1,0:T(8,128)(2,1)S(1)}, u32[]{:S(2)}, u32[]{:S(2)}) collective-permute-start(bf16[7,1,1,32,512]{4,3,2,1,0:T(8,128)(2,1)S(1)} %get-tuple-element.27), channel_id=1, source_target_pairs={{0,2},{2,4},{4,6},{1,3},{3,5},{5,7},{8,10},{10,12},{12,14},{9,11},... | collective-permute-start | bytes 688136 | tf_op jit(solution)/shard_map/ppermute | solution.py:16
  15.2 1.6 copy-start.1
  20.9 1.4 copy-start.2
  32.5 142.8 %all-gather.3.cloned.1.call-start = ((), (), s32[]{:S(2)}) async-start(), calls=%async_computation.1 | async-start | bytes 5308416 | tf_op jit(solution)/shard_map/all_gather | solution.py:53
  32.6 6.2 %collective-permute-start.2 = (bf16[1,144,512]{2,1,0:T(8,128)(2,1)S(1)}, bf16[1,144,512]{2,1,0:T(8,128)(2,1)S(1)}, u32[]{:S(2)}, u32[]{:S(2)}) collective-permute-start(bf16[1,144,512]{2,1,0:T(8,128)(2,1)S(1)} %fusion.96), channel_id=1, source_target_pairs={{0,8},{8,0},{16,24},{24,16},{1,9},{9,1},{17,25},{25,17},{2,10},{10... | collective-permute-start | bytes 442376 | tf_op jit(solution)/shard_map/ppermute | solution.py:28
  38.9 16.1 %collective-permute-start.3 = (bf16[2,144,512]{2,1,0:T(8,128)(2,1)S(1)}, bf16[2,144,512]{2,1,0:T(8,128)(2,1)S(1)}, u32[]{:S(2)}, u32[]{:S(2)}) collective-permute-start(bf16[2,144,512]{2,1,0:T(8,128)(2,1)S(1)} %maximum_select_fusion.1), channel_id=1, source_target_pairs={{0,16},{8,24},{16,0},{24,8},{1,17},{9,25},{17,1},{25,9},{2,18},{10... | collective-permute-start | bytes 884744 | tf_op jit(solution)/shard_map/ppermute | solution.py:28
  55.9 153.8 %all-gather.5.cloned.1.call-start = ((), (), s32[]{:S(2)}) async-start(), calls=%async_computation.3 | async-start | bytes 2654208 | tf_op jit(solution)/shard_map/all_gather | solution.py:100
  57.1 5.0 %collective-permute-start.1 = (bf16[6,1,1,32,512]{4,3,2,1,0:T(8,128)(2,1)S(1)}, bf16[6,1,1,32,512]{4,3,2,1,0:T(8,128)(2,1)S(1)}, u32[]{:S(2)}, u32[]{:S(2)}) collective-permute-start(bf16[6,1,1,32,512]{4,3,2,1,0:T(8,128)(2,1)S(1)} %get-tuple-element.30), channel_id=1, source_target_pairs={{2,0},{4,2},{6,4},{3,1},{5,3},{7,5},{10,8},{12,10},{14,12},{11,9},... | collective-permute-start | bytes 589832 | tf_op jit(solution)/shard_map/ppermute | solution.py:17
  58.4 4.6 %collective-permute-start = (bf16[6,1,1,32,512]{4,3,2,1,0:T(8,128)(2,1)S(1)}, bf16[6,1,1,32,512]{4,3,2,1,0:T(8,128)(2,1)S(1)}, u32[]{:S(2)}, u32[]{:S(2)}) collective-permute-start(bf16[6,1,1,32,512]{4,3,2,1,0:T(8,128)(2,1)S(1)} %get-tuple-element.29), channel_id=1, source_target_pairs={{0,2},{2,4},{4,6},{1,3},{3,5},{5,7},{8,10},{10,12},{12,14},{9,11},... | collective-permute-start | bytes 589832 | tf_op jit(solution)/shard_map/ppermute | solution.py:16
  65.3 2.0 copy-start.3
  201.1 1.1 copy-start.6
  201.1 1.3 copy-start.7
  201.2 1.5 copy-start.8
  201.2 1.7 copy-start.9
  201.2 1.9 copy-start.10
  203.1 1.7 copy-start.4
Sparse Core Ops, SparseCore 0:
  32.7 142.5 reduce-scatter.1
Sparse Core Ops, SparseCore 1:
  56.0 41.4 all-gather.2
  175.4 27.8 all-gather.4

commit v5 on v4

--- a/solution.py
+++ b/solution.py
@@ -78,9 +78,14 @@
         axis=-1,
     ).reshape(-1, 9, chans)
     grad_flat = cotangent.reshape(-1, chans)
-    weight_local = lax.dot_general(
-        spike_cols, grad_flat, (((0,), (0,)), ((), ())), preferred_element_type=jnp.float32
-    )
+    half = chans // 2
+    weight_halves = [
+        lax.dot_general(
+            spike_cols, grad_flat[:, part * half : (part + 1) * half], (((0,), (0,)), ((), ())),
+            preferred_element_type=jnp.float32,
+        )
+        for part in range(2)
+    ]
     dspikes = jnp.einsum(
         "nkd,kcd->nc",
         grad_cols,
@@ -96,7 +101,9 @@
     grad_input = jnp.stack(outs)
     membrane_grad = 0.5 * carried
     total_cells = samples * data_count * lax.axis_size("rep") * rows * lax.axis_size("space") * cols
-    shard_part = lax.psum_scatter(weight_local, ("dp",) + rest, scatter_dimension=0, tiled=True)
+    shard_part = jnp.concatenate(
+        [lax.psum_scatter(part, ("dp",) + rest, scatter_dimension=0, tiled=True) for part in weight_halves], axis=1
+    )
     summed = lax.all_gather(shard_part, rest, axis=0, tiled=True)
     weight_grad = summed * (1.0 / math.sqrt(steps_count * total_cells))
     new_moment = 0.9 * moment + 0.1 * weight_grad

time: 226 us -> 312 us (1.38)
  waiting for transfers between devices: 79.6 us -> 159 us
  matrix products: 36 us -> 42.7 us
    reduce_scatter x1 -> x2, waiting for transfers between devices: 61.6 us -> 141 us  [on_device(): lax.psum_scatter(part, ('dp',) + rest, scatter_dimension=0, tiled=True)]
    dot_general x1 -> x2, matrix products: 10.2 us -> 16.8 us  [on_device(): lax.dot_general(spike_cols, grad_flat[:, part * half:(part + 1) * half],...]
    unnamed x38 -> x44, local copies, waits for them, and re-layouts: 16.3 us -> 20.6 us
  transfers between devices with their start and end apart: 9 -> 10, of which waited for: 5 -> 6; matrix products, arithmetic and copies ran while one was open for 38% -> 29% of each run, Pallas kernels for 0% -> 0%
where the time goes in v5:
time: 312 us
  waiting for transfers between devices  159 us (51%)
  local copies, waits for them, and re-layouts  49.8 us (16%)
  matrix products  42.7 us (14%)
  other arithmetic  28.2 us (9%)
  starting transfers between devices  15.9 us (5%)
  between operations  15.8 us (5%)
    reduce_scatter x2, waiting for transfers between devices, on_device(): lax.psum_scatter(part, ('dp',) + rest, scatter_dimension=0, tiled=True)  141 us
    reshape x1, local copies, waits for them, and re-layouts, on_device(): grad_cols = jnp.concatenate([grad_pad[:, :, 1 - a:1 - a + rows, 1 - b:1 -...  26.7 us
    dot_general x1, matrix products, on_device(): jnp.einsum('nkd,kcd->nc', grad_cols, weights.reshape(9, chans, chans), pr...  25.8 us
    unnamed x44, local copies, waits for them, and re-layouts  20.6 us
    dot_general x2, matrix products, on_device(): lax.dot_general(spike_cols, grad_flat[:, part * half:(part + 1) * half],...  16.8 us
    ppermute x2, waiting for transfers between devices, doubling_gather(): other = lax.ppermute(blocks, axis, pairs)  16.1 us
    unnamed x12, other arithmetic  8.41 us
    div x1, other arithmetic, on_device(): update = new_moment / (jnp.sqrt(new_second) + 1e-08)  8.02 us
  transfers between devices with their start and end apart: 10, of which 6 were waited for; matrix products, arithmetic and copies ran while one was open for 29% of the time, Pallas kernels for 0%

profile of v5, /device:TPU:0, one launch (start us, length us, event | category | flops | bytes accessed | tf_op | source)
XLA Modules:
  0.0 311.5 jit_solution(3414096461014200515)
XLA Ops:
  8.1 1.2 pad_maximum_fusion.5
  9.3 1.4 collective-permute-start.5
  10.7 3.0 collective-permute-start.4
  13.8 1.1 collective-permute-done.4
  14.9 0.4 pad_maximum_fusion
  15.2 0.1 fusion.71
  15.4 0.3 fusion.72
  15.7 0.4 fusion.73
  16.1 0.5 fusion.74
  16.6 0.2 fusion.75
  16.8 1.2 fusion.70
  18.0 0.5 fusion.11
  18.5 0.2 slice_dynamic-update-slice_fusion.2
  18.7 0.7 fusion.12
  19.4 0.7 fusion.13
  20.2 0.2 slice_dynamic-update-slice_fusion.1
  20.3 0.7 fusion.14
  21.1 0.7 fusion.15
  21.8 0.2 slice_dynamic-update-slice_fusion
  22.0 0.7 fusion.16
  22.7 5.0 %copy-done.14 = bf16[6,1,8,32,4608]{4,3,2,1,0:T(8,128)(2,1)} copy-done((bf16[6,1,8,32,4608]{4,3,2,1,0:T(8,128)(2,1)}, bf16[6,1,8,32,4608]{4,3,2,1,0:T(8,128)(2,1)S(1)}, u32[]{:S(2)}) %copy-start.14) | copy-done | bytes 14155800
  27.8 5.7 %fusion.19 = f32[4608,256]{1,0:T(8,128)} fusion(bf16[1536,4608]{1,0:T(8,128)(2,1)S(1)} %bitcast.105, bf16[1536,512]{1,0:T(8,128)(2,1)S(1)} %bitcast.93), kind=kOutput, calls=%fused_computation.61 | convolution fusion | flops 3623878656 | bytes 19660800 | tf_op jit(solution)/shard_map/dot_general | solution.py:83
  33.4 0.2 reduce-scatter.3.cloned.1.call-start
  33.7 11.2 %fusion.21 = f32[4608,256]{1,0:T(8,128)} fusion(bf16[1536,4608]{1,0:T(8,128)(2,1)} %bitcast.106, bf16[1536,512]{1,0:T(8,128)(2,1)} %bitcast.92), kind=kOutput, calls=%fused_computation.63 | convolution fusion | flops 3623878656 | bytes 19660800 | tf_op jit(solution)/shard_map/dot_general | solution.py:83
  44.9 0.0 all-gather.3.cloned.1.call-start
  45.0 3.1 collective-permute-start.2
  48.1 3.1 %collective-permute-done.2 = bf16[1,144,512]{2,1,0:T(8,128)(2,1)S(1)} collective-permute-done((bf16[1,144,512]{2,1,0:T(8,128)(2,1)S(1)}, bf16[1,144,512]{2,1,0:T(8,128)(2,1)S(1)}, u32[]{:S(2)}, u32[]{:S(2)}) %collective-permute-start.2) | collective-permute-done | bytes 147488 | tf_op jit(solution)/shard_map/ppermute | solution.py:28
  51.2 3.1 collective-permute-start.3
  54.4 13.0 %collective-permute-done.3 = bf16[2,144,512]{2,1,0:T(8,128)(2,1)S(1)} collective-permute-done((bf16[2,144,512]{2,1,0:T(8,128)(2,1)S(1)}, bf16[2,144,512]{2,1,0:T(8,128)(2,1)S(1)}, u32[]{:S(2)}, u32[]{:S(2)}) %collective-permute-start.3) | collective-permute-done | bytes 294944 | tf_op jit(solution)/shard_map/ppermute | solution.py:28
  67.3 0.9 maximum_select_fusion
  68.4 1.3 collective-permute-start.1
  69.7 3.6 %collective-permute-start = (bf16[6,1,1,32,512]{4,3,2,1,0:T(8,128)(2,1)S(1)}, bf16[6,1,1,32,512]{4,3,2,1,0:T(8,128)(2,1)S(1)}, u32[]{:S(2)}, u32[]{:S(2)}) collective-permute-start(bf16[6,1,1,32,512]{4,3,2,1,0:T(8,128)(2,1)S(1)} %get-tuple-element.31), channel_id=1, source_target_pairs={{0,2},{2,4},{4,6},{1,3},{3,5},{5,7},{8,10},{10,12},{12,14},{9,11},... | collective-permute-start | bytes 589832 | tf_op jit(solution)/shard_map/ppermute | solution.py:16
  73.3 1.0 collective-permute-done
  74.3 1.3 fusion.10
  75.6 1.7 slice_dynamic-update-slice_fusion.8
  77.3 1.4 fusion.18
  78.6 1.4 slice_dynamic-update-slice_fusion.7
  80.0 2.1 slice_dynamic-update-slice_fusion.6
  82.1 1.4 constant_dynamic-update-slice_fusion
  83.5 1.5 slice_dynamic-update-slice_fusion.5
  85.0 2.0 slice_dynamic-update-slice_fusion.4
  86.9 1.4 fusion.17
  88.3 1.4 slice_dynamic-update-slice_fusion.3
  89.7 26.7 %reshape.619 = bf16[1536,9,512]{2,1,0:T(8,128)(2,1)} reshape(bf16[6,1,8,32,4608]{4,3,2,1,0:T(8,128)(2,1)} %slice_dynamic-update-slice_fusion.3) | data formatting | bytes 28311552 | tf_op jit(solution)/shard_map/reshape | solution.py:79
  116.4 0.9 fusion.69
  117.4 1.6 fusion.26
  119.0 28.4 %reduce-scatter.5.cloned.1.call-done = f32[144,256]{1,0:T(8,128)} async-done(((f32[4608,256]{1,0:T(8,128)}), f32[144,256]{1,0:T(8,128)}) %reduce-scatter.5.cloned.1.call-update) | async-done | bytes 147472 | tf_op jit(solution)/shard_map/reduce_scatter | solution.py:105
  147.4 112.5 %reduce-scatter.3.cloned.1.call-done = f32[144,256]{1,0:T(8,128)} async-done(((f32[4608,256]{1,0:T(8,128)}), f32[144,256]{1,0:T(8,128)}) %reduce-scatter.3.cloned.1.call-update) | async-done | bytes 147472 | tf_op jit(solution)/shard_map/reduce_scatter | solution.py:105
  259.9 1.7 pad_maximum_fusion.3
  261.7 25.8 %fusion.3 = f32[1536,512]{1,0:T(8,128)S(1)} fusion(bf16[9,512,512]{2,1,0:T(8,128)(2,1)} %bitcast.107, bf16[1536,9,512]{2,1,0:T(8,128)(2,1)} %reshape.619), kind=kOutput, calls=%fused_computation.5 | convolution fusion | flops 7247757312 | bytes 22020096 | tf_op jit(solution)/shard_map/nkd,kcd->nc/dot_general | solution.py:89
  287.6 0.3 fusion.96
  287.9 0.7 copy-done.8
  288.6 0.2 copy-done.9
  288.8 0.2 copy-done.10
  289.0 0.2 copy-done.11
  289.2 0.2 copy-done.12
  289.4 1.7 broadcast_multiply_fusion.1
  291.1 0.8 fusion.77
  291.9 0.9 fusion.79
  292.8 0.8 fusion.81
  293.6 0.8 fusion.83
  294.4 0.9 fusion.85
  295.3 0.8 fusion.87
  296.1 8.0 %add_divide_fusion = (f32[1152,512]{1,0:T(8,128)}, f32[1152,512]{1,0:T(8,128)}, f32[1152,512]{1,0:T(8,128)}, f32[1152,512]{1,0:T(8,128)}) fusion(f32[1152,512]{1,0:T(8,128)} %all-gather.5.cloned.1.call-done, f32[1152,512]{1,0:T(8,128)} %param.11, f32[1152,512]{1,0:T(8,128)} %param.10), kind=kLoop, calls=%fused_computation.11 | loop fusion | flops 5898240 | bytes 16515072 | tf_op jit(solution)/shard_map/div | solution.py:111
  (38 shorter events, 0.4 us)
Async XLA Ops:
  8.0 36.9 %copy-start = (f32[1152,512]{1,0:T(8,128)S(1)}, f32[1152,512]{1,0:T(8,128)}, u32[]{:S(2)}) copy-start(f32[1152,512]{1,0:T(8,128)} %param.9) | copy-start | bytes 7077892
  8.0 6.9 %copy-start.13 = (bf16[1,8,32,512]{3,2,1,0:T(8,128)(2,1)S(1)}, bf16[1,8,32,512]{3,2,1,0:T(8,128)(2,1)}, u32[]{:S(2)}) copy-start(bf16[1,8,32,512]{3,2,1,0:T(8,128)(2,1)} %param.7) | copy-start | bytes 786436
  8.0 139.4 %reduce-scatter.5.cloned.1.call-start = ((), (), s32[]{:S(2)}) async-start(), calls=%async_computation.4 | async-start | bytes 4866048 | tf_op jit(solution)/shard_map/reduce_scatter | solution.py:105
  8.1 6.8 %copy-start.7 = (bf16[6,1,8,32,512]{4,3,2,1,0:T(8,128)(2,1)S(1)}, bf16[6,1,8,32,512]{4,3,2,1,0:T(8,128)(2,1)}, u32[]{:S(2)}) copy-start(bf16[6,1,8,32,512]{4,3,2,1,0:T(8,128)(2,1)} %param.6) | copy-start | bytes 4718596
  9.3 4.5 %collective-permute-start.5 = (bf16[7,1,1,32,512]{4,3,2,1,0:T(8,128)(2,1)S(1)}, bf16[7,1,1,32,512]{4,3,2,1,0:T(8,128)(2,1)S(1)}, u32[]{:S(2)}, u32[]{:S(2)}) collective-permute-start(bf16[7,1,1,32,512]{4,3,2,1,0:T(8,128)(2,1)S(1)} %get-tuple-element.30), channel_id=1, source_target_pairs={{2,0},{4,2},{6,4},{3,1},{5,3},{7,5},{10,8},{12,10},{14,12},{11,9},... | collective-permute-start | bytes 688136 | tf_op jit(solution)/shard_map/ppermute | solution.py:17
  10.7 4.1 %collective-permute-start.4 = (bf16[7,1,1,32,512]{4,3,2,1,0:T(8,128)(2,1)S(1)}, bf16[7,1,1,32,512]{4,3,2,1,0:T(8,128)(2,1)S(1)}, u32[]{:S(2)}, u32[]{:S(2)}) collective-permute-start(bf16[7,1,1,32,512]{4,3,2,1,0:T(8,128)(2,1)S(1)} %get-tuple-element.29), channel_id=1, source_target_pairs={{0,2},{2,4},{4,6},{1,3},{3,5},{5,7},{8,10},{10,12},{12,14},{9,11},... | collective-permute-start | bytes 688136 | tf_op jit(solution)/shard_map/ppermute | solution.py:16
  15.2 1.6 copy-start.2
  22.0 5.8 %copy-start.4 = (bf16[6,1,8,32,512]{4,3,2,1,0:T(8,128)(2,1)S(1)}, bf16[6,1,8,32,512]{4,3,2,1,0:T(8,128)(2,1)}, u32[]{:S(2)}) copy-start(bf16[6,1,8,32,512]{4,3,2,1,0:T(8,128)(2,1)} %param.8) | copy-start | bytes 4718596
  22.7 5.0 %copy-start.14 = (bf16[6,1,8,32,4608]{4,3,2,1,0:T(8,128)(2,1)}, bf16[6,1,8,32,4608]{4,3,2,1,0:T(8,128)(2,1)S(1)}, u32[]{:S(2)}) copy-start(bf16[6,1,8,32,4608]{4,3,2,1,0:T(8,128)(2,1)S(1)} %fusion.16) | copy-start | bytes 42467332
  33.4 226.4 %reduce-scatter.3.cloned.1.call-start = ((), (), s32[]{:S(2)}) async-start(), calls=%async_computation.3 | async-start | bytes 4866048 | tf_op jit(solution)/shard_map/reduce_scatter | solution.py:105
  44.9 216.8 %all-gather.3.cloned.1.call-start = ((), (), s32[]{:S(2)}) async-start(), calls=%async_computation.2 | async-start | bytes 5308416 | tf_op jit(solution)/shard_map/all_gather | solution.py:53
  45.0 23.4 %copy-start.5 = (bf16[6,1,8,32,512]{4,3,2,1,0:T(8,128)(2,1)S(1)}, bf16[6,1,8,32,512]{4,3,2,1,0:T(8,128)(2,1)}, u32[]{:S(2)}) copy-start(bf16[6,1,8,32,512]{4,3,2,1,0:T(8,128)(2,1)} %param.8) | copy-start | bytes 4718596
  45.0 6.2 %collective-permute-start.2 = (bf16[1,144,512]{2,1,0:T(8,128)(2,1)S(1)}, bf16[1,144,512]{2,1,0:T(8,128)(2,1)S(1)}, u32[]{:S(2)}, u32[]{:S(2)}) collective-permute-start(bf16[1,144,512]{2,1,0:T(8,128)(2,1)S(1)} %fusion.88), channel_id=1, source_target_pairs={{0,8},{8,0},{16,24},{24,16},{1,9},{9,1},{17,25},{25,17},{2,10},{10... | collective-permute-start | bytes 442376 | tf_op jit(solution)/shard_map/ppermute | solution.py:28
  51.2 16.1 %collective-permute-start.3 = (bf16[2,144,512]{2,1,0:T(8,128)(2,1)S(1)}, bf16[2,144,512]{2,1,0:T(8,128)(2,1)S(1)}, u32[]{:S(2)}, u32[]{:S(2)}) collective-permute-start(bf16[2,144,512]{2,1,0:T(8,128)(2,1)S(1)} %maximum_select_fusion.1), channel_id=1, source_target_pairs={{0,16},{8,24},{16,0},{24,8},{1,17},{9,25},{17,1},{25,9},{2,18},{10... | collective-permute-start | bytes 884744 | tf_op jit(solution)/shard_map/ppermute | solution.py:28
  68.3 227.8 %all-gather.5.cloned.1.call-start = ((), (), s32[]{:S(2)}) async-start(), calls=%async_computation.5 | async-start | bytes 2654208 | tf_op jit(solution)/shard_map/all_gather | solution.py:107
  68.4 4.9 %collective-permute-start.1 = (bf16[6,1,1,32,512]{4,3,2,1,0:T(8,128)(2,1)S(1)}, bf16[6,1,1,32,512]{4,3,2,1,0:T(8,128)(2,1)S(1)}, u32[]{:S(2)}, u32[]{:S(2)}) collective-permute-start(bf16[6,1,1,32,512]{4,3,2,1,0:T(8,128)(2,1)S(1)} %get-tuple-element.32), channel_id=1, source_target_pairs={{2,0},{4,2},{6,4},{3,1},{5,3},{7,5},{10,8},{12,10},{14,12},{11,9},... | collective-permute-start | bytes 589832 | tf_op jit(solution)/shard_map/ppermute | solution.py:17
  69.7 4.6 %collective-permute-start = (bf16[6,1,1,32,512]{4,3,2,1,0:T(8,128)(2,1)S(1)}, bf16[6,1,1,32,512]{4,3,2,1,0:T(8,128)(2,1)S(1)}, u32[]{:S(2)}, u32[]{:S(2)}) collective-permute-start(bf16[6,1,1,32,512]{4,3,2,1,0:T(8,128)(2,1)S(1)} %get-tuple-element.31), channel_id=1, source_target_pairs={{0,2},{2,4},{4,6},{1,3},{3,5},{5,7},{8,10},{10,12},{12,14},{9,11},... | collective-permute-start | bytes 589832 | tf_op jit(solution)/shard_map/ppermute | solution.py:16
  89.7 26.7 %copy-start.3 = (bf16[7,1,10,32,512]{4,3,2,1,0:T(8,128)(2,1)S(1)}, bf16[7,1,10,32,512]{4,3,2,1,0:T(8,128)(2,1)}, u32[]{:S(2)}) copy-start(bf16[7,1,10,32,512]{4,3,2,1,0:T(8,128)(2,1)} %copy-done.2) | copy-start | bytes 6881284
  287.5 1.1 copy-start.8
  287.5 1.3 copy-start.9
  287.5 1.5 copy-start.10
  287.5 1.7 copy-start.11
  287.5 1.9 copy-start.12
  289.4 1.7 copy-start.6
  296.1 8.0 %copy-start.1 = (f32[1152,512]{1,0:T(8,128)S(1)}, f32[1152,512]{1,0:T(8,128)}, u32[]{:S(2)}) copy-start(f32[1152,512]{1,0:T(8,128)} %param.9) | copy-start | bytes 7077892
Sparse Core Ops, SparseCore 0:
  33.6 113.7 reduce-scatter.4
  153.8 106.0 reduce-scatter.2
Sparse Core Ops, SparseCore 1:
  68.4 45.6 all-gather.2
  261.7 27.9 all-gather.4

commit v6 on v4

--- a/solution.py
+++ b/solution.py
@@ -30,6 +30,25 @@
         blocks = jnp.where(low, jnp.concatenate([blocks, other]), jnp.concatenate([other, blocks]))
         bit += 1
     return blocks
+
+
+def halving_scatter(blocks, names, stages):
+    names = list(names)
+    for axis, bit in stages:
+        dim = names.index((axis, bit))
+        peers = lax.axis_size(axis)
+        first = (lax.axis_index(axis) // (1 << bit)) % 2 == 0
+        low = lax.index_in_dim(blocks, 0, dim, keepdims=False)
+        high = lax.index_in_dim(blocks, 1, dim, keepdims=False)
+        pairs = [(j, j ^ (1 << bit)) for j in range(peers)]
+        sent = lax.ppermute(jnp.where(first, high, low), axis, pairs)
+        blocks = jnp.where(first, low, high) + sent
+        names.pop(dim)
+    return blocks, names
+
+
+def bits_of(axis):
+    return [(axis, bit) for bit in range(lax.axis_size(axis).bit_length() - 1)]
 
 
 def surrogate(potential):
@@ -96,7 +115,20 @@
     grad_input = jnp.stack(outs)
     membrane_grad = 0.5 * carried
     total_cells = samples * data_count * lax.axis_size("rep") * rows * lax.axis_size("space") * cols
-    shard_part = lax.psum_scatter(weight_local, ("dp",) + rest, scatter_dimension=0, tiled=True)
+    names = [entry for axis in ("dp",) + rest for entry in reversed(bits_of(axis))]
+    piece_shape = (weight_local.shape[0] // 2 ** len(names), weight_local.shape[1])
+    blocks = weight_local.reshape((2,) * len(names) + piece_shape)
+    space_bits, rep_bits, dp_bits = bits_of("space"), bits_of("rep"), bits_of("dp")
+    blocks, names = halving_scatter(blocks, names, space_bits[:1])
+    half = chans // 2
+    orders = (space_bits[1:] + rep_bits + dp_bits, rep_bits + space_bits[1:] + dp_bits)
+    shard_part = jnp.concatenate(
+        [
+            halving_scatter(blocks[..., part * half : (part + 1) * half], names, order)[0]
+            for part, order in enumerate(orders)
+        ],
+        axis=1,
+    )
     summed = lax.all_gather(shard_part, rest, axis=0, tiled=True)
     weight_grad = summed * (1.0 / math.sqrt(steps_count * total_cells))
     new_moment = 0.9 * moment + 0.1 * weight_grad

time: 226 us -> 242 us (1.071)
  waiting for transfers between devices: 79.6 us -> 42.8 us
  local copies, waits for them, and re-layouts: 46.7 us -> 69.8 us
  starting transfers between devices: 15.8 us -> 33.7 us
  other arithmetic: 31.1 us -> 43 us
    reduce_scatter x1 -> x0, waiting for transfers between devices: 61.6 us -> none  [on_device(): lax.psum_scatter(weight_local, ('dp',) + rest, scatter_dimension=0, tiled...]
    ppermute x0 -> x9, waiting for transfers between devices: none -> 31 us  [halving_scatter(): sent = lax.ppermute(jnp.where(first, high, low), axis, pairs)]
    ppermute x0 -> x9, starting transfers between devices: none -> 20.4 us  [halving_scatter(): sent = lax.ppermute(jnp.where(first, high, low), axis, pairs)]
    reshape x0 -> x1, local copies, waits for them, and re-layouts: none -> 18.6 us  [on_device(): spike_cols = jnp.concatenate([spike_pad[:, :, 1 + a:1 + a + rows, 1 + b:1...]
    add x0 -> x9, other arithmetic: none -> 8.62 us  [halving_scatter(): blocks = jnp.where(first, low, high) + sent]
    select_n x0 -> x9, other arithmetic: none -> 6.94 us  [halving_scatter(): sent = lax.ppermute(jnp.where(first, high, low), axis, pairs)]
    ppermute x2, waiting for transfers between devices: 16.1 us -> 10.7 us  [doubling_gather(): other = lax.ppermute(blocks, axis, pairs)]
    unnamed x38 -> x60, local copies, waits for them, and re-layouts: 16.3 us -> 19.9 us
  transfers between devices with their start and end apart: 9 -> 17, of which waited for: 5 -> 9; matrix products, arithmetic and copies ran while one was open for 38% -> 35% of each run, Pallas kernels for 0% -> 0%
where the time goes in v6:
time: 242 us; the launch traced here: 241 us
  local copies, waits for them, and re-layouts  69.8 us (29%)
  other arithmetic  43 us (18%)
  waiting for transfers between devices  42.8 us (18%)
  matrix products  36.8 us (15%)
  starting transfers between devices  33.7 us (14%)
  between operations  14.7 us (6%)
    ppermute x9, waiting for transfers between devices, halving_scatter(): sent = lax.ppermute(jnp.where(first, high, low), axis, pairs)  31 us
    reshape x1, local copies, waits for them, and re-layouts, on_device(): grad_cols = jnp.concatenate([grad_pad[:, :, 1 - a:1 - a + rows, 1 - b:1 -...  26.8 us
    dot_general x1, matrix products, on_device(): jnp.einsum('nkd,kcd->nc', grad_cols, weights.reshape(9, chans, chans), pr...  25.8 us
    ppermute x9, starting transfers between devices, halving_scatter(): sent = lax.ppermute(jnp.where(first, high, low), axis, pairs)  20.4 us
    unnamed x60, local copies, waits for them, and re-layouts  19.9 us
    reshape x1, local copies, waits for them, and re-layouts, on_device(): spike_cols = jnp.concatenate([spike_pad[:, :, 1 + a:1 + a + rows, 1 + b:1...  18.6 us
    dot_general x1, matrix products, on_device(): lax.dot_general(spike_cols, grad_flat, (((0,), (0,)), ((), ())), preferre...  11 us
    ppermute x2, waiting for transfers between devices, doubling_gather(): other = lax.ppermute(blocks, axis, pairs)  10.7 us
  transfers between devices with their start and end apart: 17, of which 9 were waited for; matrix products, arithmetic and copies ran while one was open for 35% of the time, Pallas kernels for 0%

profile of v6, /device:TPU:0, one launch (start us, length us, event | category | flops | bytes accessed | tf_op | source)
XLA Modules:
  0.0 240.8 jit_solution(1855034459707909233)
XLA Ops:
  7.2 1.2 pad_maximum_fusion.5
  8.5 1.3 collective-permute-start.5
  9.8 3.0 %collective-permute-start.4 = (bf16[7,1,1,32,512]{4,3,2,1,0:T(8,128)(2,1)S(1)}, bf16[7,1,1,32,512]{4,3,2,1,0:T(8,128)(2,1)S(1)}, u32[]{:S(2)}, u32[]{:S(2)}) collective-permute-start(bf16[7,1,1,32,512]{4,3,2,1,0:T(8,128)(2,1)S(1)} %get-tuple-element.31), channel_id=1, source_target_pairs={{0,2},{2,4},{4,6},{1,3},{3,5},{5,7},{8,10},{10,12},{12,14},{9,11},... | collective-permute-start | bytes 688136 | tf_op jit(solution)/shard_map/ppermute | solution.py:16
  12.9 1.1 collective-permute-done.4
  13.9 1.8 pad_maximum_fusion
  17.3 1.1 fusion.72
  19.1 0.7 fusion.14
  19.8 0.7 fusion.15
  20.8 0.7 fusion.16
  21.5 0.7 fusion.17
  22.4 0.7 fusion.18
  23.2 5.1 %copy-done.9 = bf16[6,1,8,32,4608]{4,3,2,1,0:T(8,128)(2,1)} copy-done((bf16[6,1,8,32,4608]{4,3,2,1,0:T(8,128)(2,1)}, bf16[6,1,8,32,4608]{4,3,2,1,0:T(8,128)(2,1)S(1)}, u32[]{:S(2)}) %copy-start.9) | copy-done | bytes 14155800
  28.2 18.6 %copy.32 = bf16[1536,4608]{0,1:T(8,128)(2,1)} copy(bf16[1536,4608]{1,0:T(8,128)(2,1)} %bitcast.194) | data formatting | bytes 28311552 | tf_op jit(solution)/shard_map/reshape | solution.py:94
  46.8 11.0 %fusion.103 = f32[2,2,2,2,2,144,512]{6,5,4,3,2,1,0:T(8,128)S(1)} fusion(bf16[2,2,2,2,2,144,1536]{6,5,4,3,2,1,0:T(8,128)(2,1)} %bitcast.195, bf16[1536,512,1,1,1,1,1]{1,0,6,5,4,3,2:T(8,128)(2,1)} %bitcast.191), kind=kOutput, calls=%fused_computation.178 | convolution fusion | flops 7247757312 | bytes 25165824 | tf_op jit(solution)/shard_map/dot_general | solution.py:100
  57.8 3.8 %select_bitcast_fusion = f32[2,2,2,2,144,512]{5,4,3,2,1,0:T(8,128)} fusion(f32[2,2,2,2,2,144,512]{6,5,4,3,2,1,0:T(8,128)S(1)} %fusion.103, pred[]{:T(512)S(6)} %eq.37), kind=kLoop, calls=%fused_computation.8 | loop fusion | flops 1179648 | bytes 14155777 | tf_op jit(solution)/shard_map/jit(_where)/select_n | solution.py:44
  61.6 1.2 copy-done.6
  62.8 4.4 %collective-permute-start.6 = (f32[2,2,2,2,144,512]{5,4,3,2,1,0:T(8,128)}, f32[2,2,2,2,144,512]{5,4,3,2,1,0:T(8,128)}, u32[]{:S(2)}, u32[]{:S(2)}) collective-permute-start(f32[2,2,2,2,144,512]{5,4,3,2,1,0:T(8,128)} %select_bitcast_fusion), channel_id=1, source_target_pairs={{0,2},{2,0},{4,6},{6,4},{1,3},{3,1},{5,7},{7,5},{8,10},{10,8},{12,... | collective-permute-start | bytes 14155784 | tf_op jit(solution)/shard_map/ppermute | solution.py:44
  67.2 1.6 collective-permute-start.2
  68.9 4.2 %collective-permute-done.2 = bf16[1,144,512]{2,1,0:T(8,128)(2,1)S(1)} collective-permute-done((bf16[1,144,512]{2,1,0:T(8,128)(2,1)S(1)}, bf16[1,144,512]{2,1,0:T(8,128)(2,1)S(1)}, u32[]{:S(2)}, u32[]{:S(2)}) %collective-permute-start.2) | collective-permute-done | bytes 147488 | tf_op jit(solution)/shard_map/ppermute | solution.py:28
  73.1 2.7 %collective-permute-start.3 = (bf16[2,144,512]{2,1,0:T(8,128)(2,1)S(1)}, bf16[2,144,512]{2,1,0:T(8,128)(2,1)S(1)}, u32[]{:S(2)}, u32[]{:S(2)}) collective-permute-start(bf16[2,144,512]{2,1,0:T(8,128)(2,1)S(1)} %maximum_select_fusion.1), channel_id=1, source_target_pairs={{0,16},{8,24},{16,0},{24,8},{1,17},{9,25},{17,1},{25,9},{2,18},{10... | collective-permute-start | bytes 884744 | tf_op jit(solution)/shard_map/ppermute | solution.py:28
  75.7 1.7 fusion.102
  77.5 1.3 collective-permute-start.1
  78.7 3.0 %collective-permute-start = (bf16[6,1,1,32,512]{4,3,2,1,0:T(8,128)(2,1)S(1)}, bf16[6,1,1,32,512]{4,3,2,1,0:T(8,128)(2,1)S(1)}, u32[]{:S(2)}, u32[]{:S(2)}) collective-permute-start(bf16[6,1,1,32,512]{4,3,2,1,0:T(8,128)(2,1)S(1)} %get-tuple-element.33), channel_id=1, source_target_pairs={{0,2},{2,4},{4,6},{1,3},{3,5},{5,7},{8,10},{10,12},{12,14},{9,11},... | collective-permute-start | bytes 589832 | tf_op jit(solution)/shard_map/ppermute | solution.py:16
  81.9 6.5 %collective-permute-done.3 = bf16[2,144,512]{2,1,0:T(8,128)(2,1)S(1)} collective-permute-done((bf16[2,144,512]{2,1,0:T(8,128)(2,1)S(1)}, bf16[2,144,512]{2,1,0:T(8,128)(2,1)S(1)}, u32[]{:S(2)}, u32[]{:S(2)}) %collective-permute-start.3) | collective-permute-done | bytes 294944 | tf_op jit(solution)/shard_map/ppermute | solution.py:28
  88.4 0.9 maximum_select_fusion
  89.6 1.3 fusion.12
  91.8 0.7 slice_dynamic-update-slice_fusion.6
  93.0 0.7 slice_dynamic-update-slice_fusion.4
  93.7 5.5 %copy-done.8 = bf16[6,1,8,32,4608]{4,3,2,1,0:T(8,128)(2,1)} copy-done((bf16[6,1,8,32,4608]{4,3,2,1,0:T(8,128)(2,1)}, bf16[6,1,8,32,4608]{4,3,2,1,0:T(8,128)(2,1)S(1)}, u32[]{:S(2)}) %copy-start.8) | copy-done | bytes 14155800
  99.2 4.5 %fusion.4 = f32[2,2,2,2,144,512]{5,4,3,2,1,0:T(8,128)S(1)} fusion(f32[2,2,2,2,144,512]{5,4,3,2,1,0:T(8,128)} %collective-permute-done.6, f32[2,2,2,2,2,144,512]{6,5,4,3,2,1,0:T(8,128)S(1)} %bitcast.193, pred[]{:T(512)S(6)} %eq.37), kind=kLoop, calls=%fused_computation.7 | loop fusion | flops 2359296 | bytes 18874368 | tf_op jit(solution)/shard_map/add | solution.py:45
  103.7 1.6 select_bitcast_fusion.1
  105.3 1.4 collective-permute-start.11
  107.0 1.3 select_bitcast_fusion.2
  108.3 3.6 %collective-permute-start.7 = (f32[2,2,2,144,256]{4,3,0,1,2:T(8,128)}, f32[2,2,2,144,256]{4,3,0,1,2:T(8,128)}, u32[]{:S(2)}, u32[]{:S(2)}) collective-permute-start(f32[2,2,2,144,256]{4,3,0,1,2:T(8,128)} %select_bitcast_fusion.2), channel_id=1, source_target_pairs={{0,4},{2,6},{4,0},{6,2},{1,5},{3,7},{5,1},{7,3},{8,12},{10,14},{12... | collective-permute-start | bytes 3538952 | tf_op jit(solution)/shard_map/ppermute | solution.py:44
  111.9 1.4 fusion.19
  113.3 1.5 slice_dynamic-update-slice_fusion.3
  114.8 26.8 %reshape.657 = bf16[1536,9,512]{2,1,0:T(8,128)(2,1)} reshape(bf16[6,1,8,32,4608]{4,3,2,1,0:T(8,128)(2,1)} %slice_dynamic-update-slice_fusion.3) | data formatting | bytes 28311552 | tf_op jit(solution)/shard_map/reshape | solution.py:98
  141.6 1.6 fusion.26
  143.2 4.3 %collective-permute-done.11 = f32[2,2,2,144,256]{4,3,2,1,0:T(8,128)} collective-permute-done((f32[2,2,2,144,256]{4,3,2,1,0:T(8,128)}, f32[2,2,2,144,256]{4,3,2,1,0:T(8,128)}, u32[]{:S(2)}, u32[]{:S(2)}) %collective-permute-start.11) | collective-permute-done | bytes 1179680 | tf_op jit(solution)/shard_map/ppermute | solution.py:44
  147.5 2.2 fusion.22
  149.8 1.5 collective-permute-start.12
  151.4 1.5 bitcast_add_fusion
  153.0 1.1 collective-permute-start.8
  154.1 0.9 fusion.71
  155.0 9.5 %collective-permute-done.12 = f32[2,2,144,256]{3,2,1,0:T(8,128)S(1)} collective-permute-done((f32[2,2,144,256]{3,2,1,0:T(8,128)S(1)}, f32[2,2,144,256]{3,2,1,0:T(8,128)S(1)}, u32[]{:S(2)}, u32[]{:S(2)}) %collective-permute-start.12) | collective-permute-done | bytes 589856 | tf_op jit(solution)/shard_map/ppermute | solution.py:44
  164.7 2.0 collective-permute-start.13
  166.8 2.3 collective-permute-start.9
  169.1 7.1 %collective-permute-done.13 = f32[2,144,256]{2,1,0:T(8,128)S(1)} collective-permute-done((f32[2,144,256]{2,1,0:T(8,128)S(1)}, f32[2,144,256]{2,1,0:T(8,128)S(1)}, u32[]{:S(2)}, u32[]{:S(2)}) %collective-permute-start.13) | collective-permute-done | bytes 294944 | tf_op jit(solution)/shard_map/ppermute | solution.py:44
  176.3 1.9 collective-permute-start.14
  178.2 2.4 collective-permute-done.9
  180.7 2.2 collective-permute-start.10
  182.9 3.4 %collective-permute-done.14 = f32[144,256]{1,0:T(8,128)S(1)} collective-permute-done((f32[144,256]{1,0:T(8,128)S(1)}, f32[144,256]{1,0:T(8,128)S(1)}, u32[]{:S(2)}, u32[]{:S(2)}) %collective-permute-start.14) | collective-permute-done | bytes 147488 | tf_op jit(solution)/shard_map/ppermute | solution.py:44
  186.4 4.3 %collective-permute-done.10 = f32[144,256]{1,0:T(8,128)S(1)} collective-permute-done((f32[144,256]{1,0:T(8,128)S(1)}, f32[144,256]{1,0:T(8,128)S(1)}, u32[]{:S(2)}, u32[]{:S(2)}) %collective-permute-start.10) | collective-permute-done | bytes 147488 | tf_op jit(solution)/shard_map/ppermute | solution.py:44
  190.7 0.7 pad_maximum_fusion.3
  191.5 25.8 %fusion.5 = f32[1536,512]{1,0:T(8,128)S(1)} fusion(bf16[9,512,512]{2,1,0:T(8,128)(2,1)} %bitcast.207, bf16[1536,9,512]{2,1,0:T(8,128)(2,1)} %reshape.657), kind=kOutput, calls=%fused_computation.9 | convolution fusion | flops 7247757312 | bytes 22020096 | tf_op jit(solution)/shard_map/nkd,kcd->nc/dot_general | solution.py:103
  217.7 0.7 copy-done.14
  219.3 1.7 broadcast_multiply_fusion.1
  221.0 0.8 fusion.81
  221.8 0.9 fusion.83
  222.7 0.8 fusion.85
  223.5 0.8 fusion.87
  224.3 0.9 fusion.89
  225.2 0.8 fusion.91
  225.9 8.0 %add_divide_fusion = (f32[1152,512]{1,0:T(8,128)}, f32[1152,512]{1,0:T(8,128)}, f32[1152,512]{1,0:T(8,128)}, f32[1152,512]{1,0:T(8,128)}) fusion(f32[1152,512]{1,0:T(8,128)} %all-gather.5.cloned.1.call-done, f32[1152,512]{1,0:T(8,128)} %param.11, f32[1152,512]{1,0:T(8,128)} %param.10), kind=kLoop, calls=%fused_computation.15 | loop fusion | flops 5898240 | bytes 16515072 | tf_op jit(solution)/shard_map/div | solution.py:136
  (86 shorter events, 6.5 us)
Async XLA Ops:
  7.2 60.0 %copy-start = (f32[1152,512]{1,0:T(8,128)S(1)}, f32[1152,512]{1,0:T(8,128)}, u32[]{:S(2)}) copy-start(f32[1152,512]{1,0:T(8,128)} %param.9) | copy-start | bytes 7077892
  7.2 6.7 %copy-start.19 = (bf16[1,8,32,512]{3,2,1,0:T(8,128)(2,1)S(1)}, bf16[1,8,32,512]{3,2,1,0:T(8,128)(2,1)}, u32[]{:S(2)}) copy-start(bf16[1,8,32,512]{3,2,1,0:T(8,128)(2,1)} %param.7) | copy-start | bytes 786436
  7.2 184.3 %all-gather.3.cloned.1.call-start = ((), (), s32[]{:S(2)}) async-start(), calls=%async_computation | async-start | bytes 5308416 | tf_op jit(solution)/shard_map/all_gather | solution.py:72
  8.5 4.4 %collective-permute-start.5 = (bf16[7,1,1,32,512]{4,3,2,1,0:T(8,128)(2,1)S(1)}, bf16[7,1,1,32,512]{4,3,2,1,0:T(8,128)(2,1)S(1)}, u32[]{:S(2)}, u32[]{:S(2)}) collective-permute-start(bf16[7,1,1,32,512]{4,3,2,1,0:T(8,128)(2,1)S(1)} %get-tuple-element.32), channel_id=1, source_target_pairs={{2,0},{4,2},{6,4},{3,1},{5,3},{7,5},{10,8},{12,10},{14,12},{11,9},... | collective-permute-start | bytes 688136 | tf_op jit(solution)/shard_map/ppermute | solution.py:17
  9.8 4.1 %collective-permute-start.4 = (bf16[7,1,1,32,512]{4,3,2,1,0:T(8,128)(2,1)S(1)}, bf16[7,1,1,32,512]{4,3,2,1,0:T(8,128)(2,1)S(1)}, u32[]{:S(2)}, u32[]{:S(2)}) collective-permute-start(bf16[7,1,1,32,512]{4,3,2,1,0:T(8,128)(2,1)S(1)} %get-tuple-element.31), channel_id=1, source_target_pairs={{0,2},{2,4},{4,6},{1,3},{3,5},{5,7},{8,10},{10,12},{12,14},{9,11},... | collective-permute-start | bytes 688136 | tf_op jit(solution)/shard_map/ppermute | solution.py:16
  15.7 1.6 copy-start.2
  23.1 5.1 %copy-start.9 = (bf16[6,1,8,32,4608]{4,3,2,1,0:T(8,128)(2,1)}, bf16[6,1,8,32,4608]{4,3,2,1,0:T(8,128)(2,1)S(1)}, u32[]{:S(2)}) copy-start(bf16[6,1,8,32,4608]{4,3,2,1,0:T(8,128)(2,1)S(1)} %fusion.18) | copy-start | bytes 42467332
  57.8 5.0 %copy-start.6 = (f32[2,2,2,2,2,144,512]{6,5,4,3,2,1,0:T(8,128)}, f32[2,2,2,2,2,144,512]{6,5,4,3,2,1,0:T(8,128)S(1)}, u32[]{:S(2)}) copy-start(f32[2,2,2,2,2,144,512]{6,5,4,3,2,1,0:T(8,128)S(1)} %fusion.103) | copy-start | bytes 28311556
  62.8 36.4 %collective-permute-start.6 = (f32[2,2,2,2,144,512]{5,4,3,2,1,0:T(8,128)}, f32[2,2,2,2,144,512]{5,4,3,2,1,0:T(8,128)}, u32[]{:S(2)}, u32[]{:S(2)}) collective-permute-start(f32[2,2,2,2,144,512]{5,4,3,2,1,0:T(8,128)} %select_bitcast_fusion), channel_id=1, source_target_pairs={{0,2},{2,0},{4,6},{6,4},{1,3},{3,1},{5,7},{7,5},{8,10},{10,8},{12,... | collective-permute-start | bytes 14155784 | tf_op jit(solution)/shard_map/ppermute | solution.py:44
  67.2 22.4 %copy-start.4 = (bf16[6,1,8,32,512]{4,3,2,1,0:T(8,128)(2,1)S(1)}, bf16[6,1,8,32,512]{4,3,2,1,0:T(8,128)(2,1)}, u32[]{:S(2)}) copy-start(bf16[6,1,8,32,512]{4,3,2,1,0:T(8,128)(2,1)} %param.8) | copy-start | bytes 4718596
  67.2 5.8 %collective-permute-start.2 = (bf16[1,144,512]{2,1,0:T(8,128)(2,1)S(1)}, bf16[1,144,512]{2,1,0:T(8,128)(2,1)S(1)}, u32[]{:S(2)}, u32[]{:S(2)}) collective-permute-start(bf16[1,144,512]{2,1,0:T(8,128)(2,1)S(1)} %fusion.92), channel_id=1, source_target_pairs={{0,8},{8,0},{16,24},{24,16},{1,9},{9,1},{17,25},{25,17},{2,10},{10... | collective-permute-start | bytes 442376 | tf_op jit(solution)/shard_map/ppermute | solution.py:28
  73.1 15.3 %collective-permute-start.3 = (bf16[2,144,512]{2,1,0:T(8,128)(2,1)S(1)}, bf16[2,144,512]{2,1,0:T(8,128)(2,1)S(1)}, u32[]{:S(2)}, u32[]{:S(2)}) collective-permute-start(bf16[2,144,512]{2,1,0:T(8,128)(2,1)S(1)} %maximum_select_fusion.1), channel_id=1, source_target_pairs={{0,16},{8,24},{16,0},{24,8},{1,17},{9,25},{17,1},{25,9},{2,18},{10... | collective-permute-start | bytes 884744 | tf_op jit(solution)/shard_map/ppermute | solution.py:28
  77.5 12.1 %collective-permute-start.1 = (bf16[6,1,1,32,512]{4,3,2,1,0:T(8,128)(2,1)}, bf16[6,1,1,32,512]{4,3,2,1,0:T(8,128)(2,1)S(1)}, u32[]{:S(2)}, u32[]{:S(2)}) collective-permute-start(bf16[6,1,1,32,512]{4,3,2,1,0:T(8,128)(2,1)} %get-tuple-element.34), channel_id=1, source_target_pairs={{2,0},{4,2},{6,4},{3,1},{5,3},{7,5},{10,8},{12,10},{14,12},{11,9},... | collective-permute-start | bytes 589832 | tf_op jit(solution)/shard_map/ppermute | solution.py:17
  78.7 10.9 %collective-permute-start = (bf16[6,1,1,32,512]{4,3,2,1,0:T(8,128)(2,1)S(1)}, bf16[6,1,1,32,512]{4,3,2,1,0:T(8,128)(2,1)S(1)}, u32[]{:S(2)}, u32[]{:S(2)}) collective-permute-start(bf16[6,1,1,32,512]{4,3,2,1,0:T(8,128)(2,1)S(1)} %get-tuple-element.33), channel_id=1, source_target_pairs={{0,2},{2,4},{4,6},{1,3},{3,5},{5,7},{8,10},{10,12},{12,14},{9,11},... | collective-permute-start | bytes 589832 | tf_op jit(solution)/shard_map/ppermute | solution.py:16
  89.4 136.6 %all-gather.5.cloned.1.call-start = ((), (), s32[]{:S(2)}) async-start(), calls=%async_computation.1 | async-start | bytes 2654208 | tf_op jit(solution)/shard_map/all_gather | solution.py:132
  91.4 7.7 %slice-start = ((s8[9437184]{0:T(1024)(128)(4,1)}), s8[4194304]{0:T(1024)(128)(4,1)S(1)}, s32[]{:S(2)}) async-start(s8[9437184]{0:T(1024)(128)(4,1)} %bitcast.192), calls=%async_computation.2 | async-start | bytes 8388608
  91.6 7.6 %slice-start.1 = ((s8[9437184]{0:T(1024)(128)(4,1)}), s8[4194304]{0:T(1024)(128)(4,1)S(1)}, s32[]{:S(2)}) async-start(s8[9437184]{0:T(1024)(128)(4,1)} %bitcast.192), calls=%async_computation.3 | async-start | bytes 8388608
  92.6 6.6 %slice-start.2 = ((s8[9437184]{0:T(1024)(128)(4,1)}), s8[1048576]{0:T(1024)(128)(4,1)S(1)}, s32[]{:S(2)}) async-start(s8[9437184]{0:T(1024)(128)(4,1)} %bitcast.192), calls=%async_computation.4 | async-start | bytes 2097152
  93.7 5.5 %copy-start.8 = (bf16[6,1,8,32,4608]{4,3,2,1,0:T(8,128)(2,1)}, bf16[6,1,8,32,4608]{4,3,2,1,0:T(8,128)(2,1)S(1)}, u32[]{:S(2)}) copy-start(bf16[6,1,8,32,4608]{4,3,2,1,0:T(8,128)(2,1)S(1)} %slice_dynamic-update-slice_fusion.4) | copy-start | bytes 42467332
  103.7 3.3 %copy-start.7 = (f32[2,2,2,2,144,512]{5,4,3,2,1,0:T(8,128)}, f32[2,2,2,2,144,512]{5,4,3,2,1,0:T(8,128)S(1)}, u32[]{:S(2)}) copy-start(f32[2,2,2,2,144,512]{5,4,3,2,1,0:T(8,128)S(1)} %fusion.4) | copy-start | bytes 14155780
  105.3 42.3 %collective-permute-start.11 = (f32[2,2,2,144,256]{4,3,2,1,0:T(8,128)}, f32[2,2,2,144,256]{4,3,2,1,0:T(8,128)}, u32[]{:S(2)}, u32[]{:S(2)}) collective-permute-start(f32[2,2,2,144,256]{4,3,2,1,0:T(8,128)} %select_bitcast_fusion.1), channel_id=1, source_target_pairs={{0,1},{1,0},{2,3},{3,2},{4,5},{5,4},{6,7},{7,6},{8,9},{9,8},{10,11... | collective-permute-start | bytes 3538952 | tf_op jit(solution)/shard_map/ppermute | solution.py:44
  106.9 6.3 %copy-start.10 = (f32[2,2,1,2,144,256]{5,4,3,2,1,0:T(8,128)}, f32[2,2,1,2,144,256]{5,4,3,2,1,0:T(8,128)S(1)}, u32[]{:S(2)}) copy-start(f32[2,2,1,2,144,256]{5,4,3,2,1,0:T(8,128)S(1)} %get-tuple-element.21) | copy-start | bytes 3538948
  106.9 6.3 %copy-start.12 = (f32[2,2,1,2,144,256]{5,4,3,2,1,0:T(8,128)}, f32[2,2,1,2,144,256]{5,4,3,2,1,0:T(8,128)S(1)}, u32[]{:S(2)}) copy-start(f32[2,2,1,2,144,256]{5,4,3,2,1,0:T(8,128)S(1)} %get-tuple-element.22) | copy-start | bytes 3538948
  108.3 43.1 %collective-permute-start.7 = (f32[2,2,2,144,256]{4,3,0,1,2:T(8,128)}, f32[2,2,2,144,256]{4,3,0,1,2:T(8,128)}, u32[]{:S(2)}, u32[]{:S(2)}) collective-permute-start(f32[2,2,2,144,256]{4,3,0,1,2:T(8,128)} %select_bitcast_fusion.2), channel_id=1, source_target_pairs={{0,4},{2,6},{4,0},{6,2},{1,5},{3,7},{5,1},{7,3},{8,12},{10,14},{12... | collective-permute-start | bytes 3538952 | tf_op jit(solution)/shard_map/ppermute | solution.py:44
  114.8 26.8 %copy-start.3 = (bf16[7,1,10,32,512]{4,3,2,1,0:T(8,128)(2,1)S(1)}, bf16[7,1,10,32,512]{4,3,2,1,0:T(8,128)(2,1)}, u32[]{:S(2)}) copy-start(bf16[7,1,10,32,512]{4,3,2,1,0:T(8,128)(2,1)} %copy-done.2) | copy-start | bytes 6881284
  143.2 8.2 %copy-start.11 = (f32[2,2,1,2,144,256]{5,4,3,2,1,0:T(8,128)S(1)}, f32[2,2,1,2,144,256]{5,4,3,2,1,0:T(8,128)}, u32[]{:S(2)}) copy-start(f32[2,2,1,2,144,256]{5,4,3,2,1,0:T(8,128)} %copy-done.10) | copy-start | bytes 3538948
  143.2 8.2 %copy-start.13 = (f32[2,2,1,2,144,256]{5,4,3,2,1,0:T(8,128)S(1)}, f32[2,2,1,2,144,256]{5,4,3,2,1,0:T(8,128)}, u32[]{:S(2)}) copy-start(f32[2,2,1,2,144,256]{5,4,3,2,1,0:T(8,128)} %copy-done.12) | copy-start | bytes 3538948
  149.8 14.7 %collective-permute-start.12 = (f32[2,2,144,256]{3,2,1,0:T(8,128)S(1)}, f32[2,2,144,256]{3,2,1,0:T(8,128)S(1)}, u32[]{:S(2)}, u32[]{:S(2)}) collective-permute-start(f32[2,2,144,256]{3,2,1,0:T(8,128)S(1)} %select_bitcast_fusion.3), channel_id=1, source_target_pairs={{0,4},{2,6},{4,0},{6,2},{1,5},{3,7},{5,1},{7,3},{8,12},{10,14},{12... | collective-permute-start | bytes 1769480 | tf_op jit(solution)/shard_map/ppermute | solution.py:44
  153.0 13.7 %collective-permute-start.8 = (f32[2,2,144,256]{3,2,0,1:T(8,128)S(1)}, f32[2,2,144,256]{3,2,0,1:T(8,128)S(1)}, u32[]{:S(2)}, u32[]{:S(2)}) collective-permute-start(f32[2,2,144,256]{3,2,0,1:T(8,128)S(1)} %select_bitcast_fusion.4), channel_id=1, source_target_pairs={{0,1},{1,0},{2,3},{3,2},{4,5},{5,4},{6,7},{7,6},{8,9},{9,8},{10,11... | collective-permute-start | bytes 1769480 | tf_op jit(solution)/shard_map/ppermute | solution.py:44
  164.7 11.6 %collective-permute-start.13 = (f32[2,144,256]{2,1,0:T(8,128)S(1)}, f32[2,144,256]{2,1,0:T(8,128)S(1)}, u32[]{:S(2)}, u32[]{:S(2)}) collective-permute-start(f32[2,144,256]{2,1,0:T(8,128)S(1)} %select_bitcast_fusion.5), channel_id=1, source_target_pairs={{0,8},{8,0},{16,24},{24,16},{1,9},{9,1},{17,25},{25,17},{2,10},{10... | collective-permute-start | bytes 884744 | tf_op jit(solution)/shard_map/ppermute | solution.py:44
  166.8 13.8 %collective-permute-start.9 = (f32[2,144,256]{2,1,0:T(8,128)S(1)}, f32[2,144,256]{2,1,0:T(8,128)S(1)}, u32[]{:S(2)}, u32[]{:S(2)}) collective-permute-start(f32[2,144,256]{2,1,0:T(8,128)S(1)} %select_bitcast_fusion.6), channel_id=1, source_target_pairs={{0,8},{8,0},{16,24},{24,16},{1,9},{9,1},{17,25},{25,17},{2,10},{10... | collective-permute-start | bytes 884744 | tf_op jit(solution)/shard_map/ppermute | solution.py:44
  176.3 10.0 %collective-permute-start.14 = (f32[144,256]{1,0:T(8,128)S(1)}, f32[144,256]{1,0:T(8,128)S(1)}, u32[]{:S(2)}, u32[]{:S(2)}) collective-permute-start(f32[144,256]{1,0:T(8,128)S(1)} %select_bitcast_fusion.7), channel_id=1, source_target_pairs={{0,16},{8,24},{16,0},{24,8},{1,17},{9,25},{17,1},{25,9},{2,18},{10... | collective-permute-start | bytes 442376 | tf_op jit(solution)/shard_map/ppermute | solution.py:44
  180.7 10.0 %collective-permute-start.10 = (f32[144,256]{1,0:T(8,128)S(1)}, f32[144,256]{1,0:T(8,128)S(1)}, u32[]{:S(2)}, u32[]{:S(2)}) collective-permute-start(f32[144,256]{1,0:T(8,128)S(1)} %select_bitcast_fusion.8), channel_id=1, source_target_pairs={{0,16},{8,24},{16,0},{24,8},{1,17},{9,25},{17,1},{25,9},{2,18},{10... | collective-permute-start | bytes 442376 | tf_op jit(solution)/shard_map/ppermute | solution.py:44
  217.3 1.1 copy-start.14
  217.4 1.3 copy-start.15
  217.4 1.5 copy-start.16
  217.4 1.7 copy-start.17
  217.4 1.9 copy-start.18
  219.3 1.7 copy-start.5
  225.9 8.0 %copy-start.1 = (f32[1152,512]{1,0:T(8,128)S(1)}, f32[1152,512]{1,0:T(8,128)}, u32[]{:S(2)}) copy-start(f32[1152,512]{1,0:T(8,128)} %param.9) | copy-start | bytes 7077892
Sparse Core Ops, SparseCore 0:
  89.5 58.5 all-gather.2
  191.6 29.0 all-gather.4

commit v7 on v4

v7 whole, which is shorter than its diff:
```python
import math

import jax
import jax.numpy as jnp
from jax import lax
from jax.sharding import Mesh, PartitionSpec as P
import numpy as np


def extended(x, sides, width):
    for axis, dim in sides:
        peers, length = (size_of(axis), x.shape[dim])
        up = [(i, (i + 1) % peers) for i in range(peers - 1)]
        down = [(j, i) for i, j in up]
        last = lax.slice_in_dim(x, length - width, length, axis=dim)
        first = lax.slice_in_dim(x, 0, width, axis=dim)
        before = lax.ppermute(last, axis, up)
        after = lax.ppermute(first, axis, down)
        x = jnp.concatenate([before, x, after], axis=dim)
    return x


def size_of(axes):
    return math.prod(lax.axis_size(name) for name in axes)


def doubling_gather(blocks, axis):
    peers = size_of(axis)
    me = lax.axis_index(axis)
    bit = 0
    while (1 << bit) < peers:
        pairs = [(j, j ^ (1 << bit)) for j in range(peers)]
        other = lax.ppermute(blocks, axis, pairs)
        low = (me // (1 << bit)) % 2 == 0
        blocks = jnp.where(low, jnp.concatenate([blocks, other]), jnp.concatenate([other, blocks]))
        bit += 1
    return blocks


def surrogate(potential):
    return 1.0 / (1.0 + (math.pi * (potential - 1.0)) ** 2)


def offsets_list():
    return [(row_shift, col_shift) for row_shift in (-1, 0, 1) for col_shift in (-1, 0, 1)]


def build(groups, core):
  dp_axes, space_axes, rep_axes = groups["dp"], groups["space"], groups["rep"]

  def on_device(frames, membrane, cotangent, master, moment, second):
      steps_count, samples, rows, cols, chans = frames.shape
      rest = space_axes + rep_axes
      rest_count = size_of(rest)
      data_count = size_of(dp_axes)
      shard_rows = master.shape[0]
      piece_rows = shard_rows // rest_count
      local = master.astype(jnp.bfloat16)
      piece = lax.dynamic_slice_in_dim(local, lax.axis_index(rest) * piece_rows, piece_rows, 0)
      over_dp = doubling_gather(piece[None], dp_axes)
      over_all = lax.all_gather(over_dp, rest, axis=0, tiled=False)
      weights = jnp.swapaxes(over_all, 0, 1).reshape(data_count * shard_rows, master.shape[1])
      stacked = jnp.concatenate([membrane[None], frames], axis=0)
      rimmed = extended(stacked, ((space_axes, 2),), 1)
      voltage = rimmed[0].astype(jnp.float32)
      potentials = []
      fired = []
      for position in range(steps_count):
          potential = 0.5 * voltage + rimmed[position + 1].astype(jnp.float32)
          spikes = jnp.where(potential >= 1.0, jnp.float32(1.0), jnp.float32(0.0))
          voltage = potential - spikes
          potentials.append(potential[:, 1:-1])
          fired.append(spikes)
      potential_all = jnp.stack(potentials)
      spike_all = jnp.stack(fired).astype(jnp.bfloat16)
      col_pad = ((0, 0), (0, 0), (0, 0), (1, 1), (0, 0))
      spike_pad = jnp.pad(spike_all, col_pad)
      grad_rim = extended(cotangent, ((space_axes, 2),), 1)
      grad_pad = jnp.pad(grad_rim, col_pad)
      spike_cols = jnp.concatenate(
          [spike_pad[:, :, 1 + a : 1 + a + rows, 1 + b : 1 + b + cols] for a, b in offsets_list()],
          axis=-1,
      ).reshape(-1, 9 * chans)
      grad_cols = jnp.concatenate(
          [grad_pad[:, :, 1 - a : 1 - a + rows, 1 - b : 1 - b + cols] for a, b in offsets_list()],
          axis=-1,
      ).reshape(-1, 9, chans)
      grad_flat = cotangent.reshape(-1, chans)
      weight_local = lax.dot_general(
          spike_cols, grad_flat, (((0,), (0,)), ((), ())), preferred_element_type=jnp.float32
      )
      dspikes = jnp.einsum(
          "nkd,kcd->nc",
          grad_cols,
          weights.reshape(9, chans, chans),
          preferred_element_type=jnp.float32,
      )
      dspikes = dspikes.reshape(steps_count, samples, rows, cols, chans)
      carried = jnp.zeros((samples, rows, cols, chans), jnp.float32)
      outs = [None] * steps_count
      for position in reversed(range(steps_count)):
          carried = dspikes[position] * surrogate(potential_all[position]) + 0.5 * carried
          outs[position] = (cotangent[position].astype(jnp.float32) + carried).astype(jnp.bfloat16)
      grad_input = jnp.stack(outs)
      membrane_grad = 0.5 * carried
      total_cells = samples * data_count * size_of(rep_axes) * rows * size_of(space_axes) * cols
      row_axes = dp_axes + rest
      if core is None:
          shard_part = lax.psum_scatter(weight_local, row_axes, scatter_dimension=0, tiled=True)
      else:
          place = row_axes.index(core)
          outer = size_of(row_axes[:place])
          blocks = weight_local.reshape(outer, 2, -1, chans)
          first = lax.axis_index(core) == 0
          low, high = blocks[:, 0], blocks[:, 1]
          sent = lax.ppermute(jnp.where(first, high, low), core, [(0, 1), (1, 0)])
          partial = (jnp.where(first, low, high) + sent).reshape(-1, chans)
          others = row_axes[:place] + row_axes[place + 1 :]
          shard_part = lax.psum_scatter(partial, others, scatter_dimension=0, tiled=True)
      summed = lax.all_gather(shard_part, rest, axis=0, tiled=True)
      weight_grad = summed * (1.0 / math.sqrt(steps_count * total_cells))
      new_moment = 0.9 * moment + 0.1 * weight_grad
      new_second = 0.95 * second + 0.05 * weight_grad * weight_grad
      update = new_moment / (jnp.sqrt(new_second) + 1e-08)
      return (grad_input, membrane_grad, weight_grad, new_moment, new_second, update)

  return on_device


def core_axis(mesh):
    for place, name in enumerate(mesh.axis_names):
        grid = np.moveaxis(mesh.devices, place, -1)
        if grid.shape[-1] % 2:
            continue
        pairs = grid.reshape(-1, 2)
        same = all(
            getattr(a, "coords", None) is not None
            and list(a.coords) == list(b.coords)
            and getattr(a, "core_on_chip", 0) != getattr(b, "core_on_chip", 0)
            for a, b in pairs
        )
        if same:
            return name
    return None


def solution(mesh):
    split = core_axis(mesh)
    groups = {name: (name,) for name in mesh.axis_names}
    core = None
    if split is not None:
        place = list(mesh.axis_names).index(split)
        shape = mesh.devices.shape
        names = list(mesh.axis_names)
        new_names = names[:place] + [split + "_outer", split + "_core"] + names[place + 1 :]
        new_shape = shape[:place] + (shape[place] // 2, 2) + shape[place + 1 :]
        mesh = Mesh(mesh.devices.reshape(new_shape), tuple(new_names))
        groups[split] = (split + "_outer", split + "_core")
        core = split + "_core"

    def spec(*dims):
        out = []
        for dim in dims:
            if dim is None:
                out.append(None)
            else:
                names = dim if isinstance(dim, tuple) else (dim,)
                out.append(tuple(part for name in names for part in groups[name]))
        return P(*out)

    return jax.shard_map(
        build(groups, core),
        mesh=mesh,
        in_specs=(
            spec(None, ("dp", "rep"), "space", None, None),
            spec(("dp", "rep"), "space", None, None),
            spec(None, ("dp", "rep"), "space", None, None),
            spec("dp", None),
            spec("dp", None),
            spec("dp", None),
        ),
        out_specs=(
            spec(None, ("dp", "rep"), "space", None, None),
            spec(("dp", "rep"), "space", None, None),
            spec("dp", None),
            spec("dp", None),
            spec("dp", None),
            spec("dp", None),
        ),
        check_vma=False,
    )
```

time: 226 us -> 291 us (1.29)
  waiting for transfers between devices: 79.6 us -> 117 us
  local copies, waits for them, and re-layouts: 46.7 us -> 68.5 us
    reduce_scatter x1, waiting for transfers between devices: 61.6 us -> 83.5 us  [on_device(): lax.psum_scatter(partial, others, scatter_dimension=0, tiled=True)]
    reshape x0 -> x1, local copies, waits for them, and re-layouts: none -> 18.6 us  [on_device(): spike_cols = jnp.concatenate([spike_pad[:, :, 1 + a:1 + a + rows, 1 + b:1...]
    ppermute x2, waiting for transfers between devices: 16.1 us -> 24.2 us  [doubling_gather(): other = lax.ppermute(blocks, axis, pairs)]
    ppermute x0 -> x1, waiting for transfers between devices: none -> 7.54 us  [on_device(): sent = lax.ppermute(jnp.where(first, high, low), core, [(0, 1), (1, 0)])]
    ppermute x0 -> x1, starting transfers between devices: none -> 4.46 us  [on_device(): sent = lax.ppermute(jnp.where(first, high, low), core, [(0, 1), (1, 0)])]
    unnamed x38 -> x40, local copies, waits for them, and re-layouts: 16.3 us -> 20.5 us
    add x0 -> x1, other arithmetic: none -> 3.96 us  [on_device(): partial = (jnp.where(first, low, high) + sent).reshape(-1, chans)]
  transfers between devices with their start and end apart: 9 -> 10, of which waited for: 5 -> 6; matrix products, arithmetic and copies ran while one was open for 38% -> 27% of each run, Pallas kernels for 0% -> 0%
where the time goes in v7:
time: 291 us; the launch traced here: 289 us
  waiting for transfers between devices  117 us (40%)
  local copies, waits for them, and re-layouts  68.5 us (24%)
  matrix products  36.5 us (13%)
  other arithmetic  33.1 us (11%)
  starting transfers between devices  17.8 us (6%)
  between operations  15.8 us (5%)
    reduce_scatter x1, waiting for transfers between devices, on_device(): lax.psum_scatter(partial, others, scatter_dimension=0, tiled=True)  83.5 us
    reshape x1, local copies, waits for them, and re-layouts, on_device(): grad_cols = jnp.concatenate([grad_pad[:, :, 1 - a:1 - a + rows, 1 - b:1 -...  26.9 us
    dot_general x1, matrix products, on_device(): jnp.einsum('nkd,kcd->nc', grad_cols, weights.reshape(9, chans, chans), pr...  25.8 us
    ppermute x2, waiting for transfers between devices, doubling_gather(): other = lax.ppermute(blocks, axis, pairs)  24.2 us
    unnamed x40, local copies, waits for them, and re-layouts  20.5 us
    reshape x1, local copies, waits for them, and re-layouts, on_device(): spike_cols = jnp.concatenate([spike_pad[:, :, 1 + a:1 + a + rows, 1 + b:1...  18.6 us
    dot_general x1, matrix products, on_device(): lax.dot_general(spike_cols, grad_flat, (((0,), (0,)), ((), ())), preferre...  10.7 us
    unnamed x12, other arithmetic  8.51 us
  transfers between devices with their start and end apart: 10, of which 6 were waited for; matrix products, arithmetic and copies ran while one was open for 27% of the time, Pallas kernels for 0%

profile of v7, /device:TPU:0, one launch (start us, length us, event | category | flops | bytes accessed | tf_op | source)
XLA Modules:
  0.0 289.2 jit_solution(15744493309537152520)
XLA Ops:
  8.1 1.2 pad_maximum_fusion.4
  9.3 1.3 collective-permute-start.5
  10.6 3.0 %collective-permute-start.4 = (bf16[7,1,1,32,512]{4,3,2,1,0:T(8,128)(2,1)S(1)}, bf16[7,1,1,32,512]{4,3,2,1,0:T(8,128)(2,1)S(1)}, u32[]{:S(2)}, u32[]{:S(2)}) collective-permute-start(bf16[7,1,1,32,512]{4,3,2,1,0:T(8,128)(2,1)S(1)} %get-tuple-element.29), channel_id=1, source_target_pairs={{0,2},{2,4},{4,6},{1,3},{3,5},{5,7},{8,10},{10,12},{12,14},{9,11},... | collective-permute-start | bytes 688136 | tf_op jit(solution)/shard_map/ppermute | solution.py:17
  13.7 1.1 collective-permute-done.4
  14.8 1.8 pad_maximum_fusion
  16.7 0.3 fusion.70
  17.0 0.4 fusion.71
  17.4 0.5 fusion.72
  17.9 0.2 fusion.73
  18.1 1.2 fusion.68
  19.3 0.5 fusion.13
  19.8 0.2 slice_dynamic-update-slice_fusion.2
  20.0 0.7 fusion.14
  20.7 0.7 fusion.15
  21.4 0.2 slice_dynamic-update-slice_fusion.1
  21.6 0.7 fusion.16
  22.3 0.7 fusion.17
  23.1 0.2 slice_dynamic-update-slice_fusion
  23.3 0.7 fusion.18
  24.0 5.0 %copy-done.6 = bf16[6,1,8,32,4608]{4,3,2,1,0:T(8,128)(2,1)} copy-done((bf16[6,1,8,32,4608]{4,3,2,1,0:T(8,128)(2,1)}, bf16[6,1,8,32,4608]{4,3,2,1,0:T(8,128)(2,1)S(1)}, u32[]{:S(2)}) %copy-start.6) | copy-done | bytes 14155800
  29.0 18.6 %copy.18 = bf16[1536,4608]{0,1:T(8,128)(2,1)} copy(bf16[1536,4608]{1,0:T(8,128)(2,1)} %bitcast.120) | data formatting | bytes 28311552 | tf_op jit(solution)/shard_map/reshape | solution.py:83
  47.7 10.7 %fusion.96 = f32[8,2,288,512]{3,2,1,0:T(8,128)S(1)} fusion(bf16[8,2,288,1536]{3,2,1,0:T(8,128)(2,1)} %bitcast.121, bf16[1536,512,1,1]{1,0,3,2:T(8,128)(2,1)} %bitcast.118), kind=kOutput, calls=%fused_computation.154 | convolution fusion | flops 7247757312 | bytes 25165824 | tf_op jit(solution)/shard_map/dot_general | solution.py:89
  58.4 1.2 select_bitcast_fusion
  59.6 4.5 %collective-permute-start.6 = (f32[8,288,512]{2,1,0:T(8,128)S(1)}, f32[8,288,512]{2,1,0:T(8,128)S(1)}, u32[]{:S(2)}, u32[]{:S(2)}) collective-permute-start(f32[8,288,512]{2,1,0:T(8,128)S(1)} %select_bitcast_fusion), channel_id=1, source_target_pairs={{0,2},{2,0},{1,3},{3,1},{4,6},{6,4},{5,7},{7,5},{8,10},{10,8},{9,1... | collective-permute-start | bytes 14155784 | tf_op jit(solution)/shard_map/ppermute | solution.py:116
  64.0 7.5 %collective-permute-done.6 = f32[8,288,512]{2,1,0:T(8,128)S(1)} collective-permute-done((f32[8,288,512]{2,1,0:T(8,128)S(1)}, f32[8,288,512]{2,1,0:T(8,128)S(1)}, u32[]{:S(2)}, u32[]{:S(2)}) %collective-permute-start.6) | collective-permute-done | bytes 4718624 | tf_op jit(solution)/shard_map/ppermute | solution.py:116
  71.6 4.0 %fusion.4 = f32[8,288,512]{2,1,0:T(8,128)} fusion(f32[8,288,512]{2,1,0:T(8,128)S(1)} %collective-permute-done.6, f32[8,2,288,512]{3,2,1,0:T(8,128)S(1)} %fusion.96, pred[]{:T(512)S(6)} %eq.14), kind=kLoop, calls=%fused_computation.7 | loop fusion | flops 2359296 | bytes 18874368 | tf_op jit(solution)/shard_map/add | solution.py:117
  75.6 0.2 all-gather.3.cloned.1.call-start
  75.9 1.7 collective-permute-start.2
  77.5 4.5 %collective-permute-done.2 = bf16[1,144,512]{2,1,0:T(8,128)(2,1)S(1)} collective-permute-done((bf16[1,144,512]{2,1,0:T(8,128)(2,1)S(1)}, bf16[1,144,512]{2,1,0:T(8,128)(2,1)S(1)}, u32[]{:S(2)}, u32[]{:S(2)}) %collective-permute-start.2) | collective-permute-done | bytes 147488 | tf_op jit(solution)/shard_map/ppermute | solution.py:33
  82.1 2.7 collective-permute-start.3
  84.8 19.7 %collective-permute-done.3 = bf16[2,144,512]{2,1,0:T(8,128)(2,1)S(1)} collective-permute-done((bf16[2,144,512]{2,1,0:T(8,128)(2,1)S(1)}, bf16[2,144,512]{2,1,0:T(8,128)(2,1)S(1)}, u32[]{:S(2)}, u32[]{:S(2)}) %collective-permute-start.3) | collective-permute-done | bytes 294944 | tf_op jit(solution)/shard_map/ppermute | solution.py:33
  104.5 0.9 maximum_select_fusion
  105.5 1.3 collective-permute-start.1
  106.8 3.0 %collective-permute-start = (bf16[6,1,1,32,512]{4,3,2,1,0:T(8,128)(2,1)S(1)}, bf16[6,1,1,32,512]{4,3,2,1,0:T(8,128)(2,1)S(1)}, u32[]{:S(2)}, u32[]{:S(2)}) collective-permute-start(bf16[6,1,1,32,512]{4,3,2,1,0:T(8,128)(2,1)S(1)} %get-tuple-element.31), channel_id=1, source_target_pairs={{0,2},{2,4},{4,6},{1,3},{3,5},{5,7},{8,10},{10,12},{12,14},{9,11},... | collective-permute-start | bytes 589832 | tf_op jit(solution)/shard_map/ppermute | solution.py:17
  109.9 1.0 collective-permute-done
  110.9 1.3 fusion.12
  112.2 1.7 slice_dynamic-update-slice_fusion.8
  113.9 1.4 fusion.20
  115.3 1.4 slice_dynamic-update-slice_fusion.7
  116.7 2.0 slice_dynamic-update-slice_fusion.6
  118.6 1.4 constant_dynamic-update-slice_fusion
  120.0 1.5 slice_dynamic-update-slice_fusion.5
  121.5 2.0 slice_dynamic-update-slice_fusion.4
  123.5 1.4 fusion.19
  124.9 1.4 slice_dynamic-update-slice_fusion.3
  126.3 26.9 %reshape.628 = bf16[1536,9,512]{2,1,0:T(8,128)(2,1)} reshape(bf16[6,1,8,32,4608]{4,3,2,1,0:T(8,128)(2,1)} %slice_dynamic-update-slice_fusion.3) | data formatting | bytes 28311552 | tf_op jit(solution)/shard_map/reshape | solution.py:87
  153.2 0.9 fusion.67
  154.2 1.6 fusion.24
  155.8 83.5 %reduce-scatter.2.cloned.1.call-done = f32[144,512]{1,0:T(8,128)} async-done(((f32[2304,512]{1,0:T(8,128)}), f32[144,512]{1,0:T(8,128)}) %reduce-scatter.2.cloned.1.call-update) | async-done | bytes 294928 | tf_op jit(solution)/shard_map/reduce_scatter | solution.py:119
  239.3 25.8 %fusion.5 = f32[1536,512]{1,0:T(8,128)S(1)} fusion(bf16[9,512,512]{2,1,0:T(8,128)(2,1)} %bitcast.133, bf16[1536,9,512]{2,1,0:T(8,128)(2,1)} %reshape.628), kind=kOutput, calls=%fused_computation.9 | convolution fusion | flops 7247757312 | bytes 22020096 | tf_op jit(solution)/shard_map/nkd,kcd->nc/dot_general | solution.py:92
  265.2 0.3 fusion.94
  265.5 0.7 copy-done.7
  266.2 0.2 copy-done.8
  266.4 0.2 copy-done.9
  266.7 0.2 copy-done.10
  266.9 0.2 copy-done.11
  267.1 1.7 broadcast_multiply_fusion.1
  268.8 0.8 fusion.75
  269.6 0.9 fusion.77
  270.5 0.8 fusion.79
  271.3 0.8 fusion.81
  272.0 0.9 fusion.83
  272.9 0.8 fusion.85
  273.7 8.0 %add_divide_fusion = (f32[1152,512]{1,0:T(8,128)}, f32[1152,512]{1,0:T(8,128)}, f32[1152,512]{1,0:T(8,128)}, f32[1152,512]{1,0:T(8,128)}) fusion(f32[1152,512]{1,0:T(8,128)} %all-gather.5.cloned.1.call-done, f32[1152,512]{1,0:T(8,128)} %param.11, f32[1152,512]{1,0:T(8,128)} %param.10), kind=kLoop, calls=%fused_computation.15 | loop fusion | flops 5898240 | bytes 16515072 | tf_op jit(solution)/shard_map/div | solution.py:124
  (34 shorter events, 0.5 us)
Async XLA Ops:
  8.0 67.8 %copy-start = (f32[1152,512]{1,0:T(8,128)S(1)}, f32[1152,512]{1,0:T(8,128)}, u32[]{:S(2)}) copy-start(f32[1152,512]{1,0:T(8,128)} %param.9) | copy-start | bytes 7077892
  8.0 6.7 %copy-start.12 = (bf16[1,8,32,512]{3,2,1,0:T(8,128)(2,1)S(1)}, bf16[1,8,32,512]{3,2,1,0:T(8,128)(2,1)}, u32[]{:S(2)}) copy-start(bf16[1,8,32,512]{3,2,1,0:T(8,128)(2,1)} %param.7) | copy-start | bytes 786436
  8.0 231.2 %reduce-scatter.2.cloned.1.call-start = ((), (), s32[]{:S(2)}) async-start(), calls=%async_computation.2 | async-start | bytes 5013504 | tf_op jit(solution)/shard_map/reduce_scatter | solution.py:119
  9.3 4.4 %collective-permute-start.5 = (bf16[7,1,1,32,512]{4,3,2,1,0:T(8,128)(2,1)S(1)}, bf16[7,1,1,32,512]{4,3,2,1,0:T(8,128)(2,1)S(1)}, u32[]{:S(2)}, u32[]{:S(2)}) collective-permute-start(bf16[7,1,1,32,512]{4,3,2,1,0:T(8,128)(2,1)S(1)} %get-tuple-element.30), channel_id=1, source_target_pairs={{2,0},{4,2},{6,4},{3,1},{5,3},{7,5},{10,8},{12,10},{14,12},{11,9},... | collective-permute-start | bytes 688136 | tf_op jit(solution)/shard_map/ppermute | solution.py:18
  10.6 4.1 %collective-permute-start.4 = (bf16[7,1,1,32,512]{4,3,2,1,0:T(8,128)(2,1)S(1)}, bf16[7,1,1,32,512]{4,3,2,1,0:T(8,128)(2,1)S(1)}, u32[]{:S(2)}, u32[]{:S(2)}) collective-permute-start(bf16[7,1,1,32,512]{4,3,2,1,0:T(8,128)(2,1)S(1)} %get-tuple-element.29), channel_id=1, source_target_pairs={{0,2},{2,4},{4,6},{1,3},{3,5},{5,7},{8,10},{10,12},{12,14},{9,11},... | collective-permute-start | bytes 688136 | tf_op jit(solution)/shard_map/ppermute | solution.py:17
  16.5 1.6 copy-start.2
  24.0 5.0 %copy-start.6 = (bf16[6,1,8,32,4608]{4,3,2,1,0:T(8,128)(2,1)}, bf16[6,1,8,32,4608]{4,3,2,1,0:T(8,128)(2,1)S(1)}, u32[]{:S(2)}) copy-start(bf16[6,1,8,32,4608]{4,3,2,1,0:T(8,128)(2,1)S(1)} %fusion.18) | copy-start | bytes 42467332
  59.6 12.0 %collective-permute-start.6 = (f32[8,288,512]{2,1,0:T(8,128)S(1)}, f32[8,288,512]{2,1,0:T(8,128)S(1)}, u32[]{:S(2)}, u32[]{:S(2)}) collective-permute-start(f32[8,288,512]{2,1,0:T(8,128)S(1)} %select_bitcast_fusion), channel_id=1, source_target_pairs={{0,2},{2,0},{1,3},{3,1},{4,6},{6,4},{5,7},{7,5},{8,10},{10,8},{9,1... | collective-permute-start | bytes 14155784 | tf_op jit(solution)/shard_map/ppermute | solution.py:116
  75.6 163.8 %all-gather.3.cloned.1.call-start = ((), (), s32[]{:S(2)}) async-start(), calls=%async_computation.1 | async-start | bytes 5308416 | tf_op jit(solution)/shard_map/all_gather | solution.py:61
  75.8 29.6 %copy-start.4 = (bf16[6,1,8,32,512]{4,3,2,1,0:T(8,128)(2,1)S(1)}, bf16[6,1,8,32,512]{4,3,2,1,0:T(8,128)(2,1)}, u32[]{:S(2)}) copy-start(bf16[6,1,8,32,512]{4,3,2,1,0:T(8,128)(2,1)} %param.8) | copy-start | bytes 4718596
  75.9 6.2 %collective-permute-start.2 = (bf16[1,144,512]{2,1,0:T(8,128)(2,1)S(1)}, bf16[1,144,512]{2,1,0:T(8,128)(2,1)S(1)}, u32[]{:S(2)}, u32[]{:S(2)}) collective-permute-start(bf16[1,144,512]{2,1,0:T(8,128)(2,1)S(1)} %fusion.86), channel_id=1, source_target_pairs={{0,8},{8,0},{16,24},{24,16},{1,9},{9,1},{17,25},{25,17},{2,10},{10... | collective-permute-start | bytes 442376 | tf_op jit(solution)/shard_map/ppermute | solution.py:33
  82.1 22.4 %collective-permute-start.3 = (bf16[2,144,512]{2,1,0:T(8,128)(2,1)S(1)}, bf16[2,144,512]{2,1,0:T(8,128)(2,1)S(1)}, u32[]{:S(2)}, u32[]{:S(2)}) collective-permute-start(bf16[2,144,512]{2,1,0:T(8,128)(2,1)S(1)} %maximum_select_fusion.1), channel_id=1, source_target_pairs={{0,16},{8,24},{16,0},{24,8},{1,17},{9,25},{17,1},{25,9},{2,18},{10... | collective-permute-start | bytes 884744 | tf_op jit(solution)/shard_map/ppermute | solution.py:33
  105.4 168.3 %all-gather.5.cloned.1.call-start = ((), (), s32[]{:S(2)}) async-start(), calls=%async_computation.3 | async-start | bytes 2654208 | tf_op jit(solution)/shard_map/all_gather | solution.py:120
  105.5 4.4 %collective-permute-start.1 = (bf16[6,1,1,32,512]{4,3,2,1,0:T(8,128)(2,1)S(1)}, bf16[6,1,1,32,512]{4,3,2,1,0:T(8,128)(2,1)S(1)}, u32[]{:S(2)}, u32[]{:S(2)}) collective-permute-start(bf16[6,1,1,32,512]{4,3,2,1,0:T(8,128)(2,1)S(1)} %get-tuple-element.32), channel_id=1, source_target_pairs={{2,0},{4,2},{6,4},{3,1},{5,3},{7,5},{10,8},{12,10},{14,12},{11,9},... | collective-permute-start | bytes 589832 | tf_op jit(solution)/shard_map/ppermute | solution.py:18
  106.8 4.1 %collective-permute-start = (bf16[6,1,1,32,512]{4,3,2,1,0:T(8,128)(2,1)S(1)}, bf16[6,1,1,32,512]{4,3,2,1,0:T(8,128)(2,1)S(1)}, u32[]{:S(2)}, u32[]{:S(2)}) collective-permute-start(bf16[6,1,1,32,512]{4,3,2,1,0:T(8,128)(2,1)S(1)} %get-tuple-element.31), channel_id=1, source_target_pairs={{0,2},{2,4},{4,6},{1,3},{3,5},{5,7},{8,10},{10,12},{12,14},{9,11},... | collective-permute-start | bytes 589832 | tf_op jit(solution)/shard_map/ppermute | solution.py:17
  126.3 26.9 %copy-start.3 = (bf16[7,1,10,32,512]{4,3,2,1,0:T(8,128)(2,1)S(1)}, bf16[7,1,10,32,512]{4,3,2,1,0:T(8,128)(2,1)}, u32[]{:S(2)}) copy-start(bf16[7,1,10,32,512]{4,3,2,1,0:T(8,128)(2,1)} %copy-done.2) | copy-start | bytes 6881284
  265.2 1.1 copy-start.7
  265.2 1.3 copy-start.8
  265.2 1.5 copy-start.9
  265.2 1.7 copy-start.10
  265.2 1.9 copy-start.11
  267.1 1.7 copy-start.5
  273.7 8.0 %copy-start.1 = (f32[1152,512]{1,0:T(8,128)S(1)}, f32[1152,512]{1,0:T(8,128)}, u32[]{:S(2)}) copy-start(f32[1152,512]{1,0:T(8,128)} %param.9) | copy-start | bytes 7077892
Sparse Core Ops, SparseCore 0:
  75.7 163.5 reduce-scatter.1
Sparse Core Ops, SparseCore 1:
  105.5 43.5 all-gather.2
  239.4 27.9 all-gather.4

commit v8 on v7

--- a/solution.py
+++ b/solution.py
@@ -110,7 +110,7 @@
       else:
           place = row_axes.index(core)
           outer = size_of(row_axes[:place])
-          blocks = weight_local.reshape(outer, 2, -1, chans)
+          blocks = lax.optimization_barrier(weight_local).reshape(outer, 2, -1, chans)
           first = lax.axis_index(core) == 0
           low, high = blocks[:, 0], blocks[:, 1]
           sent = lax.ppermute(jnp.where(first, high, low), core, [(0, 1), (1, 0)])

time: 291 us -> 274 us (0.942)
  local copies, waits for them, and re-layouts: 68.5 us -> 57.1 us
  waiting for transfers between devices: 117 us -> 109 us
  other arithmetic: 33.1 us -> 37.6 us
    reshape x1 -> x0, local copies, waits for them, and re-layouts: 18.6 us -> none  [on_device(): spike_cols = jnp.concatenate([spike_pad[:, :, 1 + a:1 + a + rows, 1 + b:1...]
    reduce_scatter x1, waiting for transfers between devices: 83.5 us -> 74.7 us  [on_device(): lax.psum_scatter(partial, others, scatter_dimension=0, tiled=True)]
    unnamed x40 -> x36, local copies, waits for them, and re-layouts: 20.5 us -> 25.6 us
  transfers between devices with their start and end apart: 10 -> 10, of which waited for: 6 -> 6; matrix products, arithmetic and copies ran while one was open for 27% -> 31% of each run, Pallas kernels for 0% -> 0%
where the time goes in v8:
time: 274 us; the launch traced here: 273 us
  waiting for transfers between devices  109 us (40%)
  local copies, waits for them, and re-layouts  57.1 us (21%)
  other arithmetic  37.6 us (14%)
  matrix products  36.3 us (13%)
  starting transfers between devices  17.6 us (6%)
  between operations  15.8 us (6%)
    reduce_scatter x1, waiting for transfers between devices, on_device(): lax.psum_scatter(partial, others, scatter_dimension=0, tiled=True)  74.7 us
    reshape x1, local copies, waits for them, and re-layouts, on_device(): grad_cols = jnp.concatenate([grad_pad[:, :, 1 - a:1 - a + rows, 1 - b:1 -...  26.7 us
    dot_general x1, matrix products, on_device(): jnp.einsum('nkd,kcd->nc', grad_cols, weights.reshape(9, chans, chans), pr...  25.9 us
    unnamed x36, local copies, waits for them, and re-layouts  25.6 us
    ppermute x2, waiting for transfers between devices, doubling_gather(): other = lax.ppermute(blocks, axis, pairs)  24.3 us
    dot_general x1, matrix products, on_device(): lax.dot_general(spike_cols, grad_flat, (((0,), (0,)), ((), ())), preferre...  10.4 us
    unnamed x12, other arithmetic  8.43 us
    div x1, other arithmetic, on_device(): update = new_moment / (jnp.sqrt(new_second) + 1e-08)  7.88 us
  transfers between devices with their start and end apart: 10, of which 6 were waited for; matrix products, arithmetic and copies ran while one was open for 31% of the time, Pallas kernels for 0%

profile of v8, /device:TPU:0, one launch (start us, length us, event | category | flops | bytes accessed | tf_op | source)
XLA Modules:
  0.0 272.9 jit_solution(6221478958135564883)
XLA Ops:
  8.1 1.2 pad_maximum_fusion.4
  9.3 1.3 collective-permute-start.5
  10.6 3.0 %collective-permute-start.4 = (bf16[7,1,1,32,512]{4,3,2,1,0:T(8,128)(2,1)S(1)}, bf16[7,1,1,32,512]{4,3,2,1,0:T(8,128)(2,1)S(1)}, u32[]{:S(2)}, u32[]{:S(2)}) collective-permute-start(bf16[7,1,1,32,512]{4,3,2,1,0:T(8,128)(2,1)S(1)} %get-tuple-element.27), channel_id=1, source_target_pairs={{0,2},{2,4},{4,6},{1,3},{3,5},{5,7},{8,10},{10,12},{12,14},{9,11},... | collective-permute-start | bytes 688136 | tf_op jit(solution)/shard_map/ppermute | solution.py:17
  13.7 1.1 collective-permute-done.4
  14.8 1.8 pad_maximum_fusion
  16.5 0.1 fusion.78
  16.7 0.3 fusion.80
  17.0 0.4 fusion.82
  17.4 0.5 fusion.84
  17.9 0.2 fusion.85
  18.1 0.3 fusion.76
  18.4 1.7 fusion.18
  20.1 1.4 slice_dynamic-update-slice_fusion.2
  21.5 2.0 fusion.19
  23.5 2.1 fusion.20
  25.6 1.5 slice_dynamic-update-slice_fusion.1
  27.1 2.0 fusion.21
  29.1 2.1 fusion.22
  31.1 1.4 slice_dynamic-update-slice_fusion
  32.5 2.0 fusion.23
  34.5 10.4 %fusion.4 = f32[4608,512]{1,0:T(8,128)S(1)} fusion(bf16[6,1,8,32,4608]{4,3,2,0,1:T(8,128)(2,1)} %fusion.23, bf16[6,1,8,32,512]{4,3,2,1,0:T(8,128)(2,1)S(1)} %copy-done.2), kind=kOutput, calls=%fused_computation.4 | convolution fusion | flops 7247757312 | bytes 25165824 | tf_op jit(solution)/shard_map/dot_general | solution.py:89
  44.9 1.2 select_bitcast_fusion
  46.1 4.5 %collective-permute-start.6 = (f32[8,288,512]{2,1,0:T(8,128)S(1)}, f32[8,288,512]{2,1,0:T(8,128)S(1)}, u32[]{:S(2)}, u32[]{:S(2)}) collective-permute-start(f32[8,288,512]{2,1,0:T(8,128)S(1)} %select_bitcast_fusion), channel_id=1, source_target_pairs={{0,2},{2,0},{1,3},{3,1},{4,6},{6,4},{5,7},{7,5},{8,10},{10,8},{9,1... | collective-permute-start | bytes 14155784 | tf_op jit(solution)/shard_map/ppermute | solution.py:116
  50.5 7.5 %collective-permute-done.6 = f32[8,288,512]{2,1,0:T(8,128)S(1)} collective-permute-done((f32[8,288,512]{2,1,0:T(8,128)S(1)}, f32[8,288,512]{2,1,0:T(8,128)S(1)}, u32[]{:S(2)}, u32[]{:S(2)}) %collective-permute-start.6) | collective-permute-done | bytes 4718624 | tf_op jit(solution)/shard_map/ppermute | solution.py:116
  58.1 4.0 %fusion.9 = f32[8,288,512]{2,1,0:T(8,128)} fusion(f32[8,288,512]{2,1,0:T(8,128)S(1)} %collective-permute-done.6, f32[8,2,288,512]{3,2,1,0:T(8,128)S(1)} %bitcast.176, pred[]{:T(512)S(6)} %eq.14), kind=kLoop, calls=%fused_computation.10 | loop fusion | flops 2359296 | bytes 18874368 | tf_op jit(solution)/shard_map/add | solution.py:117
  62.2 1.7 collective-permute-start.2
  63.8 4.5 %collective-permute-done.2 = bf16[1,144,512]{2,1,0:T(8,128)(2,1)S(1)} collective-permute-done((bf16[1,144,512]{2,1,0:T(8,128)(2,1)S(1)}, bf16[1,144,512]{2,1,0:T(8,128)(2,1)S(1)}, u32[]{:S(2)}, u32[]{:S(2)}) %collective-permute-start.2) | collective-permute-done | bytes 147488 | tf_op jit(solution)/shard_map/ppermute | solution.py:33
  68.4 2.7 collective-permute-start.3
  71.1 19.7 %collective-permute-done.3 = bf16[2,144,512]{2,1,0:T(8,128)(2,1)S(1)} collective-permute-done((bf16[2,144,512]{2,1,0:T(8,128)(2,1)S(1)}, bf16[2,144,512]{2,1,0:T(8,128)(2,1)S(1)}, u32[]{:S(2)}, u32[]{:S(2)}) %collective-permute-start.3) | collective-permute-done | bytes 294944 | tf_op jit(solution)/shard_map/ppermute | solution.py:33
  90.8 0.9 maximum_select_fusion
  91.8 1.1 fusion.107
  92.9 1.3 collective-permute-start.1
  94.2 3.0 %collective-permute-start = (bf16[6,1,1,32,512]{4,3,2,1,0:T(8,128)(2,1)S(1)}, bf16[6,1,1,32,512]{4,3,2,1,0:T(8,128)(2,1)S(1)}, u32[]{:S(2)}, u32[]{:S(2)}) collective-permute-start(bf16[6,1,1,32,512]{4,3,2,1,0:T(8,128)(2,1)S(1)} %get-tuple-element.29), channel_id=1, source_target_pairs={{0,2},{2,4},{4,6},{1,3},{3,5},{5,7},{8,10},{10,12},{12,14},{9,11},... | collective-permute-start | bytes 589832 | tf_op jit(solution)/shard_map/ppermute | solution.py:17
  97.2 1.0 collective-permute-done
  98.3 2.3 fusion.17
  100.6 1.7 slice_dynamic-update-slice_fusion.8
  102.3 1.4 fusion.25
  103.7 1.5 slice_dynamic-update-slice_fusion.7
  105.1 2.0 slice_dynamic-update-slice_fusion.6
  107.1 1.5 constant_dynamic-update-slice_fusion
  108.6 1.4 slice_dynamic-update-slice_fusion.5
  110.0 2.0 slice_dynamic-update-slice_fusion.4
  112.0 1.4 fusion.24
  113.3 1.4 slice_dynamic-update-slice_fusion.3
  114.8 26.7 %reshape.631 = bf16[1536,9,512]{2,1,0:T(8,128)(2,1)} reshape(bf16[6,1,8,32,4608]{4,3,2,1,0:T(8,128)(2,1)} %slice_dynamic-update-slice_fusion.3) | data formatting | bytes 28311552 | tf_op jit(solution)/shard_map/reshape | solution.py:87
  141.4 2.0 fusion.75
  143.5 1.9 convert_bitcast_fusion.1
  145.4 3.1 %fusion.30 = (f32[1,10,32,512]{3,2,1,0:T(8,128)S(1)}, f32[1,10,32,512]{3,2,1,0:T(8,128)}, f32[1,10,32,512]{3,2,1,0:T(8,128)}, f32[1,10,32,512]{3,2,1,0:T(8,128)}) fusion(bf16[7,1,10,32,512]{4,3,2,1,0:T(8,128)(2,1)} %copy-done.1), kind=kLoop, calls=%fused_computation.72 | loop fusion | flops 4587520 | bytes 4587520 | tf_op jit(solution)/shard_map/add | solution.py:69
  148.5 74.7 %reduce-scatter.2.cloned.1.call-done = f32[144,512]{1,0:T(8,128)} async-done(((f32[2304,512]{1,0:T(8,128)}), f32[144,512]{1,0:T(8,128)}) %reduce-scatter.2.cloned.1.call-update) | async-done | bytes 294928 | tf_op jit(solution)/shard_map/reduce_scatter | solution.py:119
  223.2 25.9 %fusion.10 = f32[1536,512]{1,0:T(8,128)S(1)} fusion(bf16[9,512,512]{2,1,0:T(8,128)(2,1)} %bitcast.189, bf16[1536,9,512]{2,1,0:T(8,128)(2,1)} %reshape.631), kind=kOutput, calls=%fused_computation.12 | convolution fusion | flops 7247757312 | bytes 22020096 | tf_op jit(solution)/shard_map/nkd,kcd->nc/dot_general | solution.py:92
  249.1 0.3 fusion.106
  249.4 0.7 copy-done.5
  250.1 0.2 copy-done.6
  250.3 0.2 copy-done.7
  250.5 0.2 copy-done.8
  250.7 0.2 copy-done.9
  251.0 1.7 broadcast_multiply_fusion.1
  252.7 0.8 fusion.87
  253.5 0.9 fusion.89
  254.4 0.8 fusion.91
  255.1 0.8 fusion.93
  255.9 0.9 fusion.95
  256.8 0.8 fusion.97
  257.6 7.9 %add_divide_fusion = (f32[1152,512]{1,0:T(8,128)}, f32[1152,512]{1,0:T(8,128)}, f32[1152,512]{1,0:T(8,128)}, f32[1152,512]{1,0:T(8,128)}) fusion(f32[1152,512]{1,0:T(8,128)} %all-gather.5.cloned.1.call-done, f32[1152,512]{1,0:T(8,128)} %param.11, f32[1152,512]{1,0:T(8,128)} %param.10), kind=kLoop, calls=%fused_computation.18 | loop fusion | flops 5898240 | bytes 16515072 | tf_op jit(solution)/shard_map/div | solution.py:124
  (30 shorter events, 0.3 us)
Async XLA Ops:
  8.0 54.1 %copy-start = (f32[1152,512]{1,0:T(8,128)S(1)}, f32[1152,512]{1,0:T(8,128)}, u32[]{:S(2)}) copy-start(f32[1152,512]{1,0:T(8,128)} %param.9) | copy-start | bytes 7077892
  8.0 6.7 %copy-start.10 = (bf16[1,8,32,512]{3,2,1,0:T(8,128)(2,1)S(1)}, bf16[1,8,32,512]{3,2,1,0:T(8,128)(2,1)}, u32[]{:S(2)}) copy-start(bf16[1,8,32,512]{3,2,1,0:T(8,128)(2,1)} %param.7) | copy-start | bytes 786436
  8.0 215.1 %reduce-scatter.2.cloned.1.call-start = ((), (), s32[]{:S(2)}) async-start(), calls=%async_computation.2 | async-start | bytes 5013504 | tf_op jit(solution)/shard_map/reduce_scatter | solution.py:119
  9.3 4.4 %collective-permute-start.5 = (bf16[7,1,1,32,512]{4,3,2,1,0:T(8,128)(2,1)S(1)}, bf16[7,1,1,32,512]{4,3,2,1,0:T(8,128)(2,1)S(1)}, u32[]{:S(2)}, u32[]{:S(2)}) collective-permute-start(bf16[7,1,1,32,512]{4,3,2,1,0:T(8,128)(2,1)S(1)} %get-tuple-element.28), channel_id=1, source_target_pairs={{2,0},{4,2},{6,4},{3,1},{5,3},{7,5},{10,8},{12,10},{14,12},{11,9},... | collective-permute-start | bytes 688136 | tf_op jit(solution)/shard_map/ppermute | solution.py:18
  10.6 4.1 %collective-permute-start.4 = (bf16[7,1,1,32,512]{4,3,2,1,0:T(8,128)(2,1)S(1)}, bf16[7,1,1,32,512]{4,3,2,1,0:T(8,128)(2,1)S(1)}, u32[]{:S(2)}, u32[]{:S(2)}) collective-permute-start(bf16[7,1,1,32,512]{4,3,2,1,0:T(8,128)(2,1)S(1)} %get-tuple-element.27), channel_id=1, source_target_pairs={{0,2},{2,4},{4,6},{1,3},{3,5},{5,7},{8,10},{10,12},{12,14},{9,11},... | collective-permute-start | bytes 688136 | tf_op jit(solution)/shard_map/ppermute | solution.py:17
  16.5 1.6 copy-start.1
  32.5 2.0 copy-start.2
  46.1 12.0 %collective-permute-start.6 = (f32[8,288,512]{2,1,0:T(8,128)S(1)}, f32[8,288,512]{2,1,0:T(8,128)S(1)}, u32[]{:S(2)}, u32[]{:S(2)}) collective-permute-start(f32[8,288,512]{2,1,0:T(8,128)S(1)} %select_bitcast_fusion), channel_id=1, source_target_pairs={{0,2},{2,0},{1,3},{3,1},{4,6},{6,4},{5,7},{7,5},{8,10},{10,8},{9,1... | collective-permute-start | bytes 14155784 | tf_op jit(solution)/shard_map/ppermute | solution.py:116
  62.1 161.1 %all-gather.3.cloned.1.call-start = ((), (), s32[]{:S(2)}) async-start(), calls=%async_computation.1 | async-start | bytes 5308416 | tf_op jit(solution)/shard_map/all_gather | solution.py:61
  62.2 6.2 %collective-permute-start.2 = (bf16[1,144,512]{2,1,0:T(8,128)(2,1)S(1)}, bf16[1,144,512]{2,1,0:T(8,128)(2,1)S(1)}, u32[]{:S(2)}, u32[]{:S(2)}) collective-permute-start(bf16[1,144,512]{2,1,0:T(8,128)(2,1)S(1)} %fusion.98), channel_id=1, source_target_pairs={{0,8},{8,0},{16,24},{24,16},{1,9},{9,1},{17,25},{25,17},{2,10},{10... | collective-permute-start | bytes 442376 | tf_op jit(solution)/shard_map/ppermute | solution.py:33
  68.4 22.4 %collective-permute-start.3 = (bf16[2,144,512]{2,1,0:T(8,128)(2,1)S(1)}, bf16[2,144,512]{2,1,0:T(8,128)(2,1)S(1)}, u32[]{:S(2)}, u32[]{:S(2)}) collective-permute-start(bf16[2,144,512]{2,1,0:T(8,128)(2,1)S(1)} %maximum_select_fusion.1), channel_id=1, source_target_pairs={{0,16},{8,24},{16,0},{24,8},{1,17},{9,25},{17,1},{25,9},{2,18},{10... | collective-permute-start | bytes 884744 | tf_op jit(solution)/shard_map/ppermute | solution.py:33
  91.8 165.9 %all-gather.5.cloned.1.call-start = ((), (), s32[]{:S(2)}) async-start(), calls=%async_computation.3 | async-start | bytes 2654208 | tf_op jit(solution)/shard_map/all_gather | solution.py:120
  92.9 4.4 %collective-permute-start.1 = (bf16[6,1,1,32,512]{4,3,2,1,0:T(8,128)(2,1)S(1)}, bf16[6,1,1,32,512]{4,3,2,1,0:T(8,128)(2,1)S(1)}, u32[]{:S(2)}, u32[]{:S(2)}) collective-permute-start(bf16[6,1,1,32,512]{4,3,2,1,0:T(8,128)(2,1)S(1)} %get-tuple-element.30), channel_id=1, source_target_pairs={{2,0},{4,2},{6,4},{3,1},{5,3},{7,5},{10,8},{12,10},{14,12},{11,9},... | collective-permute-start | bytes 589832 | tf_op jit(solution)/shard_map/ppermute | solution.py:18
  94.2 4.1 %collective-permute-start = (bf16[6,1,1,32,512]{4,3,2,1,0:T(8,128)(2,1)S(1)}, bf16[6,1,1,32,512]{4,3,2,1,0:T(8,128)(2,1)S(1)}, u32[]{:S(2)}, u32[]{:S(2)}) collective-permute-start(bf16[6,1,1,32,512]{4,3,2,1,0:T(8,128)(2,1)S(1)} %get-tuple-element.29), channel_id=1, source_target_pairs={{0,2},{2,4},{4,6},{1,3},{3,5},{5,7},{8,10},{10,12},{12,14},{9,11},... | collective-permute-start | bytes 589832 | tf_op jit(solution)/shard_map/ppermute | solution.py:17
  100.6 1.7 copy-start.3
  249.0 1.1 copy-start.5
  249.1 1.3 copy-start.6
  249.1 1.5 copy-start.7
  249.1 1.7 copy-start.8
  249.1 1.9 copy-start.9
  250.9 1.7 copy-start.4
Sparse Core Ops, SparseCore 0:
  62.2 160.8 reduce-scatter.1
Sparse Core Ops, SparseCore 1:
  91.8 43.1 all-gather.2
  223.2 27.9 all-gather.4

commit v9 on v6

--- a/solution.py
+++ b/solution.py
@@ -117,7 +117,7 @@
     total_cells = samples * data_count * lax.axis_size("rep") * rows * lax.axis_size("space") * cols
     names = [entry for axis in ("dp",) + rest for entry in reversed(bits_of(axis))]
     piece_shape = (weight_local.shape[0] // 2 ** len(names), weight_local.shape[1])
-    blocks = weight_local.reshape((2,) * len(names) + piece_shape)
+    blocks = lax.optimization_barrier(weight_local).reshape((2,) * len(names) + piece_shape)
     space_bits, rep_bits, dp_bits = bits_of("space"), bits_of("rep"), bits_of("dp")
     blocks, names = halving_scatter(blocks, names, space_bits[:1])
     half = chans // 2

time: 242 us -> 224 us (0.926)
  local copies, waits for them, and re-layouts: 69.8 us -> 54 us
  waiting for transfers between devices: 42.8 us -> 39.9 us
    reshape x1 -> x0, local copies, waits for them, and re-layouts: 18.6 us -> none  [on_device(): spike_cols = jnp.concatenate([spike_pad[:, :, 1 + a:1 + a + rows, 1 + b:1...]
    slice x1, local copies, waits for them, and re-layouts: 0.3 us -> 4.89 us  [halving_scatter(): low = lax.index_in_dim(blocks, 0, dim, keepdims=False)]
    ppermute x9, waiting for transfers between devices: 31 us -> 28 us  [halving_scatter(): sent = lax.ppermute(jnp.where(first, high, low), axis, pairs)]
    unnamed x60 -> x56, local copies, waits for them, and re-layouts: 19.9 us -> 18.2 us
    add x9 -> x8, other arithmetic: 8.62 us -> 8.37 us  [halving_scatter(): blocks = jnp.where(first, low, high) + sent]
    unnamed x13 -> x14, other arithmetic: 7.24 us -> 7.26 us
  transfers between devices with their start and end apart: 17 -> 17, of which waited for: 9 -> 10; matrix products, arithmetic and copies ran while one was open for 35% -> 39% of each run, Pallas kernels for 0% -> 0%
where the time goes in v9:
time: 224 us; the launch traced here: 223 us
  local copies, waits for them, and re-layouts  54 us (24%)
  other arithmetic  43.1 us (19%)
  waiting for transfers between devices  39.9 us (18%)
  matrix products  36 us (16%)
  starting transfers between devices  35.2 us (16%)
  between operations  14.7 us (7%)
    ppermute x9, waiting for transfers between devices, halving_scatter(): sent = lax.ppermute(jnp.where(first, high, low), axis, pairs)  28 us
    reshape x1, local copies, waits for them, and re-layouts, on_device(): grad_cols = jnp.concatenate([grad_pad[:, :, 1 - a:1 - a + rows, 1 - b:1 -...  26.8 us
    dot_general x1, matrix products, on_device(): jnp.einsum('nkd,kcd->nc', grad_cols, weights.reshape(9, chans, chans), pr...  25.9 us
    ppermute x9, starting transfers between devices, halving_scatter(): sent = lax.ppermute(jnp.where(first, high, low), axis, pairs)  22.2 us
    unnamed x56, local copies, waits for them, and re-layouts  18.2 us
    ppermute x2, waiting for transfers between devices, doubling_gather(): other = lax.ppermute(blocks, axis, pairs)  10.7 us
    dot_general x1, matrix products, on_device(): lax.dot_general(spike_cols, grad_flat, (((0,), (0,)), ((), ())), preferre...  10.1 us
    add x8, other arithmetic, halving_scatter(): blocks = jnp.where(first, low, high) + sent  8.37 us
  transfers between devices with their start and end apart: 17, of which 10 were waited for; matrix products, arithmetic and copies ran while one was open for 39% of the time, Pallas kernels for 0%

profile of v9, /device:TPU:0, one launch (start us, length us, event | category | flops | bytes accessed | tf_op | source)
XLA Modules:
  0.0 222.9 jit_solution(10988562659282680215)
XLA Ops:
  7.2 1.2 pad_maximum_fusion.5
  8.5 1.3 collective-permute-start.5
  9.8 3.0 %collective-permute-start.4 = (bf16[7,1,1,32,512]{4,3,2,1,0:T(8,128)(2,1)S(1)}, bf16[7,1,1,32,512]{4,3,2,1,0:T(8,128)(2,1)S(1)}, u32[]{:S(2)}, u32[]{:S(2)}) collective-permute-start(bf16[7,1,1,32,512]{4,3,2,1,0:T(8,128)(2,1)S(1)} %get-tuple-element.31), channel_id=1, source_target_pairs={{0,2},{2,4},{4,6},{1,3},{3,5},{5,7},{8,10},{10,12},{12,14},{9,11},... | collective-permute-start | bytes 688136 | tf_op jit(solution)/shard_map/ppermute | solution.py:16
  12.9 1.1 collective-permute-done.4
  13.9 1.8 pad_maximum_fusion
  16.5 0.5 fusion.84
  18.2 0.7 fusion.17
  18.9 0.7 fusion.18
  19.8 0.7 fusion.19
  20.5 0.7 fusion.20
  21.4 0.7 fusion.21
  22.1 0.7 copy-done.4
  22.8 10.1 %fusion.4 = f32[4608,512]{1,0:T(8,128)} fusion(bf16[6,1,8,32,4608]{4,3,2,0,1:T(8,128)(2,1)S(1)} %fusion.21, bf16[6,1,8,32,512]{4,3,2,1,0:T(8,128)(2,1)S(1)} %copy-done.4), kind=kOutput, calls=%fused_computation.4 | convolution fusion | flops 7247757312 | bytes 25165824 | tf_op jit(solution)/shard_map/dot_general | solution.py:100
  32.9 4.9 %fusion.106 = (f32[2,2,2,1,2,144,512]{6,5,4,3,2,1,0:T(8,128)S(1)}, f32[2,2,2,1,2,144,512]{6,5,4,3,2,1,0:T(8,128)S(1)}) fusion(f32[2,2,2,2,2,144,512]{6,5,4,3,2,1,0:T(8,128)} %bitcast.210), kind=kLoop, calls=%fused_computation.180 | loop fusion | bytes 18874368 | tf_op jit(solution)/shard_map/slice | solution.py:41
  37.8 3.8 %select_bitcast_fusion = f32[2,2,2,2,144,512]{5,4,0,1,2,3:T(8,128)} fusion(f32[2,2,2,1,2,144,512]{6,5,4,3,2,1,0:T(8,128)S(1)} %get-tuple-element.22, f32[2,2,2,1,2,144,512]{6,5,4,3,2,1,0:T(8,128)S(1)} %get-tuple-element.21, pred[]{:T(512)S(6)} %eq.37), kind=kLoop, calls=%fused_computation.9 | loop fusion | flops 1179648 | bytes 14155777 | tf_op jit(solution)/shard_map/jit(_where)/select_n | solution.py:44
  41.6 1.2 copy-done.9
  42.9 4.4 %collective-permute-start.6 = (f32[2,2,2,2,144,512]{5,4,0,1,2,3:T(8,128)}, f32[2,2,2,2,144,512]{5,4,0,1,2,3:T(8,128)}, u32[]{:S(2)}, u32[]{:S(2)}) collective-permute-start(f32[2,2,2,2,144,512]{5,4,0,1,2,3:T(8,128)} %select_bitcast_fusion), channel_id=1, source_target_pairs={{0,2},{2,0},{4,6},{6,4},{1,3},{3,1},{5,7},{7,5},{8,10},{10,8},{12,... | collective-permute-start | bytes 14155784 | tf_op jit(solution)/shard_map/ppermute | solution.py:44
  47.3 1.6 collective-permute-start.2
  48.9 4.2 %collective-permute-done.2 = bf16[1,144,512]{2,1,0:T(8,128)(2,1)S(1)} collective-permute-done((bf16[1,144,512]{2,1,0:T(8,128)(2,1)S(1)}, bf16[1,144,512]{2,1,0:T(8,128)(2,1)S(1)}, u32[]{:S(2)}, u32[]{:S(2)}) %collective-permute-start.2) | collective-permute-done | bytes 147488 | tf_op jit(solution)/shard_map/ppermute | solution.py:28
  53.2 2.7 %collective-permute-start.3 = (bf16[2,144,512]{2,1,0:T(8,128)(2,1)S(1)}, bf16[2,144,512]{2,1,0:T(8,128)(2,1)S(1)}, u32[]{:S(2)}, u32[]{:S(2)}) collective-permute-start(bf16[2,144,512]{2,1,0:T(8,128)(2,1)S(1)} %maximum_select_fusion.1), channel_id=1, source_target_pairs={{0,16},{8,24},{16,0},{24,8},{1,17},{9,25},{17,1},{25,9},{2,18},{10... | collective-permute-start | bytes 884744 | tf_op jit(solution)/shard_map/ppermute | solution.py:28
  55.8 1.7 fusion.108
  57.5 1.3 collective-permute-start.1
  58.8 3.0 %collective-permute-start = (bf16[6,1,1,32,512]{4,3,2,1,0:T(8,128)(2,1)S(1)}, bf16[6,1,1,32,512]{4,3,2,1,0:T(8,128)(2,1)S(1)}, u32[]{:S(2)}, u32[]{:S(2)}) collective-permute-start(bf16[6,1,1,32,512]{4,3,2,1,0:T(8,128)(2,1)S(1)} %get-tuple-element.33), channel_id=1, source_target_pairs={{0,2},{2,4},{4,6},{1,3},{3,5},{5,7},{8,10},{10,12},{12,14},{9,11},... | collective-permute-start | bytes 589832 | tf_op jit(solution)/shard_map/ppermute | solution.py:16
  61.9 6.6 %collective-permute-done.3 = bf16[2,144,512]{2,1,0:T(8,128)(2,1)S(1)} collective-permute-done((bf16[2,144,512]{2,1,0:T(8,128)(2,1)S(1)}, bf16[2,144,512]{2,1,0:T(8,128)(2,1)S(1)}, u32[]{:S(2)}, u32[]{:S(2)}) %collective-permute-start.3) | collective-permute-done | bytes 294944 | tf_op jit(solution)/shard_map/ppermute | solution.py:28
  68.5 0.9 maximum_select_fusion
  69.6 1.5 fusion.15
  72.0 0.7 slice_dynamic-update-slice_fusion.6
  72.9 5.9 %copy-done.10 = bf16[6,1,8,32,4608]{4,3,2,1,0:T(8,128)(2,1)} copy-done((bf16[6,1,8,32,4608]{4,3,2,1,0:T(8,128)(2,1)}, bf16[6,1,8,32,4608]{4,3,2,1,0:T(8,128)(2,1)S(1)}, u32[]{:S(2)}) %copy-start.10) | copy-done | bytes 14155800
  78.9 4.4 %bitcast_add_fusion = f32[2,2,2,2,144,512]{5,4,0,1,2,3:T(8,128)S(1)} fusion(f32[2,2,2,2,144,512]{5,4,0,1,2,3:T(8,128)} %collective-permute-done.6, f32[2,2,2,1,2,144,512]{6,5,4,3,2,1,0:T(8,128)S(1)} %bitcast.209, f32[2,2,2,1,2,144,512]{6,5,4,3,2,1,0:T(8,128)S(1)} %bitcast.207, pred[]{:T(512)S(6)} %eq.37), kind=kLoop, calls=%fused_computation.8 | loop fusion | flops 2359296 | bytes 18874368 | tf_op jit(solution)/shard_map/add | solution.py:45
  83.3 1.6 select_bitcast_fusion.2
  84.9 3.6 %collective-permute-start.7 = (f32[2,2,2,144,256]{4,3,0,1,2:T(8,128)}, f32[2,2,2,144,256]{4,3,0,1,2:T(8,128)}, u32[]{:S(2)}, u32[]{:S(2)}) collective-permute-start(f32[2,2,2,144,256]{4,3,0,1,2:T(8,128)} %select_bitcast_fusion.2), channel_id=1, source_target_pairs={{0,4},{2,6},{4,0},{6,2},{1,5},{3,7},{5,1},{7,3},{8,12},{10,14},{12... | collective-permute-start | bytes 3538952 | tf_op jit(solution)/shard_map/ppermute | solution.py:44
  88.4 1.3 select_bitcast_fusion.1
  89.7 1.5 collective-permute-start.11
  91.3 1.4 slice_dynamic-update-slice_fusion.5
  92.7 2.0 slice_dynamic-update-slice_fusion.4
  94.7 1.4 fusion.22
  96.1 1.4 slice_dynamic-update-slice_fusion.3
  97.5 26.8 %reshape.660 = bf16[1536,9,512]{2,1,0:T(8,128)(2,1)} reshape(bf16[6,1,8,32,4608]{4,3,2,1,0:T(8,128)(2,1)} %slice_dynamic-update-slice_fusion.3) | data formatting | bytes 28311552 | tf_op jit(solution)/shard_map/reshape | solution.py:98
  124.3 1.6 fusion.30
  125.9 1.4 collective-permute-done.7
  127.3 2.0 collective-permute-done.11
  129.3 3.6 %fusion.26 = (f32[2,2,2,144,256]{4,3,0,1,2:T(8,128)S(1)}, f32[2,2,2,144,256]{4,3,0,1,2:T(8,128)S(1)}) fusion(f32[2,2,2,144,256]{4,3,0,1,2:T(8,128)} %collective-permute-done.7, f32[2,2,2,2,144,512]{5,4,0,1,2,3:T(8,128)} %copy-done.7, pred[]{:T(512)S(6)} %eq.36, f32[2,2,2,144,256]{4,3,0,1,2:T(8,128)} %collective-permute-done.11, pred[]{:T(512)S(6)} %eq.35), kind=kLoop, calls=%fused_computation.48 | loop fusion | flops 1179648 | bytes 9437186 | tf_op jit(solution)/shard_map/add | solution.py:45
  133.3 0.9 fusion.75
  134.4 1.6 collective-permute-start.8
  135.9 0.9 convert_bitcast_fusion.1
  136.9 9.2 %collective-permute-done.12 = f32[2,2,144,256]{3,2,0,1:T(8,128)S(1)} collective-permute-done((f32[2,2,144,256]{3,2,0,1:T(8,128)S(1)}, f32[2,2,144,256]{3,2,0,1:T(8,128)S(1)}, u32[]{:S(2)}, u32[]{:S(2)}) %collective-permute-start.12) | collective-permute-done | bytes 589856 | tf_op jit(solution)/shard_map/ppermute | solution.py:44
  146.2 2.9 %collective-permute-start.13 = (f32[2,144,256]{2,1,0:T(8,128)S(1)}, f32[2,144,256]{2,1,0:T(8,128)S(1)}, u32[]{:S(2)}, u32[]{:S(2)}) collective-permute-start(f32[2,144,256]{2,1,0:T(8,128)S(1)} %select_bitcast_fusion.5), channel_id=1, source_target_pairs={{0,8},{8,0},{16,24},{24,16},{1,9},{9,1},{17,25},{25,17},{2,10},{10... | collective-permute-start | bytes 884744 | tf_op jit(solution)/shard_map/ppermute | solution.py:44
  149.2 1.3 collective-permute-start.9
  150.5 8.0 %collective-permute-done.13 = f32[2,144,256]{2,1,0:T(8,128)S(1)} collective-permute-done((f32[2,144,256]{2,1,0:T(8,128)S(1)}, f32[2,144,256]{2,1,0:T(8,128)S(1)}, u32[]{:S(2)}, u32[]{:S(2)}) %collective-permute-start.13) | collective-permute-done | bytes 294944 | tf_op jit(solution)/shard_map/ppermute | solution.py:44
  158.6 3.0 %collective-permute-start.14 = (f32[144,256]{1,0:T(8,128)S(1)}, f32[144,256]{1,0:T(8,128)S(1)}, u32[]{:S(2)}, u32[]{:S(2)}) collective-permute-start(f32[144,256]{1,0:T(8,128)S(1)} %select_bitcast_fusion.7), channel_id=1, source_target_pairs={{0,16},{8,24},{16,0},{24,8},{1,17},{9,25},{17,1},{25,9},{2,18},{10... | collective-permute-start | bytes 442376 | tf_op jit(solution)/shard_map/ppermute | solution.py:44
  162.1 3.6 %collective-permute-start.10 = (f32[144,256]{1,0:T(8,128)S(1)}, f32[144,256]{1,0:T(8,128)S(1)}, u32[]{:S(2)}, u32[]{:S(2)}) collective-permute-start(f32[144,256]{1,0:T(8,128)S(1)} %select_bitcast_fusion.8), channel_id=1, source_target_pairs={{0,16},{8,24},{16,0},{24,8},{1,17},{9,25},{17,1},{25,9},{2,18},{10... | collective-permute-start | bytes 442376 | tf_op jit(solution)/shard_map/ppermute | solution.py:44
  165.7 5.4 %collective-permute-done.14 = f32[144,256]{1,0:T(8,128)S(1)} collective-permute-done((f32[144,256]{1,0:T(8,128)S(1)}, f32[144,256]{1,0:T(8,128)S(1)}, u32[]{:S(2)}, u32[]{:S(2)}) %collective-permute-start.14) | collective-permute-done | bytes 147488 | tf_op jit(solution)/shard_map/ppermute | solution.py:44
  171.2 1.5 collective-permute-done.10
  172.8 0.7 pad_maximum_fusion.3
  173.6 25.9 %fusion.8 = f32[1536,512]{1,0:T(8,128)S(1)} fusion(bf16[9,512,512]{2,1,0:T(8,128)(2,1)} %bitcast.222, bf16[1536,9,512]{2,1,0:T(8,128)(2,1)} %reshape.660), kind=kOutput, calls=%fused_computation.10 | convolution fusion | flops 7247757312 | bytes 22020096 | tf_op jit(solution)/shard_map/nkd,kcd->nc/dot_general | solution.py:103
  199.8 0.7 copy-done.11
  201.3 1.7 broadcast_multiply_fusion.1
  203.1 0.8 fusion.87
  203.8 0.9 fusion.89
  204.8 0.8 fusion.91
  205.5 0.8 fusion.93
  206.3 0.9 fusion.95
  207.2 0.8 fusion.97
  208.0 8.0 %add_divide_fusion = (f32[1152,512]{1,0:T(8,128)}, f32[1152,512]{1,0:T(8,128)}, f32[1152,512]{1,0:T(8,128)}, f32[1152,512]{1,0:T(8,128)}) fusion(f32[1152,512]{1,0:T(8,128)} %all-gather.5.cloned.1.call-done, f32[1152,512]{1,0:T(8,128)} %param.11, f32[1152,512]{1,0:T(8,128)} %param.10), kind=kLoop, calls=%fused_computation.16 | loop fusion | flops 5898240 | bytes 16515072 | tf_op jit(solution)/shard_map/div | solution.py:136
  (82 shorter events, 6.1 us)
Async XLA Ops:
  7.2 40.1 %copy-start = (f32[1152,512]{1,0:T(8,128)S(1)}, f32[1152,512]{1,0:T(8,128)}, u32[]{:S(2)}) copy-start(f32[1152,512]{1,0:T(8,128)} %param.9) | copy-start | bytes 7077892
  7.2 6.7 %copy-start.16 = (bf16[1,8,32,512]{3,2,1,0:T(8,128)(2,1)S(1)}, bf16[1,8,32,512]{3,2,1,0:T(8,128)(2,1)}, u32[]{:S(2)}) copy-start(bf16[1,8,32,512]{3,2,1,0:T(8,128)(2,1)} %param.7) | copy-start | bytes 786436
  7.2 166.4 %all-gather.3.cloned.1.call-start = ((), (), s32[]{:S(2)}) async-start(), calls=%async_computation | async-start | bytes 5308416 | tf_op jit(solution)/shard_map/all_gather | solution.py:72
  8.5 4.4 %collective-permute-start.5 = (bf16[7,1,1,32,512]{4,3,2,1,0:T(8,128)(2,1)S(1)}, bf16[7,1,1,32,512]{4,3,2,1,0:T(8,128)(2,1)S(1)}, u32[]{:S(2)}, u32[]{:S(2)}) collective-permute-start(bf16[7,1,1,32,512]{4,3,2,1,0:T(8,128)(2,1)S(1)} %get-tuple-element.32), channel_id=1, source_target_pairs={{2,0},{4,2},{6,4},{3,1},{5,3},{7,5},{10,8},{12,10},{14,12},{11,9},... | collective-permute-start | bytes 688136 | tf_op jit(solution)/shard_map/ppermute | solution.py:17
  9.8 4.1 %collective-permute-start.4 = (bf16[7,1,1,32,512]{4,3,2,1,0:T(8,128)(2,1)S(1)}, bf16[7,1,1,32,512]{4,3,2,1,0:T(8,128)(2,1)S(1)}, u32[]{:S(2)}, u32[]{:S(2)}) collective-permute-start(bf16[7,1,1,32,512]{4,3,2,1,0:T(8,128)(2,1)S(1)} %get-tuple-element.31), channel_id=1, source_target_pairs={{0,2},{2,4},{4,6},{1,3},{3,5},{5,7},{8,10},{10,12},{12,14},{9,11},... | collective-permute-start | bytes 688136 | tf_op jit(solution)/shard_map/ppermute | solution.py:16
  15.7 1.6 copy-start.2
  21.4 1.4 copy-start.4
  37.8 3.8 %copy-start.8 = (f32[2,2,2,1,2,144,512]{6,5,4,3,2,1,0:T(8,128)}, f32[2,2,2,1,2,144,512]{6,5,4,3,2,1,0:T(8,128)S(1)}, u32[]{:S(2)}) copy-start(f32[2,2,2,1,2,144,512]{6,5,4,3,2,1,0:T(8,128)S(1)} %get-tuple-element.21) | copy-start | bytes 14155780
  37.8 5.0 %copy-start.9 = (f32[2,2,2,1,2,144,512]{6,5,4,3,2,1,0:T(8,128)}, f32[2,2,2,1,2,144,512]{6,5,4,3,2,1,0:T(8,128)S(1)}, u32[]{:S(2)}) copy-start(f32[2,2,2,1,2,144,512]{6,5,4,3,2,1,0:T(8,128)S(1)} %get-tuple-element.22) | copy-start | bytes 14155780
  42.9 36.0 %collective-permute-start.6 = (f32[2,2,2,2,144,512]{5,4,0,1,2,3:T(8,128)}, f32[2,2,2,2,144,512]{5,4,0,1,2,3:T(8,128)}, u32[]{:S(2)}, u32[]{:S(2)}) collective-permute-start(f32[2,2,2,2,144,512]{5,4,0,1,2,3:T(8,128)} %select_bitcast_fusion), channel_id=1, source_target_pairs={{0,2},{2,0},{4,6},{6,4},{1,3},{3,1},{5,7},{7,5},{8,10},{10,8},{12,... | collective-permute-start | bytes 14155784 | tf_op jit(solution)/shard_map/ppermute | solution.py:44
  47.3 22.3 %copy-start.5 = (bf16[6,1,8,32,512]{4,3,2,1,0:T(8,128)(2,1)S(1)}, bf16[6,1,8,32,512]{4,3,2,1,0:T(8,128)(2,1)}, u32[]{:S(2)}) copy-start(bf16[6,1,8,32,512]{4,3,2,1,0:T(8,128)(2,1)} %param.8) | copy-start | bytes 4718596
  47.3 5.8 %collective-permute-start.2 = (bf16[1,144,512]{2,1,0:T(8,128)(2,1)S(1)}, bf16[1,144,512]{2,1,0:T(8,128)(2,1)S(1)}, u32[]{:S(2)}, u32[]{:S(2)}) collective-permute-start(bf16[1,144,512]{2,1,0:T(8,128)(2,1)S(1)} %fusion.98), channel_id=1, source_target_pairs={{0,8},{8,0},{16,24},{24,16},{1,9},{9,1},{17,25},{25,17},{2,10},{10... | collective-permute-start | bytes 442376 | tf_op jit(solution)/shard_map/ppermute | solution.py:28
  53.2 15.3 %collective-permute-start.3 = (bf16[2,144,512]{2,1,0:T(8,128)(2,1)S(1)}, bf16[2,144,512]{2,1,0:T(8,128)(2,1)S(1)}, u32[]{:S(2)}, u32[]{:S(2)}) collective-permute-start(bf16[2,144,512]{2,1,0:T(8,128)(2,1)S(1)} %maximum_select_fusion.1), channel_id=1, source_target_pairs={{0,16},{8,24},{16,0},{24,8},{1,17},{9,25},{17,1},{25,9},{2,18},{10... | collective-permute-start | bytes 884744 | tf_op jit(solution)/shard_map/ppermute | solution.py:28
  57.5 12.0 %collective-permute-start.1 = (bf16[6,1,1,32,512]{4,3,2,1,0:T(8,128)(2,1)}, bf16[6,1,1,32,512]{4,3,2,1,0:T(8,128)(2,1)S(1)}, u32[]{:S(2)}, u32[]{:S(2)}) collective-permute-start(bf16[6,1,1,32,512]{4,3,2,1,0:T(8,128)(2,1)} %get-tuple-element.34), channel_id=1, source_target_pairs={{2,0},{4,2},{6,4},{3,1},{5,3},{7,5},{10,8},{12,10},{14,12},{11,9},... | collective-permute-start | bytes 589832 | tf_op jit(solution)/shard_map/ppermute | solution.py:17
  58.8 10.7 %collective-permute-start = (bf16[6,1,1,32,512]{4,3,2,1,0:T(8,128)(2,1)S(1)}, bf16[6,1,1,32,512]{4,3,2,1,0:T(8,128)(2,1)S(1)}, u32[]{:S(2)}, u32[]{:S(2)}) collective-permute-start(bf16[6,1,1,32,512]{4,3,2,1,0:T(8,128)(2,1)S(1)} %get-tuple-element.33), channel_id=1, source_target_pairs={{0,2},{2,4},{4,6},{1,3},{3,5},{5,7},{8,10},{10,12},{12,14},{9,11},... | collective-permute-start | bytes 589832 | tf_op jit(solution)/shard_map/ppermute | solution.py:16
  69.4 138.6 %all-gather.5.cloned.1.call-start = ((), (), s32[]{:S(2)}) async-start(), calls=%async_computation.1 | async-start | bytes 2654208 | tf_op jit(solution)/shard_map/all_gather | solution.py:132
  71.1 7.8 %slice-start.2 = ((s8[4718592]{0:T(1024)(128)(4,1)}), s8[4194304]{0:T(1024)(128)(4,1)S(1)}, s32[]{:S(2)}) async-start(s8[4718592]{0:T(1024)(128)(4,1)} %bitcast.208), calls=%async_computation.4 | async-start | bytes 8388608
  71.6 7.3 %slice-start = ((s8[4718592]{0:T(1024)(128)(4,1)}), s8[4194304]{0:T(1024)(128)(4,1)S(1)}, s32[]{:S(2)}) async-start(s8[4718592]{0:T(1024)(128)(4,1)} %bitcast.206), calls=%async_computation.2 | async-start | bytes 8388608
  71.8 7.1 %slice-start.1 = ((s8[4718592]{0:T(1024)(128)(4,1)}), s8[524288]{0:T(1024)(128)(4,1)S(1)}, s32[]{:S(2)}) async-start(s8[4718592]{0:T(1024)(128)(4,1)} %bitcast.206), calls=%async_computation.3 | async-start | bytes 1048576
  71.8 7.1 %slice-start.3 = ((s8[4718592]{0:T(1024)(128)(4,1)}), s8[524288]{0:T(1024)(128)(4,1)S(1)}, s32[]{:S(2)}) async-start(s8[4718592]{0:T(1024)(128)(4,1)} %bitcast.208), calls=%async_computation.5 | async-start | bytes 1048576
  72.9 5.9 %copy-start.10 = (bf16[6,1,8,32,4608]{4,3,2,1,0:T(8,128)(2,1)}, bf16[6,1,8,32,4608]{4,3,2,1,0:T(8,128)(2,1)S(1)}, u32[]{:S(2)}) copy-start(bf16[6,1,8,32,4608]{4,3,2,1,0:T(8,128)(2,1)S(1)} %constant_dynamic-update-slice_fusion) | copy-start | bytes 42467332
  83.3 6.5 %copy-start.7 = (f32[2,2,2,2,144,512]{5,4,0,1,2,3:T(8,128)}, f32[2,2,2,2,144,512]{5,4,0,1,2,3:T(8,128)S(1)}, u32[]{:S(2)}) copy-start(f32[2,2,2,2,144,512]{5,4,0,1,2,3:T(8,128)S(1)} %bitcast_add_fusion) | copy-start | bytes 14155780
  84.9 42.4 %collective-permute-start.7 = (f32[2,2,2,144,256]{4,3,0,1,2:T(8,128)}, f32[2,2,2,144,256]{4,3,0,1,2:T(8,128)}, u32[]{:S(2)}, u32[]{:S(2)}) collective-permute-start(f32[2,2,2,144,256]{4,3,0,1,2:T(8,128)} %select_bitcast_fusion.2), channel_id=1, source_target_pairs={{0,4},{2,6},{4,0},{6,2},{1,5},{3,7},{5,1},{7,3},{8,12},{10,14},{12... | collective-permute-start | bytes 3538952 | tf_op jit(solution)/shard_map/ppermute | solution.py:44
  89.7 39.5 %collective-permute-start.11 = (f32[2,2,2,144,256]{4,3,0,1,2:T(8,128)}, f32[2,2,2,144,256]{4,3,0,1,2:T(8,128)}, u32[]{:S(2)}, u32[]{:S(2)}) collective-permute-start(f32[2,2,2,144,256]{4,3,0,1,2:T(8,128)} %select_bitcast_fusion.1), channel_id=1, source_target_pairs={{0,1},{1,0},{2,3},{3,2},{4,5},{5,4},{6,7},{7,6},{8,9},{9,8},{10,11... | collective-permute-start | bytes 3538952 | tf_op jit(solution)/shard_map/ppermute | solution.py:44
  97.5 26.8 %copy-start.3 = (bf16[7,1,10,32,512]{4,3,2,1,0:T(8,128)(2,1)S(1)}, bf16[7,1,10,32,512]{4,3,2,1,0:T(8,128)(2,1)}, u32[]{:S(2)}) copy-start(bf16[7,1,10,32,512]{4,3,2,1,0:T(8,128)(2,1)} %copy-done.2) | copy-start | bytes 6881284
  132.9 13.1 %collective-permute-start.12 = (f32[2,2,144,256]{3,2,0,1:T(8,128)S(1)}, f32[2,2,144,256]{3,2,0,1:T(8,128)S(1)}, u32[]{:S(2)}, u32[]{:S(2)}) collective-permute-start(f32[2,2,144,256]{3,2,0,1:T(8,128)S(1)} %select_bitcast_fusion.3), channel_id=1, source_target_pairs={{0,4},{2,6},{4,0},{6,2},{1,5},{3,7},{5,1},{7,3},{8,12},{10,14},{12... | collective-permute-start | bytes 1769480 | tf_op jit(solution)/shard_map/ppermute | solution.py:44
  134.4 14.7 %collective-permute-start.8 = (f32[2,2,144,256]{3,2,0,1:T(8,128)S(1)}, f32[2,2,144,256]{3,2,0,1:T(8,128)S(1)}, u32[]{:S(2)}, u32[]{:S(2)}) collective-permute-start(f32[2,2,144,256]{3,2,0,1:T(8,128)S(1)} %select_bitcast_fusion.4), channel_id=1, source_target_pairs={{0,1},{1,0},{2,3},{3,2},{4,5},{5,4},{6,7},{7,6},{8,9},{9,8},{10,11... | collective-permute-start | bytes 1769480 | tf_op jit(solution)/shard_map/ppermute | solution.py:44
  146.2 12.4 %collective-permute-start.13 = (f32[2,144,256]{2,1,0:T(8,128)S(1)}, f32[2,144,256]{2,1,0:T(8,128)S(1)}, u32[]{:S(2)}, u32[]{:S(2)}) collective-permute-start(f32[2,144,256]{2,1,0:T(8,128)S(1)} %select_bitcast_fusion.5), channel_id=1, source_target_pairs={{0,8},{8,0},{16,24},{24,16},{1,9},{9,1},{17,25},{25,17},{2,10},{10... | collective-permute-start | bytes 884744 | tf_op jit(solution)/shard_map/ppermute | solution.py:44
  149.2 12.8 %collective-permute-start.9 = (f32[2,144,256]{2,1,0:T(8,128)S(1)}, f32[2,144,256]{2,1,0:T(8,128)S(1)}, u32[]{:S(2)}, u32[]{:S(2)}) collective-permute-start(f32[2,144,256]{2,1,0:T(8,128)S(1)} %select_bitcast_fusion.6), channel_id=1, source_target_pairs={{0,8},{8,0},{16,24},{24,16},{1,9},{9,1},{17,25},{25,17},{2,10},{10... | collective-permute-start | bytes 884744 | tf_op jit(solution)/shard_map/ppermute | solution.py:44
  158.6 12.5 %collective-permute-start.14 = (f32[144,256]{1,0:T(8,128)S(1)}, f32[144,256]{1,0:T(8,128)S(1)}, u32[]{:S(2)}, u32[]{:S(2)}) collective-permute-start(f32[144,256]{1,0:T(8,128)S(1)} %select_bitcast_fusion.7), channel_id=1, source_target_pairs={{0,16},{8,24},{16,0},{24,8},{1,17},{9,25},{17,1},{25,9},{2,18},{10... | collective-permute-start | bytes 442376 | tf_op jit(solution)/shard_map/ppermute | solution.py:44
  162.1 10.6 %collective-permute-start.10 = (f32[144,256]{1,0:T(8,128)S(1)}, f32[144,256]{1,0:T(8,128)S(1)}, u32[]{:S(2)}, u32[]{:S(2)}) collective-permute-start(f32[144,256]{1,0:T(8,128)S(1)} %select_bitcast_fusion.8), channel_id=1, source_target_pairs={{0,16},{8,24},{16,0},{24,8},{1,17},{9,25},{17,1},{25,9},{2,18},{10... | collective-permute-start | bytes 442376 | tf_op jit(solution)/shard_map/ppermute | solution.py:44
  199.4 1.1 copy-start.11
  199.4 1.3 copy-start.12
  199.5 1.5 copy-start.13
  199.5 1.7 copy-start.14
  199.5 1.9 copy-start.15
  201.3 1.7 copy-start.6
  208.0 8.0 %copy-start.1 = (f32[1152,512]{1,0:T(8,128)S(1)}, f32[1152,512]{1,0:T(8,128)}, u32[]{:S(2)}) copy-start(f32[1152,512]{1,0:T(8,128)} %param.9) | copy-start | bytes 7077892
Sparse Core Ops, SparseCore 0:
  69.6 57.3 all-gather.2
  173.7 29.3 all-gather.4

commit v10 on v9

--- a/solution.py
+++ b/solution.py
@@ -68,9 +68,7 @@
     piece_rows = shard_rows // rest_count
     local = master.astype(jnp.bfloat16)
     piece = lax.dynamic_slice_in_dim(local, lax.axis_index(rest) * piece_rows, piece_rows, 0)
-    over_dp = doubling_gather(piece[None], "dp")
-    over_all = lax.all_gather(over_dp, rest, axis=0, tiled=False)
-    weights = jnp.swapaxes(over_all, 0, 1).reshape(data_count * shard_rows, master.shape[1])
+    weights = lax.all_gather(piece, ("dp",) + rest, axis=0, tiled=True)
     stacked = jnp.concatenate([membrane[None], frames], axis=0)
     rimmed = extended(stacked, (("space", 2),), 1)
     voltage = rimmed[0].astype(jnp.float32)

time: 224 us -> 205 us (0.915)
  waiting for transfers between devices: 39.9 us -> 23 us
  starting transfers between devices: 35.2 us -> 32.8 us
    ppermute x2 -> x0, waiting for transfers between devices: 10.7 us -> none  [doubling_gather(): other = lax.ppermute(blocks, axis, pairs)]
    ppermute x9, waiting for transfers between devices: 28 us -> 20.4 us  [halving_scatter(): sent = lax.ppermute(jnp.where(first, high, low), axis, pairs)]
    ppermute x2 -> x0, starting transfers between devices: 4.29 us -> none  [doubling_gather(): other = lax.ppermute(blocks, axis, pairs)]
  transfers between devices with their start and end apart: 17 -> 15, of which waited for: 10 -> 10; matrix products, arithmetic and copies ran while one was open for 39% -> 43% of each run, Pallas kernels for 0% -> 0%
where the time goes in v10:
time: 205 us; the launch traced here: 204 us
  local copies, waits for them, and re-layouts  54.4 us (27%)
  other arithmetic  42.8 us (21%)
  matrix products  36 us (18%)
  starting transfers between devices  32.8 us (16%)
  waiting for transfers between devices  23 us (11%)
  between operations  14.6 us (7%)
    reshape x1, local copies, waits for them, and re-layouts, on_device(): grad_cols = jnp.concatenate([grad_pad[:, :, 1 - a:1 - a + rows, 1 - b:1 -...  26.7 us
    dot_general x1, matrix products, on_device(): jnp.einsum('nkd,kcd->nc', grad_cols, weights.reshape(9, chans, chans), pr...  25.9 us
    ppermute x9, starting transfers between devices, halving_scatter(): sent = lax.ppermute(jnp.where(first, high, low), axis, pairs)  24.1 us
    ppermute x9, waiting for transfers between devices, halving_scatter(): sent = lax.ppermute(jnp.where(first, high, low), axis, pairs)  20.4 us
    unnamed x56, local copies, waits for them, and re-layouts  18.6 us
    dot_general x1, matrix products, on_device(): lax.dot_general(spike_cols, grad_flat, (((0,), (0,)), ((), ())), preferre...  10.1 us
    add x8, other arithmetic, halving_scatter(): blocks = jnp.where(first, low, high) + sent  8.19 us
    div x1, other arithmetic, on_device(): update = new_moment / (jnp.sqrt(new_second) + 1e-08)  8.02 us
  transfers between devices with their start and end apart: 15, of which 10 were waited for; matrix products, arithmetic and copies ran while one was open for 43% of the time, Pallas kernels for 0%

profile of v10, /device:TPU:0, one launch (start us, length us, event | category | flops | bytes accessed | tf_op | source)
XLA Modules:
  0.0 203.7 jit_solution(5034185524007884014)
XLA Ops:
  7.2 1.2 pad_maximum_fusion.5
  8.5 1.3 collective-permute-start.3
  9.8 3.0 %collective-permute-start.2 = (bf16[7,1,1,32,512]{4,3,2,1,0:T(8,128)(2,1)S(1)}, bf16[7,1,1,32,512]{4,3,2,1,0:T(8,128)(2,1)S(1)}, u32[]{:S(2)}, u32[]{:S(2)}) collective-permute-start(bf16[7,1,1,32,512]{4,3,2,1,0:T(8,128)(2,1)S(1)} %get-tuple-element.31), channel_id=1, source_target_pairs={{0,2},{2,4},{4,6},{1,3},{3,5},{5,7},{8,10},{10,12},{12,14},{9,11},... | collective-permute-start | bytes 688136 | tf_op jit(solution)/shard_map/ppermute | solution.py:16
  12.9 1.1 collective-permute-done.2
  13.9 1.8 pad_maximum_fusion
  16.5 0.5 fusion.84
  18.2 0.7 fusion.17
  18.9 0.7 fusion.18
  19.8 0.7 fusion.19
  20.5 0.7 fusion.20
  21.4 0.7 fusion.21
  22.1 0.7 copy-done.4
  22.8 10.1 %fusion.4 = f32[4608,512]{1,0:T(8,128)} fusion(bf16[6,1,8,32,4608]{4,3,2,0,1:T(8,128)(2,1)S(1)} %fusion.21, bf16[6,1,8,32,512]{4,3,2,1,0:T(8,128)(2,1)S(1)} %copy-done.4), kind=kOutput, calls=%fused_computation.4 | convolution fusion | flops 7247757312 | bytes 25165824 | tf_op jit(solution)/shard_map/dot_general | solution.py:98
  32.9 4.9 %fusion.105 = (f32[2,2,2,1,2,144,512]{6,5,4,3,2,1,0:T(8,128)S(1)}, f32[2,2,2,1,2,144,512]{6,5,4,3,2,1,0:T(8,128)S(1)}) fusion(f32[2,2,2,2,2,144,512]{6,5,4,3,2,1,0:T(8,128)} %bitcast.203), kind=kLoop, calls=%fused_computation.177 | loop fusion | bytes 18874368 | tf_op jit(solution)/shard_map/slice | solution.py:41
  37.8 3.8 %select_bitcast_fusion = f32[2,2,2,2,144,512]{5,4,0,1,2,3:T(8,128)} fusion(f32[2,2,2,1,2,144,512]{6,5,4,3,2,1,0:T(8,128)S(1)} %get-tuple-element.22, f32[2,2,2,1,2,144,512]{6,5,4,3,2,1,0:T(8,128)S(1)} %get-tuple-element.21, pred[]{:T(512)S(6)} %eq.33), kind=kLoop, calls=%fused_computation.9 | loop fusion | flops 1179648 | bytes 14155777 | tf_op jit(solution)/shard_map/jit(_where)/select_n | solution.py:44
  41.6 1.3 copy-done.9
  42.9 4.4 %collective-permute-start.4 = (f32[2,2,2,2,144,512]{5,4,0,1,2,3:T(8,128)}, f32[2,2,2,2,144,512]{5,4,0,1,2,3:T(8,128)}, u32[]{:S(2)}, u32[]{:S(2)}) collective-permute-start(f32[2,2,2,2,144,512]{5,4,0,1,2,3:T(8,128)} %select_bitcast_fusion), channel_id=1, source_target_pairs={{0,2},{2,0},{4,6},{6,4},{1,3},{3,1},{5,7},{7,5},{8,10},{10,8},{12,... | collective-permute-start | bytes 14155784 | tf_op jit(solution)/shard_map/ppermute | solution.py:44
  47.3 0.7 dynamic-slice_convert_fusion
  48.1 1.1 fusion.107
  49.1 1.3 collective-permute-start.1
  50.4 3.0 %collective-permute-start = (bf16[6,1,1,32,512]{4,3,2,1,0:T(8,128)(2,1)S(1)}, bf16[6,1,1,32,512]{4,3,2,1,0:T(8,128)(2,1)S(1)}, u32[]{:S(2)}, u32[]{:S(2)}) collective-permute-start(bf16[6,1,1,32,512]{4,3,2,1,0:T(8,128)(2,1)S(1)} %get-tuple-element.33), channel_id=1, source_target_pairs={{0,2},{2,4},{4,6},{1,3},{3,5},{5,7},{8,10},{10,12},{12,14},{9,11},... | collective-permute-start | bytes 589832 | tf_op jit(solution)/shard_map/ppermute | solution.py:16
  53.5 1.4 collective-permute-done.1
  55.1 2.3 %fusion.15 = bf16[6,1,10,34,512]{4,3,2,1,0:T(8,128)(2,1)S(1)} fusion(bf16[6,1,1,32,512]{4,3,2,1,0:T(8,128)(2,1)S(1)} %collective-permute-done.1, bf16[6,1,8,32,512]{4,3,2,1,0:T(8,128)(2,1)} %param.8, bf16[6,1,1,32,512]{4,3,2,1,0:T(8,128)(2,1)S(1)} %collective-permute-done), kind=kLoop, calls=%fused_computation.15 | loop fusion | flops 12533760 | bytes 4055040 | tf_op jit(solution)/shard_map/concatenate | solution.py:18
  57.5 0.5 slice_dynamic-update-slice_fusion.8
  58.0 0.9 copy-done.5
  59.3 0.7 slice_dynamic-update-slice_fusion.6
  60.2 5.3 %copy-done.10 = bf16[6,1,8,32,4608]{4,3,2,1,0:T(8,128)(2,1)} copy-done((bf16[6,1,8,32,4608]{4,3,2,1,0:T(8,128)(2,1)}, bf16[6,1,8,32,4608]{4,3,2,1,0:T(8,128)(2,1)S(1)}, u32[]{:S(2)}) %copy-start.10) | copy-done | bytes 14155800
  65.6 4.1 %bitcast_add_fusion = f32[2,2,2,2,144,512]{5,4,0,1,2,3:T(8,128)S(1)} fusion(f32[2,2,2,2,144,512]{5,4,0,1,2,3:T(8,128)} %collective-permute-done.4, f32[2,2,2,1,2,144,512]{6,5,4,3,2,1,0:T(8,128)S(1)} %bitcast.202, f32[2,2,2,1,2,144,512]{6,5,4,3,2,1,0:T(8,128)S(1)} %bitcast.200, pred[]{:T(512)S(6)} %eq.33), kind=kLoop, calls=%fused_computation.8 | loop fusion | flops 2359296 | bytes 18874368 | tf_op jit(solution)/shard_map/add | solution.py:45
  69.7 1.6 select_bitcast_fusion.2
  71.3 5.2 %collective-permute-start.5 = (f32[2,2,2,144,256]{4,3,0,1,2:T(8,128)}, f32[2,2,2,144,256]{4,3,0,1,2:T(8,128)}, u32[]{:S(2)}, u32[]{:S(2)}) collective-permute-start(f32[2,2,2,144,256]{4,3,0,1,2:T(8,128)} %select_bitcast_fusion.2), channel_id=1, source_target_pairs={{0,4},{2,6},{4,0},{6,2},{1,5},{3,7},{5,1},{7,3},{8,12},{10,14},{12... | collective-permute-start | bytes 3538952 | tf_op jit(solution)/shard_map/ppermute | solution.py:44
  76.5 1.3 select_bitcast_fusion.1
  77.8 1.5 collective-permute-start.9
  79.3 1.5 slice_dynamic-update-slice_fusion.5
  80.8 2.0 slice_dynamic-update-slice_fusion.4
  82.7 1.4 fusion.22
  84.2 1.4 slice_dynamic-update-slice_fusion.3
  85.6 26.7 %reshape.554 = bf16[1536,9,512]{2,1,0:T(8,128)(2,1)} reshape(bf16[6,1,8,32,4608]{4,3,2,1,0:T(8,128)(2,1)} %slice_dynamic-update-slice_fusion.3) | data formatting | bytes 28311552 | tf_op jit(solution)/shard_map/reshape | solution.py:96
  112.3 1.6 fusion.30
  113.9 0.6 collective-permute-done.5
  114.5 3.7 %fusion.26 = (f32[2,2,2,144,256]{4,3,0,1,2:T(8,128)S(1)}, f32[2,2,2,144,256]{4,3,0,1,2:T(8,128)S(1)}) fusion(f32[2,2,2,144,256]{4,3,0,1,2:T(8,128)} %collective-permute-done.5, f32[2,2,2,2,144,512]{5,4,0,1,2,3:T(8,128)} %copy-done.7, pred[]{:T(512)S(6)} %eq.32, f32[2,2,2,144,256]{4,3,0,1,2:T(8,128)} %collective-permute-done.9, pred[]{:T(512)S(6)} %eq.31), kind=kLoop, calls=%fused_computation.48 | loop fusion | flops 1179648 | bytes 9437186 | tf_op jit(solution)/shard_map/add | solution.py:45
  118.3 0.7 collective-permute-start.10
  119.1 0.9 fusion.75
  120.1 1.6 collective-permute-start.6
  121.7 0.9 convert_bitcast_fusion.1
  122.6 7.7 %collective-permute-done.10 = f32[2,2,144,256]{3,2,0,1:T(8,128)S(1)} collective-permute-done((f32[2,2,144,256]{3,2,0,1:T(8,128)S(1)}, f32[2,2,144,256]{3,2,0,1:T(8,128)S(1)}, u32[]{:S(2)}, u32[]{:S(2)}) %collective-permute-start.10) | collective-permute-done | bytes 589856 | tf_op jit(solution)/shard_map/ppermute | solution.py:44
  130.5 1.9 collective-permute-start.11
  133.0 1.7 collective-permute-start.7
  134.6 5.7 %collective-permute-done.11 = f32[2,144,256]{2,1,0:T(8,128)S(1)} collective-permute-done((f32[2,144,256]{2,1,0:T(8,128)S(1)}, f32[2,144,256]{2,1,0:T(8,128)S(1)}, u32[]{:S(2)}, u32[]{:S(2)}) %collective-permute-start.11) | collective-permute-done | bytes 294944 | tf_op jit(solution)/shard_map/ppermute | solution.py:44
  140.4 3.4 %collective-permute-start.12 = (f32[144,256]{1,0:T(8,128)S(1)}, f32[144,256]{1,0:T(8,128)S(1)}, u32[]{:S(2)}, u32[]{:S(2)}) collective-permute-start(f32[144,256]{1,0:T(8,128)S(1)} %select_bitcast_fusion.7), channel_id=1, source_target_pairs={{0,16},{8,24},{16,0},{24,8},{1,17},{9,25},{17,1},{25,9},{2,18},{10... | collective-permute-start | bytes 442376 | tf_op jit(solution)/shard_map/ppermute | solution.py:44
  143.8 1.3 collective-permute-done.7
  145.2 3.7 %collective-permute-start.8 = (f32[144,256]{1,0:T(8,128)S(1)}, f32[144,256]{1,0:T(8,128)S(1)}, u32[]{:S(2)}, u32[]{:S(2)}) collective-permute-start(f32[144,256]{1,0:T(8,128)S(1)} %select_bitcast_fusion.8), channel_id=1, source_target_pairs={{0,16},{8,24},{16,0},{24,8},{1,17},{9,25},{17,1},{25,9},{2,18},{10... | collective-permute-start | bytes 442376 | tf_op jit(solution)/shard_map/ppermute | solution.py:44
  148.9 1.0 collective-permute-done.12
  149.9 3.6 %collective-permute-done.8 = f32[144,256]{1,0:T(8,128)S(1)} collective-permute-done((f32[144,256]{1,0:T(8,128)S(1)}, f32[144,256]{1,0:T(8,128)S(1)}, u32[]{:S(2)}, u32[]{:S(2)}) %collective-permute-start.8) | collective-permute-done | bytes 147488 | tf_op jit(solution)/shard_map/ppermute | solution.py:44
  153.5 0.8 pad_maximum_fusion.3
  154.4 25.9 %fusion.8 = f32[1536,512]{1,0:T(8,128)S(1)} fusion(bf16[9,512,512]{2,1,0:T(8,128)(2,1)} %bitcast.214, bf16[1536,9,512]{2,1,0:T(8,128)(2,1)} %reshape.554), kind=kOutput, calls=%fused_computation.10 | convolution fusion | flops 7247757312 | bytes 22020096 | tf_op jit(solution)/shard_map/nkd,kcd->nc/dot_general | solution.py:101
  180.6 0.7 copy-done.11
  182.1 1.7 broadcast_multiply_fusion.1
  183.9 0.8 fusion.87
  184.6 0.9 fusion.89
  185.6 0.8 fusion.91
  186.3 0.8 fusion.93
  187.1 0.9 fusion.95
  188.0 0.8 fusion.97
  188.8 8.0 %add_divide_fusion = (f32[1152,512]{1,0:T(8,128)}, f32[1152,512]{1,0:T(8,128)}, f32[1152,512]{1,0:T(8,128)}, f32[1152,512]{1,0:T(8,128)}) fusion(f32[1152,512]{1,0:T(8,128)} %all-gather.5.cloned.1.call-done, f32[1152,512]{1,0:T(8,128)} %param.11, f32[1152,512]{1,0:T(8,128)} %param.10), kind=kLoop, calls=%fused_computation.16 | loop fusion | flops 5898240 | bytes 16515072 | tf_op jit(solution)/shard_map/div | solution.py:134
  (75 shorter events, 5.3 us)
Async XLA Ops:
  7.2 40.1 %copy-start = (f32[1152,512]{1,0:T(8,128)S(1)}, f32[1152,512]{1,0:T(8,128)}, u32[]{:S(2)}) copy-start(f32[1152,512]{1,0:T(8,128)} %param.9) | copy-start | bytes 7077892
  7.2 6.7 %copy-start.16 = (bf16[1,8,32,512]{3,2,1,0:T(8,128)(2,1)S(1)}, bf16[1,8,32,512]{3,2,1,0:T(8,128)(2,1)}, u32[]{:S(2)}) copy-start(bf16[1,8,32,512]{3,2,1,0:T(8,128)(2,1)} %param.7) | copy-start | bytes 786436
  7.2 147.2 %all-gather.3.cloned.1.call-start = ((), (), s32[]{:S(2)}) async-start(), calls=%async_computation | async-start | bytes 4866048 | tf_op jit(solution)/shard_map/all_gather | solution.py:71
  8.5 4.4 %collective-permute-start.3 = (bf16[7,1,1,32,512]{4,3,2,1,0:T(8,128)(2,1)S(1)}, bf16[7,1,1,32,512]{4,3,2,1,0:T(8,128)(2,1)S(1)}, u32[]{:S(2)}, u32[]{:S(2)}) collective-permute-start(bf16[7,1,1,32,512]{4,3,2,1,0:T(8,128)(2,1)S(1)} %get-tuple-element.32), channel_id=1, source_target_pairs={{2,0},{4,2},{6,4},{3,1},{5,3},{7,5},{10,8},{12,10},{14,12},{11,9},... | collective-permute-start | bytes 688136 | tf_op jit(solution)/shard_map/ppermute | solution.py:17
  9.8 4.1 %collective-permute-start.2 = (bf16[7,1,1,32,512]{4,3,2,1,0:T(8,128)(2,1)S(1)}, bf16[7,1,1,32,512]{4,3,2,1,0:T(8,128)(2,1)S(1)}, u32[]{:S(2)}, u32[]{:S(2)}) collective-permute-start(bf16[7,1,1,32,512]{4,3,2,1,0:T(8,128)(2,1)S(1)} %get-tuple-element.31), channel_id=1, source_target_pairs={{0,2},{2,4},{4,6},{1,3},{3,5},{5,7},{8,10},{10,12},{12,14},{9,11},... | collective-permute-start | bytes 688136 | tf_op jit(solution)/shard_map/ppermute | solution.py:16
  15.7 1.6 copy-start.2
  21.4 1.4 copy-start.4
  37.8 3.8 %copy-start.8 = (f32[2,2,2,1,2,144,512]{6,5,4,3,2,1,0:T(8,128)}, f32[2,2,2,1,2,144,512]{6,5,4,3,2,1,0:T(8,128)S(1)}, u32[]{:S(2)}) copy-start(f32[2,2,2,1,2,144,512]{6,5,4,3,2,1,0:T(8,128)S(1)} %get-tuple-element.21) | copy-start | bytes 14155780
  37.8 5.0 %copy-start.9 = (f32[2,2,2,1,2,144,512]{6,5,4,3,2,1,0:T(8,128)}, f32[2,2,2,1,2,144,512]{6,5,4,3,2,1,0:T(8,128)S(1)}, u32[]{:S(2)}) copy-start(f32[2,2,2,1,2,144,512]{6,5,4,3,2,1,0:T(8,128)S(1)} %get-tuple-element.22) | copy-start | bytes 14155780
  42.9 22.7 %collective-permute-start.4 = (f32[2,2,2,2,144,512]{5,4,0,1,2,3:T(8,128)}, f32[2,2,2,2,144,512]{5,4,0,1,2,3:T(8,128)}, u32[]{:S(2)}, u32[]{:S(2)}) collective-permute-start(f32[2,2,2,2,144,512]{5,4,0,1,2,3:T(8,128)} %select_bitcast_fusion), channel_id=1, source_target_pairs={{0,2},{2,0},{4,6},{6,4},{1,3},{3,1},{5,7},{7,5},{8,10},{10,8},{12,... | collective-permute-start | bytes 14155784 | tf_op jit(solution)/shard_map/ppermute | solution.py:44
  48.0 140.8 %all-gather.5.cloned.1.call-start = ((), (), s32[]{:S(2)}) async-start(), calls=%async_computation.1 | async-start | bytes 2654208 | tf_op jit(solution)/shard_map/all_gather | solution.py:130
  49.1 5.9 %collective-permute-start.1 = (bf16[6,1,1,32,512]{4,3,2,1,0:T(8,128)(2,1)S(1)}, bf16[6,1,1,32,512]{4,3,2,1,0:T(8,128)(2,1)S(1)}, u32[]{:S(2)}, u32[]{:S(2)}) collective-permute-start(bf16[6,1,1,32,512]{4,3,2,1,0:T(8,128)(2,1)S(1)} %get-tuple-element.34), channel_id=1, source_target_pairs={{2,0},{4,2},{6,4},{3,1},{5,3},{7,5},{10,8},{12,10},{14,12},{11,9},... | collective-permute-start | bytes 589832 | tf_op jit(solution)/shard_map/ppermute | solution.py:17
  50.4 4.7 %collective-permute-start = (bf16[6,1,1,32,512]{4,3,2,1,0:T(8,128)(2,1)S(1)}, bf16[6,1,1,32,512]{4,3,2,1,0:T(8,128)(2,1)S(1)}, u32[]{:S(2)}, u32[]{:S(2)}) collective-permute-start(bf16[6,1,1,32,512]{4,3,2,1,0:T(8,128)(2,1)S(1)} %get-tuple-element.33), channel_id=1, source_target_pairs={{0,2},{2,4},{4,6},{1,3},{3,5},{5,7},{8,10},{10,12},{12,14},{9,11},... | collective-permute-start | bytes 589832 | tf_op jit(solution)/shard_map/ppermute | solution.py:16
  57.4 1.4 copy-start.5
  57.5 8.1 %slice-start.2 = ((s8[4718592]{0:T(1024)(128)(4,1)}), s8[4194304]{0:T(1024)(128)(4,1)S(1)}, s32[]{:S(2)}) async-start(s8[4718592]{0:T(1024)(128)(4,1)} %bitcast.201), calls=%async_computation.4 | async-start | bytes 8388608
  58.9 6.7 %slice-start = ((s8[4718592]{0:T(1024)(128)(4,1)}), s8[4194304]{0:T(1024)(128)(4,1)S(1)}, s32[]{:S(2)}) async-start(s8[4718592]{0:T(1024)(128)(4,1)} %bitcast.199), calls=%async_computation.2 | async-start | bytes 8388608
  59.1 6.5 %slice-start.1 = ((s8[4718592]{0:T(1024)(128)(4,1)}), s8[524288]{0:T(1024)(128)(4,1)S(1)}, s32[]{:S(2)}) async-start(s8[4718592]{0:T(1024)(128)(4,1)} %bitcast.199), calls=%async_computation.3 | async-start | bytes 1048576
  59.1 6.5 %slice-start.3 = ((s8[4718592]{0:T(1024)(128)(4,1)}), s8[524288]{0:T(1024)(128)(4,1)S(1)}, s32[]{:S(2)}) async-start(s8[4718592]{0:T(1024)(128)(4,1)} %bitcast.201), calls=%async_computation.5 | async-start | bytes 1048576
  60.2 5.4 %copy-start.10 = (bf16[6,1,8,32,4608]{4,3,2,1,0:T(8,128)(2,1)}, bf16[6,1,8,32,4608]{4,3,2,1,0:T(8,128)(2,1)S(1)}, u32[]{:S(2)}) copy-start(bf16[6,1,8,32,4608]{4,3,2,1,0:T(8,128)(2,1)S(1)} %constant_dynamic-update-slice_fusion) | copy-start | bytes 42467332
  69.7 8.0 %copy-start.7 = (f32[2,2,2,2,144,512]{5,4,0,1,2,3:T(8,128)}, f32[2,2,2,2,144,512]{5,4,0,1,2,3:T(8,128)S(1)}, u32[]{:S(2)}) copy-start(f32[2,2,2,2,144,512]{5,4,0,1,2,3:T(8,128)S(1)} %bitcast_add_fusion) | copy-start | bytes 14155780
  71.3 43.2 %collective-permute-start.5 = (f32[2,2,2,144,256]{4,3,0,1,2:T(8,128)}, f32[2,2,2,144,256]{4,3,0,1,2:T(8,128)}, u32[]{:S(2)}, u32[]{:S(2)}) collective-permute-start(f32[2,2,2,144,256]{4,3,0,1,2:T(8,128)} %select_bitcast_fusion.2), channel_id=1, source_target_pairs={{0,4},{2,6},{4,0},{6,2},{1,5},{3,7},{5,1},{7,3},{8,12},{10,14},{12... | collective-permute-start | bytes 3538952 | tf_op jit(solution)/shard_map/ppermute | solution.py:44
  77.8 36.8 %collective-permute-start.9 = (f32[2,2,2,144,256]{4,3,0,1,2:T(8,128)}, f32[2,2,2,144,256]{4,3,0,1,2:T(8,128)}, u32[]{:S(2)}, u32[]{:S(2)}) collective-permute-start(f32[2,2,2,144,256]{4,3,0,1,2:T(8,128)} %select_bitcast_fusion.1), channel_id=1, source_target_pairs={{0,1},{1,0},{2,3},{3,2},{4,5},{5,4},{6,7},{7,6},{8,9},{9,8},{10,11... | collective-permute-start | bytes 3538952 | tf_op jit(solution)/shard_map/ppermute | solution.py:44
  85.6 26.7 %copy-start.3 = (bf16[7,1,10,32,512]{4,3,2,1,0:T(8,128)(2,1)S(1)}, bf16[7,1,10,32,512]{4,3,2,1,0:T(8,128)(2,1)}, u32[]{:S(2)}) copy-start(bf16[7,1,10,32,512]{4,3,2,1,0:T(8,128)(2,1)} %copy-done.2) | copy-start | bytes 6881284
  118.3 12.0 %collective-permute-start.10 = (f32[2,2,144,256]{3,2,0,1:T(8,128)S(1)}, f32[2,2,144,256]{3,2,0,1:T(8,128)S(1)}, u32[]{:S(2)}, u32[]{:S(2)}) collective-permute-start(f32[2,2,144,256]{3,2,0,1:T(8,128)S(1)} %select_bitcast_fusion.3), channel_id=1, source_target_pairs={{0,4},{2,6},{4,0},{6,2},{1,5},{3,7},{5,1},{7,3},{8,12},{10,14},{12... | collective-permute-start | bytes 1769480 | tf_op jit(solution)/shard_map/ppermute | solution.py:44
  120.1 12.7 %collective-permute-start.6 = (f32[2,2,144,256]{3,2,0,1:T(8,128)S(1)}, f32[2,2,144,256]{3,2,0,1:T(8,128)S(1)}, u32[]{:S(2)}, u32[]{:S(2)}) collective-permute-start(f32[2,2,144,256]{3,2,0,1:T(8,128)S(1)} %select_bitcast_fusion.4), channel_id=1, source_target_pairs={{0,1},{1,0},{2,3},{3,2},{4,5},{5,4},{6,7},{7,6},{8,9},{9,8},{10,11... | collective-permute-start | bytes 1769480 | tf_op jit(solution)/shard_map/ppermute | solution.py:44
  130.5 9.9 %collective-permute-start.11 = (f32[2,144,256]{2,1,0:T(8,128)S(1)}, f32[2,144,256]{2,1,0:T(8,128)S(1)}, u32[]{:S(2)}, u32[]{:S(2)}) collective-permute-start(f32[2,144,256]{2,1,0:T(8,128)S(1)} %select_bitcast_fusion.5), channel_id=1, source_target_pairs={{0,8},{8,0},{16,24},{24,16},{1,9},{9,1},{17,25},{25,17},{2,10},{10... | collective-permute-start | bytes 884744 | tf_op jit(solution)/shard_map/ppermute | solution.py:44
  133.0 12.1 %collective-permute-start.7 = (f32[2,144,256]{2,1,0:T(8,128)S(1)}, f32[2,144,256]{2,1,0:T(8,128)S(1)}, u32[]{:S(2)}, u32[]{:S(2)}) collective-permute-start(f32[2,144,256]{2,1,0:T(8,128)S(1)} %select_bitcast_fusion.6), channel_id=1, source_target_pairs={{0,8},{8,0},{16,24},{24,16},{1,9},{9,1},{17,25},{25,17},{2,10},{10... | collective-permute-start | bytes 884744 | tf_op jit(solution)/shard_map/ppermute | solution.py:44
  140.4 9.4 %collective-permute-start.12 = (f32[144,256]{1,0:T(8,128)S(1)}, f32[144,256]{1,0:T(8,128)S(1)}, u32[]{:S(2)}, u32[]{:S(2)}) collective-permute-start(f32[144,256]{1,0:T(8,128)S(1)} %select_bitcast_fusion.7), channel_id=1, source_target_pairs={{0,16},{8,24},{16,0},{24,8},{1,17},{9,25},{17,1},{25,9},{2,18},{10... | collective-permute-start | bytes 442376 | tf_op jit(solution)/shard_map/ppermute | solution.py:44
  145.2 8.4 %collective-permute-start.8 = (f32[144,256]{1,0:T(8,128)S(1)}, f32[144,256]{1,0:T(8,128)S(1)}, u32[]{:S(2)}, u32[]{:S(2)}) collective-permute-start(f32[144,256]{1,0:T(8,128)S(1)} %select_bitcast_fusion.8), channel_id=1, source_target_pairs={{0,16},{8,24},{16,0},{24,8},{1,17},{9,25},{17,1},{25,9},{2,18},{10... | collective-permute-start | bytes 442376 | tf_op jit(solution)/shard_map/ppermute | solution.py:44
  180.2 1.1 copy-start.11
  180.2 1.3 copy-start.12
  180.2 1.5 copy-start.13
  180.3 1.7 copy-start.14
  180.3 1.9 copy-start.15
  182.1 1.7 copy-start.6
  188.8 8.0 %copy-start.1 = (f32[1152,512]{1,0:T(8,128)S(1)}, f32[1152,512]{1,0:T(8,128)}, u32[]{:S(2)}) copy-start(f32[1152,512]{1,0:T(8,128)} %param.9) | copy-start | bytes 7077892
Sparse Core Ops, SparseCore 0:
  48.1 76.0 all-gather.2
  154.4 29.2 all-gather.4

commit v11 on v10

--- a/solution.py
+++ b/solution.py
@@ -119,7 +119,7 @@
     space_bits, rep_bits, dp_bits = bits_of("space"), bits_of("rep"), bits_of("dp")
     blocks, names = halving_scatter(blocks, names, space_bits[:1])
     half = chans // 2
-    orders = (space_bits[1:] + rep_bits + dp_bits, rep_bits + space_bits[1:] + dp_bits)
+    orders = (space_bits[1:] + rep_bits + dp_bits, rep_bits + dp_bits[:1] + space_bits[1:] + dp_bits[1:])
     shard_part = jnp.concatenate(
         [
             halving_scatter(blocks[..., part * half : (part + 1) * half], names, order)[0]

time: 205 us -> 208 us (1.015)
  waiting for transfers between devices: 23 us -> 35.4 us
  starting transfers between devices: 32.8 us -> 26.2 us
    ppermute x9, waiting for transfers between devices: 20.4 us -> 32.7 us  [halving_scatter(): sent = lax.ppermute(jnp.where(first, high, low), axis, pairs)]
    ppermute x9, starting transfers between devices: 24.1 us -> 17.4 us  [halving_scatter(): sent = lax.ppermute(jnp.where(first, high, low), axis, pairs)]
    unnamed x56 -> x58, local copies, waits for them, and re-layouts: 18.6 us -> 17 us
    add x8 -> x9, other arithmetic: 8.19 us -> 7.8 us  [halving_scatter(): blocks = jnp.where(first, low, high) + sent]
  transfers between devices with their start and end apart: 15 -> 15, of which waited for: 10 -> 7; matrix products, arithmetic and copies ran while one was open for 43% -> 41% of each run, Pallas kernels for 0% -> 0%
where the time goes in v11:
time: 208 us; the launch traced here: 207 us
  local copies, waits for them, and re-layouts  52.8 us (25%)
  other arithmetic  42.4 us (20%)
  matrix products  36 us (17%)
  waiting for transfers between devices  35.4 us (17%)
  starting transfers between devices  26.2 us (13%)
  between operations  14.7 us (7%)
    ppermute x9, waiting for transfers between devices, halving_scatter(): sent = lax.ppermute(jnp.where(first, high, low), axis, pairs)  32.7 us
    reshape x1, local copies, waits for them, and re-layouts, on_device(): grad_cols = jnp.concatenate([grad_pad[:, :, 1 - a:1 - a + rows, 1 - b:1 -...  26.7 us
    dot_general x1, matrix products, on_device(): jnp.einsum('nkd,kcd->nc', grad_cols, weights.reshape(9, chans, chans), pr...  25.9 us
    ppermute x9, starting transfers between devices, halving_scatter(): sent = lax.ppermute(jnp.where(first, high, low), axis, pairs)  17.4 us
    unnamed x58, local copies, waits for them, and re-layouts  17 us
    dot_general x1, matrix products, on_device(): lax.dot_general(spike_cols, grad_flat, (((0,), (0,)), ((), ())), preferre...  10.1 us
    div x1, other arithmetic, on_device(): update = new_moment / (jnp.sqrt(new_second) + 1e-08)  8.02 us
    add x9, other arithmetic, halving_scatter(): blocks = jnp.where(first, low, high) + sent  7.8 us
  transfers between devices with their start and end apart: 15, of which 7 were waited for; matrix products, arithmetic and copies ran while one was open for 41% of the time, Pallas kernels for 0%

profile of v11, /device:TPU:0, one launch (start us, length us, event | category | flops | bytes accessed | tf_op | source)
XLA Modules:
  0.0 207.4 jit_solution(9491133090735337569)
XLA Ops:
  7.2 1.2 pad_maximum_fusion.5
  8.5 1.3 collective-permute-start.3
  9.8 3.0 %collective-permute-start.2 = (bf16[7,1,1,32,512]{4,3,2,1,0:T(8,128)(2,1)S(1)}, bf16[7,1,1,32,512]{4,3,2,1,0:T(8,128)(2,1)S(1)}, u32[]{:S(2)}, u32[]{:S(2)}) collective-permute-start(bf16[7,1,1,32,512]{4,3,2,1,0:T(8,128)(2,1)S(1)} %get-tuple-element.29), channel_id=1, source_target_pairs={{0,2},{2,4},{4,6},{1,3},{3,5},{5,7},{8,10},{10,12},{12,14},{9,11},... | collective-permute-start | bytes 688136 | tf_op jit(solution)/shard_map/ppermute | solution.py:16
  12.9 1.1 collective-permute-done.2
  13.9 1.8 pad_maximum_fusion
  16.1 0.4 fusion.82
  16.5 0.5 fusion.84
  17.6 0.5 fusion.16
  18.2 0.7 fusion.17
  18.9 0.7 fusion.18
  19.8 0.7 fusion.19
  20.5 0.7 fusion.20
  21.4 0.7 fusion.21
  22.1 0.7 copy-done.4
  22.8 10.1 %fusion.4 = f32[4608,512]{1,0:T(8,128)} fusion(bf16[6,1,8,32,4608]{4,3,2,0,1:T(8,128)(2,1)S(1)} %fusion.21, bf16[6,1,8,32,512]{4,3,2,1,0:T(8,128)(2,1)S(1)} %copy-done.4), kind=kOutput, calls=%fused_computation.4 | convolution fusion | flops 7247757312 | bytes 25165824 | tf_op jit(solution)/shard_map/dot_general | solution.py:98
  32.9 4.9 %fusion.105 = (f32[2,2,2,1,2,144,512]{6,5,4,3,2,1,0:T(8,128)S(1)}, f32[2,2,2,1,2,144,512]{6,5,4,3,2,1,0:T(8,128)S(1)}) fusion(f32[2,2,2,2,2,144,512]{6,5,4,3,2,1,0:T(8,128)} %bitcast.203), kind=kLoop, calls=%fused_computation.177 | loop fusion | bytes 18874368 | tf_op jit(solution)/shard_map/slice | solution.py:41
  37.8 3.8 %select_bitcast_fusion = f32[2,2,2,2,144,512]{5,4,0,2,1,3:T(8,128)} fusion(f32[2,2,2,1,2,144,512]{6,5,4,3,2,1,0:T(8,128)S(1)} %get-tuple-element.22, f32[2,2,2,1,2,144,512]{6,5,4,3,2,1,0:T(8,128)S(1)} %get-tuple-element.21, pred[]{:T(512)S(6)} %eq.33), kind=kLoop, calls=%fused_computation.9 | loop fusion | flops 1179648 | bytes 14155777 | tf_op jit(solution)/shard_map/jit(_where)/select_n | solution.py:44
  41.6 1.3 copy-done.10
  42.9 4.4 %collective-permute-start.4 = (f32[2,2,2,2,144,512]{5,4,0,2,1,3:T(8,128)}, f32[2,2,2,2,144,512]{5,4,0,2,1,3:T(8,128)}, u32[]{:S(2)}, u32[]{:S(2)}) collective-permute-start(f32[2,2,2,2,144,512]{5,4,0,2,1,3:T(8,128)} %select_bitcast_fusion), channel_id=1, source_target_pairs={{0,2},{2,0},{4,6},{6,4},{1,3},{3,1},{5,7},{7,5},{8,10},{10,8},{12,... | collective-permute-start | bytes 14155784 | tf_op jit(solution)/shard_map/ppermute | solution.py:44
  47.3 0.7 dynamic-slice_convert_fusion
  48.1 1.1 fusion.107
  49.1 1.3 collective-permute-start.1
  50.4 3.0 %collective-permute-start = (bf16[6,1,1,32,512]{4,3,2,1,0:T(8,128)(2,1)S(1)}, bf16[6,1,1,32,512]{4,3,2,1,0:T(8,128)(2,1)S(1)}, u32[]{:S(2)}, u32[]{:S(2)}) collective-permute-start(bf16[6,1,1,32,512]{4,3,2,1,0:T(8,128)(2,1)S(1)} %get-tuple-element.31), channel_id=1, source_target_pairs={{0,2},{2,4},{4,6},{1,3},{3,5},{5,7},{8,10},{10,12},{12,14},{9,11},... | collective-permute-start | bytes 589832 | tf_op jit(solution)/shard_map/ppermute | solution.py:16
  53.5 1.4 collective-permute-done.1
  55.1 2.3 %fusion.15 = bf16[6,1,10,34,512]{4,3,2,1,0:T(8,128)(2,1)S(1)} fusion(bf16[6,1,1,32,512]{4,3,2,1,0:T(8,128)(2,1)S(1)} %collective-permute-done.1, bf16[6,1,8,32,512]{4,3,2,1,0:T(8,128)(2,1)} %param.8, bf16[6,1,1,32,512]{4,3,2,1,0:T(8,128)(2,1)S(1)} %collective-permute-done), kind=kLoop, calls=%fused_computation.15 | loop fusion | flops 12533760 | bytes 4055040 | tf_op jit(solution)/shard_map/concatenate | solution.py:18
  57.5 0.5 slice_dynamic-update-slice_fusion.8
  58.0 0.9 copy-done.5
  59.3 0.7 slice_dynamic-update-slice_fusion.6
  60.5 0.7 slice_dynamic-update-slice_fusion.4
  61.2 5.5 %copy-done.11 = bf16[6,1,8,32,4608]{4,3,2,1,0:T(8,128)(2,1)} copy-done((bf16[6,1,8,32,4608]{4,3,2,1,0:T(8,128)(2,1)}, bf16[6,1,8,32,4608]{4,3,2,1,0:T(8,128)(2,1)S(1)}, u32[]{:S(2)}) %copy-start.11) | copy-done | bytes 14155800
  66.7 4.1 %bitcast_add_fusion = f32[2,2,2,2,144,512]{5,4,0,2,1,3:T(8,128)S(1)} fusion(f32[2,2,2,2,144,512]{5,4,0,2,1,3:T(8,128)} %collective-permute-done.4, f32[2,2,2,1,2,144,512]{6,5,4,3,2,1,0:T(8,128)S(1)} %bitcast.202, f32[2,2,2,1,2,144,512]{6,5,4,3,2,1,0:T(8,128)S(1)} %bitcast.200, pred[]{:T(512)S(6)} %eq.33), kind=kLoop, calls=%fused_computation.8 | loop fusion | flops 2359296 | bytes 18874368 | tf_op jit(solution)/shard_map/add | solution.py:45
  70.9 1.6 select_bitcast_fusion.1
  72.4 1.5 collective-permute-start.9
  74.0 1.4 fusion.22
  75.4 1.3 select_bitcast_fusion.2
  76.7 5.2 %collective-permute-start.5 = (f32[2,2,2,144,256]{4,3,0,1,2:T(8,128)}, f32[2,2,2,144,256]{4,3,0,1,2:T(8,128)}, u32[]{:S(2)}, u32[]{:S(2)}) collective-permute-start(f32[2,2,2,144,256]{4,3,0,1,2:T(8,128)} %select_bitcast_fusion.2), channel_id=1, source_target_pairs={{0,4},{2,6},{4,0},{6,2},{1,5},{3,7},{5,1},{7,3},{8,12},{10,14},{12... | collective-permute-start | bytes 3538952 | tf_op jit(solution)/shard_map/ppermute | solution.py:44
  81.9 1.4 slice_dynamic-update-slice_fusion.3
  83.3 26.7 %reshape.554 = bf16[1536,9,512]{2,1,0:T(8,128)(2,1)} reshape(bf16[6,1,8,32,4608]{4,3,2,1,0:T(8,128)(2,1)} %slice_dynamic-update-slice_fusion.3) | data formatting | bytes 28311552 | tf_op jit(solution)/shard_map/reshape | solution.py:96
  110.0 0.9 fusion.75
  111.0 1.6 fusion.30
  112.6 0.7 copy-done.8
  113.3 1.6 bitcast_add_fusion.1
  115.1 1.6 collective-permute-start.10
  116.7 1.6 fusion.26
  118.4 0.9 collective-permute-start.6
  119.3 0.9 convert_bitcast_fusion.1
  120.2 13.1 %collective-permute-done.10 = f32[2,2,144,256]{3,2,0,1:T(8,128)S(1)} collective-permute-done((f32[2,2,144,256]{3,2,0,1:T(8,128)S(1)}, f32[2,2,144,256]{3,2,0,1:T(8,128)S(1)}, u32[]{:S(2)}, u32[]{:S(2)}) %collective-permute-start.10) | collective-permute-done | bytes 589856 | tf_op jit(solution)/shard_map/ppermute | solution.py:44
  134.0 0.4 collective-permute-start.7
  134.3 7.8 %collective-permute-done.11 = f32[2,144,256]{2,1,0:T(8,128)S(1)} collective-permute-done((f32[2,144,256]{2,1,0:T(8,128)S(1)}, f32[2,144,256]{2,1,0:T(8,128)S(1)}, u32[]{:S(2)}, u32[]{:S(2)}) %collective-permute-start.11) | collective-permute-done | bytes 294944 | tf_op jit(solution)/shard_map/ppermute | solution.py:44
  142.2 2.2 %collective-permute-start.12 = (f32[144,256]{1,0:T(8,128)S(1)}, f32[144,256]{1,0:T(8,128)S(1)}, u32[]{:S(2)}, u32[]{:S(2)}) collective-permute-start(f32[144,256]{1,0:T(8,128)S(1)} %select_bitcast_fusion.7), channel_id=1, source_target_pairs={{0,16},{8,24},{16,0},{24,8},{1,17},{9,25},{17,1},{25,9},{2,18},{10... | collective-permute-start | bytes 442376 | tf_op jit(solution)/shard_map/ppermute | solution.py:44
  144.5 0.9 collective-permute-start.8
  145.4 8.9 %collective-permute-done.12 = f32[144,256]{1,0:T(8,128)S(1)} collective-permute-done((f32[144,256]{1,0:T(8,128)S(1)}, f32[144,256]{1,0:T(8,128)S(1)}, u32[]{:S(2)}, u32[]{:S(2)}) %collective-permute-start.12) | collective-permute-done | bytes 147488 | tf_op jit(solution)/shard_map/ppermute | solution.py:44
  154.3 2.9 %collective-permute-done.8 = f32[144,256]{1,0:T(8,128)S(1)} collective-permute-done((f32[144,256]{1,0:T(8,128)S(1)}, f32[144,256]{1,0:T(8,128)S(1)}, u32[]{:S(2)}, u32[]{:S(2)}) %collective-permute-start.8) | collective-permute-done | bytes 147488 | tf_op jit(solution)/shard_map/ppermute | solution.py:44
  157.2 0.7 pad_maximum_fusion.3
  158.0 25.9 %fusion.8 = f32[1536,512]{1,0:T(8,128)S(1)} fusion(bf16[9,512,512]{2,1,0:T(8,128)(2,1)} %bitcast.214, bf16[1536,9,512]{2,1,0:T(8,128)(2,1)} %reshape.554), kind=kOutput, calls=%fused_computation.10 | convolution fusion | flops 7247757312 | bytes 22020096 | tf_op jit(solution)/shard_map/nkd,kcd->nc/dot_general | solution.py:101
  184.3 0.7 copy-done.12
  185.8 1.7 broadcast_multiply_fusion.1
  187.6 0.8 fusion.87
  188.3 0.9 fusion.89
  189.3 0.8 fusion.91
  190.0 0.8 fusion.93
  190.8 0.9 fusion.95
  191.7 0.8 fusion.97
  192.5 8.0 %add_divide_fusion = (f32[1152,512]{1,0:T(8,128)}, f32[1152,512]{1,0:T(8,128)}, f32[1152,512]{1,0:T(8,128)}, f32[1152,512]{1,0:T(8,128)}) fusion(f32[1152,512]{1,0:T(8,128)} %all-gather.5.cloned.1.call-done, f32[1152,512]{1,0:T(8,128)} %param.11, f32[1152,512]{1,0:T(8,128)} %param.10), kind=kLoop, calls=%fused_computation.16 | loop fusion | flops 5898240 | bytes 16515072 | tf_op jit(solution)/shard_map/div | solution.py:134
  (78 shorter events, 4.5 us)
Async XLA Ops:
  7.2 40.1 %copy-start = (f32[1152,512]{1,0:T(8,128)S(1)}, f32[1152,512]{1,0:T(8,128)}, u32[]{:S(2)}) copy-start(f32[1152,512]{1,0:T(8,128)} %param.9) | copy-start | bytes 7077892
  7.2 6.7 %copy-start.17 = (bf16[1,8,32,512]{3,2,1,0:T(8,128)(2,1)S(1)}, bf16[1,8,32,512]{3,2,1,0:T(8,128)(2,1)}, u32[]{:S(2)}) copy-start(bf16[1,8,32,512]{3,2,1,0:T(8,128)(2,1)} %param.7) | copy-start | bytes 786436
  7.2 150.8 %all-gather.3.cloned.1.call-start = ((), (), s32[]{:S(2)}) async-start(), calls=%async_computation | async-start | bytes 4866048 | tf_op jit(solution)/shard_map/all_gather | solution.py:71
  8.5 4.4 %collective-permute-start.3 = (bf16[7,1,1,32,512]{4,3,2,1,0:T(8,128)(2,1)S(1)}, bf16[7,1,1,32,512]{4,3,2,1,0:T(8,128)(2,1)S(1)}, u32[]{:S(2)}, u32[]{:S(2)}) collective-permute-start(bf16[7,1,1,32,512]{4,3,2,1,0:T(8,128)(2,1)S(1)} %get-tuple-element.30), channel_id=1, source_target_pairs={{2,0},{4,2},{6,4},{3,1},{5,3},{7,5},{10,8},{12,10},{14,12},{11,9},... | collective-permute-start | bytes 688136 | tf_op jit(solution)/shard_map/ppermute | solution.py:17
  9.8 4.1 %collective-permute-start.2 = (bf16[7,1,1,32,512]{4,3,2,1,0:T(8,128)(2,1)S(1)}, bf16[7,1,1,32,512]{4,3,2,1,0:T(8,128)(2,1)S(1)}, u32[]{:S(2)}, u32[]{:S(2)}) collective-permute-start(bf16[7,1,1,32,512]{4,3,2,1,0:T(8,128)(2,1)S(1)} %get-tuple-element.29), channel_id=1, source_target_pairs={{0,2},{2,4},{4,6},{1,3},{3,5},{5,7},{8,10},{10,12},{12,14},{9,11},... | collective-permute-start | bytes 688136 | tf_op jit(solution)/shard_map/ppermute | solution.py:16
  15.7 1.6 copy-start.2
  21.4 1.4 copy-start.4
  37.8 3.8 %copy-start.9 = (f32[2,2,2,1,2,144,512]{6,5,4,3,2,1,0:T(8,128)}, f32[2,2,2,1,2,144,512]{6,5,4,3,2,1,0:T(8,128)S(1)}, u32[]{:S(2)}) copy-start(f32[2,2,2,1,2,144,512]{6,5,4,3,2,1,0:T(8,128)S(1)} %get-tuple-element.21) | copy-start | bytes 14155780
  37.8 5.0 %copy-start.10 = (f32[2,2,2,1,2,144,512]{6,5,4,3,2,1,0:T(8,128)}, f32[2,2,2,1,2,144,512]{6,5,4,3,2,1,0:T(8,128)S(1)}, u32[]{:S(2)}) copy-start(f32[2,2,2,1,2,144,512]{6,5,4,3,2,1,0:T(8,128)S(1)} %get-tuple-element.22) | copy-start | bytes 14155780
  42.9 23.8 %collective-permute-start.4 = (f32[2,2,2,2,144,512]{5,4,0,2,1,3:T(8,128)}, f32[2,2,2,2,144,512]{5,4,0,2,1,3:T(8,128)}, u32[]{:S(2)}, u32[]{:S(2)}) collective-permute-start(f32[2,2,2,2,144,512]{5,4,0,2,1,3:T(8,128)} %select_bitcast_fusion), channel_id=1, source_target_pairs={{0,2},{2,0},{4,6},{6,4},{1,3},{3,1},{5,7},{7,5},{8,10},{10,8},{12,... | collective-permute-start | bytes 14155784 | tf_op jit(solution)/shard_map/ppermute | solution.py:44
  48.0 144.5 %all-gather.5.cloned.1.call-start = ((), (), s32[]{:S(2)}) async-start(), calls=%async_computation.1 | async-start | bytes 2654208 | tf_op jit(solution)/shard_map/all_gather | solution.py:130
  49.1 5.9 %collective-permute-start.1 = (bf16[6,1,1,32,512]{4,3,2,1,0:T(8,128)(2,1)S(1)}, bf16[6,1,1,32,512]{4,3,2,1,0:T(8,128)(2,1)S(1)}, u32[]{:S(2)}, u32[]{:S(2)}) collective-permute-start(bf16[6,1,1,32,512]{4,3,2,1,0:T(8,128)(2,1)S(1)} %get-tuple-element.32), channel_id=1, source_target_pairs={{2,0},{4,2},{6,4},{3,1},{5,3},{7,5},{10,8},{12,10},{14,12},{11,9},... | collective-permute-start | bytes 589832 | tf_op jit(solution)/shard_map/ppermute | solution.py:17
  50.4 4.7 %collective-permute-start = (bf16[6,1,1,32,512]{4,3,2,1,0:T(8,128)(2,1)S(1)}, bf16[6,1,1,32,512]{4,3,2,1,0:T(8,128)(2,1)S(1)}, u32[]{:S(2)}, u32[]{:S(2)}) collective-permute-start(bf16[6,1,1,32,512]{4,3,2,1,0:T(8,128)(2,1)S(1)} %get-tuple-element.31), channel_id=1, source_target_pairs={{0,2},{2,4},{4,6},{1,3},{3,5},{5,7},{8,10},{10,12},{12,14},{9,11},... | collective-permute-start | bytes 589832 | tf_op jit(solution)/shard_map/ppermute | solution.py:16
  57.4 1.4 copy-start.5
  59.1 7.6 %slice-start = ((s8[4718592]{0:T(1024)(128)(4,1)}), s8[4194304]{0:T(1024)(128)(4,1)S(1)}, s32[]{:S(2)}) async-start(s8[4718592]{0:T(1024)(128)(4,1)} %bitcast.199), calls=%async_computation.2 | async-start | bytes 8388608
  59.1 7.6 %slice-start.2 = ((s8[4718592]{0:T(1024)(128)(4,1)}), s8[4194304]{0:T(1024)(128)(4,1)S(1)}, s32[]{:S(2)}) async-start(s8[4718592]{0:T(1024)(128)(4,1)} %bitcast.201), calls=%async_computation.4 | async-start | bytes 8388608
  60.0 6.7 %slice-start.1 = ((s8[4718592]{0:T(1024)(128)(4,1)}), s8[524288]{0:T(1024)(128)(4,1)S(1)}, s32[]{:S(2)}) async-start(s8[4718592]{0:T(1024)(128)(4,1)} %bitcast.199), calls=%async_computation.3 | async-start | bytes 1048576
  60.0 6.7 %slice-start.3 = ((s8[4718592]{0:T(1024)(128)(4,1)}), s8[524288]{0:T(1024)(128)(4,1)S(1)}, s32[]{:S(2)}) async-start(s8[4718592]{0:T(1024)(128)(4,1)} %bitcast.201), calls=%async_computation.5 | async-start | bytes 1048576
  61.2 5.5 %copy-start.11 = (bf16[6,1,8,32,4608]{4,3,2,1,0:T(8,128)(2,1)}, bf16[6,1,8,32,4608]{4,3,2,1,0:T(8,128)(2,1)S(1)}, u32[]{:S(2)}) copy-start(bf16[6,1,8,32,4608]{4,3,2,1,0:T(8,128)(2,1)S(1)} %slice_dynamic-update-slice_fusion.4) | copy-start | bytes 42467332
  70.9 4.5 %copy-start.7 = (f32[2,2,2,2,144,512]{5,4,0,2,1,3:T(8,128)}, f32[2,2,2,2,144,512]{5,4,0,2,1,3:T(8,128)S(1)}, u32[]{:S(2)}) copy-start(f32[2,2,2,2,144,512]{5,4,0,2,1,3:T(8,128)S(1)} %bitcast_add_fusion) | copy-start | bytes 14155780
  72.4 40.2 %collective-permute-start.9 = (f32[2,2,2,144,256]{4,3,0,2,1:T(8,128)}, f32[2,2,2,144,256]{4,3,0,2,1:T(8,128)}, u32[]{:S(2)}, u32[]{:S(2)}) collective-permute-start(f32[2,2,2,144,256]{4,3,0,2,1:T(8,128)} %select_bitcast_fusion.1), channel_id=1, source_target_pairs={{0,1},{1,0},{2,3},{3,2},{4,5},{5,4},{6,7},{7,6},{8,9},{9,8},{10,11... | collective-permute-start | bytes 3538952 | tf_op jit(solution)/shard_map/ppermute | solution.py:44
  76.7 40.0 %collective-permute-start.5 = (f32[2,2,2,144,256]{4,3,0,1,2:T(8,128)}, f32[2,2,2,144,256]{4,3,0,1,2:T(8,128)}, u32[]{:S(2)}, u32[]{:S(2)}) collective-permute-start(f32[2,2,2,144,256]{4,3,0,1,2:T(8,128)} %select_bitcast_fusion.2), channel_id=1, source_target_pairs={{0,4},{2,6},{4,0},{6,2},{1,5},{3,7},{5,1},{7,3},{8,12},{10,14},{12... | collective-permute-start | bytes 3538952 | tf_op jit(solution)/shard_map/ppermute | solution.py:44
  83.3 26.7 %copy-start.3 = (bf16[7,1,10,32,512]{4,3,2,1,0:T(8,128)(2,1)S(1)}, bf16[7,1,10,32,512]{4,3,2,1,0:T(8,128)(2,1)}, u32[]{:S(2)}) copy-start(bf16[7,1,10,32,512]{4,3,2,1,0:T(8,128)(2,1)} %copy-done.2) | copy-start | bytes 6881284
  110.0 3.3 %copy-start.8 = (f32[2,2,2,2,144,512]{5,4,0,2,1,3:T(8,128)S(1)}, f32[2,2,2,2,144,512]{5,4,0,2,1,3:T(8,128)}, u32[]{:S(2)}) copy-start(f32[2,2,2,2,144,512]{5,4,0,2,1,3:T(8,128)} %copy-done.7) | copy-start | bytes 14155780
  115.1 18.2 %collective-permute-start.10 = (f32[2,2,144,256]{3,2,0,1:T(8,128)S(1)}, f32[2,2,144,256]{3,2,0,1:T(8,128)S(1)}, u32[]{:S(2)}, u32[]{:S(2)}) collective-permute-start(f32[2,2,144,256]{3,2,0,1:T(8,128)S(1)} %select_bitcast_fusion.3), channel_id=1, source_target_pairs={{0,8},{8,0},{16,24},{24,16},{1,9},{9,1},{17,25},{25,17},{2,10},{10... | collective-permute-start | bytes 1769480 | tf_op jit(solution)/shard_map/ppermute | solution.py:44
  118.4 15.4 %collective-permute-start.6 = (f32[2,2,144,256]{3,2,0,1:T(8,128)S(1)}, f32[2,2,144,256]{3,2,0,1:T(8,128)S(1)}, u32[]{:S(2)}, u32[]{:S(2)}) collective-permute-start(f32[2,2,144,256]{3,2,0,1:T(8,128)S(1)} %select_bitcast_fusion.4), channel_id=1, source_target_pairs={{0,1},{1,0},{2,3},{3,2},{4,5},{5,4},{6,7},{7,6},{8,9},{9,8},{10,11... | collective-permute-start | bytes 1769480 | tf_op jit(solution)/shard_map/ppermute | solution.py:44
  133.5 8.7 %collective-permute-start.11 = (f32[2,144,256]{2,1,0:T(8,128)S(1)}, f32[2,144,256]{2,1,0:T(8,128)S(1)}, u32[]{:S(2)}, u32[]{:S(2)}) collective-permute-start(f32[2,144,256]{2,1,0:T(8,128)S(1)} %select_bitcast_fusion.5), channel_id=1, source_target_pairs={{0,4},{2,6},{4,0},{6,2},{1,5},{3,7},{5,1},{7,3},{8,12},{10,14},{12... | collective-permute-start | bytes 884744 | tf_op jit(solution)/shard_map/ppermute | solution.py:44
  134.0 10.4 %collective-permute-start.7 = (f32[2,144,256]{2,1,0:T(8,128)S(1)}, f32[2,144,256]{2,1,0:T(8,128)S(1)}, u32[]{:S(2)}, u32[]{:S(2)}) collective-permute-start(f32[2,144,256]{2,1,0:T(8,128)S(1)} %select_bitcast_fusion.6), channel_id=1, source_target_pairs={{0,8},{8,0},{16,24},{24,16},{1,9},{9,1},{17,25},{25,17},{2,10},{10... | collective-permute-start | bytes 884744 | tf_op jit(solution)/shard_map/ppermute | solution.py:44
  142.2 12.1 %collective-permute-start.12 = (f32[144,256]{1,0:T(8,128)S(1)}, f32[144,256]{1,0:T(8,128)S(1)}, u32[]{:S(2)}, u32[]{:S(2)}) collective-permute-start(f32[144,256]{1,0:T(8,128)S(1)} %select_bitcast_fusion.7), channel_id=1, source_target_pairs={{0,16},{8,24},{16,0},{24,8},{1,17},{9,25},{17,1},{25,9},{2,18},{10... | collective-permute-start | bytes 442376 | tf_op jit(solution)/shard_map/ppermute | solution.py:44
  144.5 12.7 %collective-permute-start.8 = (f32[144,256]{1,0:T(8,128)S(1)}, f32[144,256]{1,0:T(8,128)S(1)}, u32[]{:S(2)}, u32[]{:S(2)}) collective-permute-start(f32[144,256]{1,0:T(8,128)S(1)} %select_bitcast_fusion.8), channel_id=1, source_target_pairs={{0,16},{8,24},{16,0},{24,8},{1,17},{9,25},{17,1},{25,9},{2,18},{10... | collective-permute-start | bytes 442376 | tf_op jit(solution)/shard_map/ppermute | solution.py:44
  183.9 1.1 copy-start.12
  183.9 1.3 copy-start.13
  183.9 1.5 copy-start.14
  183.9 1.7 copy-start.15
  184.0 1.9 copy-start.16
  185.8 1.7 copy-start.6
  192.5 8.0 %copy-start.1 = (f32[1152,512]{1,0:T(8,128)S(1)}, f32[1152,512]{1,0:T(8,128)}, u32[]{:S(2)}) copy-start(f32[1152,512]{1,0:T(8,128)} %param.9) | copy-start | bytes 7077892
Sparse Core Ops, SparseCore 0:
  48.1 76.2 all-gather.2
  158.1 28.5 all-gather.4
